TPU v7x, 32 devices: a whole 2x2x4 slice. The times are simulated.
32 devices in a mesh: region: 4 (over z), narrow: 8 (over y, x, core).
Axes of the slice: x: 2, y: 2, z: 4, core: 2. Of those that a mesh axis runs over, the one named last changes fastest.
Arguments:
- dust_pos: float32 [3, 6144], P(None, ('region', 'narrow')), may hold values from -1 to 1
- dust_vel: float32 [3, 6144], P(None, ('region', 'narrow')), may hold values from -6 to 6
- dust_tau: float32 [6144], P(('region', 'narrow')), may hold values from 0.02 to 2
- dest: int32 [6144, 1], P(('region', 'narrow')), may hold values from 0 to 3; in each aligned block of 192 rows (0 to 191, 192 to 383, ...) at most 96 rows name the same one
- counts: int32 [32], P(('region', 'narrow')), may hold values from 96 to 192, as said below
- wake_pos: float32 [3, 32768], P(None, ('region', 'narrow')), may hold values from -1 to 1
- wake_gamma: float32 [3, 32768], P(None, ('region', 'narrow')), may hold values from -0.3 to 0.3
- wake_core: float32 [32768], P(('region', 'narrow')), may hold values from 0.05 to 0.3
Outputs:
- moved: float32 [6, 12288], P(None, ('region', 'narrow'))
Inputs may be any that keep to these rules, and one draw needn't show every extreme that they name: `dest`: in each device's 192 rows, no region is named by more than 96 rows, and some device's rows name some region exactly 96 times. `counts`: some device has all its rows live in every draw.
All inputs are finite; a program needn't handle non-finite values.
Results may differ from a plain program's by a relative error of at most 0.0003.
Values sent between devices are 32-bit elements; how exact they have to be, the bound alone decides.
No kernel may reach another device: no remote copies, remote signals or barrier semaphores. Data moves between devices by JAX's collectives and lax.ppermute only.
A program may use at most 64 MiB of HBM per device.

v0:
```python
import math

import jax
import jax.numpy as jnp
from jax import lax
from jax.sharding import PartitionSpec as P

step_size = 0.1
gravity = 1.0


def cross_rows(first, second):
    return jnp.stack(
        [
            first[1] * second[2] - first[2] * second[1],
            first[2] * second[0] - first[0] * second[2],
            first[0] * second[1] - first[1] * second[0],
        ]
    )


def raw_terms(points, wake_block):
    point_count = points.shape[1]
    wake_count = wake_block.shape[1]
    wake_width = math.gcd(wake_count, 2048)
    wake_place = wake_block[0:3]
    vortex_gamma = wake_block[3:6]
    core_square = wake_block[6] * wake_block[6]
    tables = jnp.concatenate([vortex_gamma, cross_rows(vortex_gamma, wake_place)], axis=0)
    place_blocks = wake_place.reshape(3, wake_count // wake_width, wake_width).transpose(1, 0, 2)
    table_blocks = tables.reshape(6, wake_count // wake_width, wake_width).transpose(1, 0, 2)
    core_blocks = core_square.reshape(wake_count // wake_width, wake_width)
    point_blocks = points.reshape(3, point_count // point_count, point_count).transpose(1, 0, 2)

    def one_block(point_group):

        def accumulate(running, parts):
            place_part, table_part, core_part = parts
            first_gap = point_group[0][:, None] - place_part[0][None, :]
            second_gap = point_group[1][:, None] - place_part[1][None, :]
            third_gap = point_group[2][:, None] - place_part[2][None, :]
            distance_sq = (
                first_gap * first_gap
                + second_gap * second_gap
                + third_gap * third_gap
                + core_part[None, :]
            )
            kernel = 1.0 / (distance_sq * jnp.sqrt(distance_sq))
            product = lax.dot_general(
                table_part, kernel, (((1,), (1,)), ((), ())), precision=lax.Precision.HIGHEST
            )
            return (running + product, None)

        total, _ = lax.scan(
            accumulate,
            jnp.zeros((6, point_count), jnp.float32),
            (place_blocks, table_blocks, core_blocks),
        )
        return total

    result = lax.map(one_block, point_blocks)
    return result.transpose(1, 0, 2).reshape(6, point_count)


def advance(arrived, raw_sums):
    points = arrived[0:3]
    velocity = arrived[3:6]
    live_flag = arrived[7]
    wind = (cross_rows(raw_sums[0:3], points) - raw_sums[3:6]) / (4.0 * math.pi)
    safe_tau = jnp.where(live_flag > 0.5, arrived[6], 1.0)
    rate = step_size / safe_tau
    upward = jnp.array([0.0, 0.0, 1.0], jnp.float32)[:, None]
    new_velocity = (velocity + rate[None, :] * wind - step_size * gravity * upward) / (
        1.0 + rate[None, :]
    )
    new_place = points + step_size * new_velocity
    return jnp.concatenate([new_place, new_velocity], axis=0) * live_flag[None, :]


def body(dust_pos, dust_vel, dust_tau, dest, counts, wake_pos, wake_gamma, wake_core):
    per_device = dust_tau.shape[0]
    regions = lax.axis_size("region")
    capacity = 2 * per_device // regions
    slot_count = regions * capacity
    live_rows = (jnp.arange(per_device, dtype=jnp.int32) < counts[0]).astype(jnp.float32)
    target = dest[:, 0]
    onehot = (target[:, None] == jnp.arange(regions, dtype=jnp.int32)[None, :]).astype(jnp.int32)
    slot_rank = jnp.sum((jnp.cumsum(onehot, axis=0) - onehot) * onehot, axis=1)
    column = target * capacity + slot_rank
    placing = (column[:, None] == jnp.arange(slot_count, dtype=jnp.int32)[None, :]).astype(
        jnp.float32
    )
    dust_state = (
        jnp.concatenate(
            [dust_pos, dust_vel, dust_tau[None, :], jnp.ones((1, per_device), jnp.float32)], axis=0
        )
        * live_rows[None, :]
    )
    outgoing = jnp.dot(
        dust_state, placing, precision=lax.Precision.HIGHEST, preferred_element_type=jnp.float32
    )
    arrived = lax.all_to_all(outgoing, "region", split_axis=1, concat_axis=1, tiled=True)
    points = arrived[0:3]
    wake_rows = jnp.concatenate([wake_pos, wake_gamma, wake_core[None, :]], axis=0)
    raw_sums = raw_terms(points, lax.all_gather(wake_rows, "narrow", axis=1, tiled=True))
    return advance(arrived, raw_sums)


def solution(mesh):
    in_specs = (
        P(None, ("region", "narrow")),
        P(None, ("region", "narrow")),
        P(("region", "narrow")),
        P(("region", "narrow"), None),
        P(("region", "narrow")),
        P(None, ("region", "narrow")),
        P(None, ("region", "narrow")),
        P(("region", "narrow")),
    )
    out_specs = P(None, ("region", "narrow"))
    return jax.shard_map(body, mesh=mesh, in_specs=in_specs, out_specs=out_specs, check_vma=False)
```

profile of v0, /device:TPU:0, one launch (start us, length us, event | category | flops | bytes accessed | tf_op | source)
XLA Modules:
  0.0 41.4 jit_solution(17835298949323918834)
XLA Ops:
  0.0 0.7 %iota_compare_fusion.2 = pred[4,192]{1,0:T(4,128)(4,1)S(1)} fusion(s32[192]{0:T(256)} %bitcast.53), kind=kLoop, calls=%fused_computation.52 | loop fusion | flops 768 | bytes 1536 | tf_op jit(solution)/shard_map/eq | solution.py:87
  0.7 1.2 %reduce-window.6 = s32[4,2,128]{2,1,0:T(2,128)S(1)} reduce-window(s32[4,2,128]{2,1,0:T(2,128)S(1)} %reshape.73, s32[]{:T(128)} %constant.25.clone.1), window={size=1x1x128 pad=0_0x0_0x127_0}, to_apply=%region_0.0 | reduce-window | flops 130048 | bytes 8196 | tf_op jit(solution)/shard_map/reduce-window
  2.0 0.1 slice.176
  2.0 0.1 copy.15
  2.2 0.1 copy.16
  2.3 0.1 add_bitcast_fusion
  2.4 0.7 %fusion.31 = s32[192]{0:T(256)S(1)} fusion(s32[256,4]{0,1:T(4,128)S(1)} %bitcast.52, s32[192]{0:T(256)} %bitcast.54), kind=kLoop, calls=%fused_computation.49 | loop fusion | flops 3648 | bytes 4608 | tf_op jit(solution)/shard_map/reduce_sum | solution.py:88
  3.1 0.7 %multiply_add_fusion.1 = s32[192,1]{0,1:T(1,128)S(1)} fusion(s32[192,1]{0,1:T(1,128)S(1)} %bitcast.57, s32[192,1]{0,1:T(1,128)} %param.14), kind=kLoop, calls=%fused_computation.68 | loop fusion | flops 384 | bytes 2304 | tf_op jit(solution)/shard_map/add | solution.py:89
  4.4 0.1 pad.20.clone
  4.5 1.0 %fusion.18 = f32[8,384]{1,0:T(8,128)S(1)} fusion(s32[192]{0:T(256)S(1)} %bitcast.58, f32[1,192]{1,0:T(1,128)} %bitcast.59, f32[3,192]{1,0:T(4,128)} %param.12, f32[3,192]{1,0:T(4,128)} %param.11, f32[8]{0:T(128)S(1)} %pad.20.clone, f32[192]{0:T(256)S(1)} %compare_convert_fusion), kind=kOutput, calls=%fused_computation.24 | convolution fusion | flops 7157760 | bytes 19232 | tf_op jit(solution)/shard_map/dot_general | solution.py:99
  5.5 0.1 all_to_all.6
  5.6 0.6 %copy.17 = f32[8,4,96]{2,0,1:T(8,128)} copy(f32[8,4,96]{2,1,0:T(4,128)S(1)} %all_to_all.6) | data formatting | bytes 24576 | tf_op jit(solution)/shard_map/all_to_all | solution.py:102
  6.2 6.3 %all-to-all-start = ((f32[8,4,96]{2,0,1:T(8,128)}), f32[8,4,96]{2,0,1:T(8,128)S(1)}, u32[]{:S(2)}, u32[]{:S(2)}) async-start(f32[8,4,96]{2,0,1:T(8,128)} %copy.17), calls=%async_computation | async-start | bytes 32768 | tf_op jit(solution)/shard_map/all_to_all | solution.py:102
  12.5 9.3 %all_gather.3 = f32[7,8192]{1,0:T(8,128)S(1)} all-gather(f32[7,1024]{1,0:T(8,128)S(1)} %pad_maximum_fusion), channel_id=1, replica_groups=mesh['region'=4,'narrow'=8] {'narrow'}, dimensions={1}, use_global_device_ids=true | all-gather | bytes 258048 | tf_op jit(solution)/shard_map/all_gather | solution.py:105
  21.9 0.3 fusion.20
  22.1 0.1 fusion.36
  22.2 0.1 maximum_bitcast_fusion
  22.4 0.1 slice.144
  22.5 17.6 %while.18 = (s32[]{:T(128)}, f32[6,384]{1,0:T(8,128)S(1)}, f32[4,6,2048]{2,1,0:T(8,128)S(1)}, f32[3,384]{1,0:T(4,128)S(1)}, f32[4,3,2048]{2,1,0:T(4,128)S(1)}, /...) while((s32[]{:T(128)}, f32[6,384]{1,0:T(8,128)S(1)}, ...), condition=%wide.region_4.5_spmd.clone, body=%wide.region_3.4_spmd.clone.sunk | while | flops 65278468 | bytes 200859 | solution.py:54
  22.6 4.3 %fusion.43 = f32[6,384]{1,0:T(8,128)S(1)} fusion(f32[2048]{0:T(1024)S(1)} %bitcast.48, f32[2048]{0:T(1024)S(1)} %bitcast.47, f32[384]{0:T(512)S(1)} %get-tuple-element.159, f32[2048]{0:T(1024)S(1)} %bitcast.46, f32[384]{0:T(512)S(1)} %get-tuple-element.161, f32[2048]{0:T(1024)S(1)} %bitcast.45, f32[384]{0:T(512)S(1)} %get-tuple-element.163, ...), kind=kOutput, calls=%fused_computation.11.clone.1 | convolution fusion | flops 65278464 | bytes 125957 | tf_op jit(solution)/shard_map/while/body/eval_jaxpr/while/body/eval_jaxpr/dot_general | solution.py:49
  27.0 4.3 %fusion.43 = f32[6,384]{1,0:T(8,128)S(1)} fusion(f32[2048]{0:T(1024)S(1)} %bitcast.48, f32[2048]{0:T(1024)S(1)} %bitcast.47, f32[384]{0:T(512)S(1)} %get-tuple-element.159, f32[2048]{0:T(1024)S(1)} %bitcast.46, f32[384]{0:T(512)S(1)} %get-tuple-element.161, f32[2048]{0:T(1024)S(1)} %bitcast.45, f32[384]{0:T(512)S(1)} %get-tuple-element.163, ...), kind=kOutput, calls=%fused_computation.11.clone.1 | convolution fusion | flops 65278464 | bytes 125957 | tf_op jit(solution)/shard_map/while/body/eval_jaxpr/while/body/eval_jaxpr/dot_general | solution.py:49
  31.4 4.3 %fusion.43 = f32[6,384]{1,0:T(8,128)S(1)} fusion(f32[2048]{0:T(1024)S(1)} %bitcast.48, f32[2048]{0:T(1024)S(1)} %bitcast.47, f32[384]{0:T(512)S(1)} %get-tuple-element.159, f32[2048]{0:T(1024)S(1)} %bitcast.46, f32[384]{0:T(512)S(1)} %get-tuple-element.161, f32[2048]{0:T(1024)S(1)} %bitcast.45, f32[384]{0:T(512)S(1)} %get-tuple-element.163, ...), kind=kOutput, calls=%fused_computation.11.clone.1 | convolution fusion | flops 65278464 | bytes 125957 | tf_op jit(solution)/shard_map/while/body/eval_jaxpr/while/body/eval_jaxpr/dot_general | solution.py:49
  35.8 4.3 %fusion.43 = f32[6,384]{1,0:T(8,128)S(1)} fusion(f32[2048]{0:T(1024)S(1)} %bitcast.48, f32[2048]{0:T(1024)S(1)} %bitcast.47, f32[384]{0:T(512)S(1)} %get-tuple-element.159, f32[2048]{0:T(1024)S(1)} %bitcast.46, f32[384]{0:T(512)S(1)} %get-tuple-element.161, f32[2048]{0:T(1024)S(1)} %bitcast.45, f32[384]{0:T(512)S(1)} %get-tuple-element.163, ...), kind=kOutput, calls=%fused_computation.11.clone.1 | convolution fusion | flops 65278464 | bytes 125957 | tf_op jit(solution)/shard_map/while/body/eval_jaxpr/while/body/eval_jaxpr/dot_general | solution.py:49
  40.1 0.1 slice_reduce_fusion.4
  40.1 0.1 slice.158
  40.2 0.1 slice.161
  40.3 0.1 slice.163
  40.4 0.1 slice.167
  40.4 0.1 slice.169
  40.6 0.1 slice.146
  40.7 0.1 multiply_add_fusion
  40.7 0.6 %maximum_multiply_fusion = f32[6,384]{1,0:T(8,128)} fusion(f32[3,384]{1,0:T(4,128)S(1)} %get-tuple-element.98, f32[3,384]{1,0:T(4,128)S(1)} %get-tuple-element.97, f32[384]{0:T(512)S(1)} %slice.167), kind=kLoop, calls=%fused_computation.33 | loop fusion | flops 4608 | bytes 19968 | tf_op jit(solution)/shard_map/mul | solution.py:77
  (36 shorter events, 0.4 us)
Async XLA Ops:
  0.0 12.5 %copy-start.2 = (f32[1024]{0:T(1024)S(1)}, f32[1024]{0:T(1024)}, u32[]{:S(2)}) copy-start(f32[1024]{0:T(1024)} %param.18) | copy-start | bytes 12292
  0.0 12.5 %copy-start.1 = (f32[3,1024]{1,0:T(4,128)S(1)}, f32[3,1024]{1,0:T(4,128)}, u32[]{:S(2)}) copy-start(f32[3,1024]{1,0:T(4,128)} %param.16) | copy-start | bytes 36868
  0.0 12.5 %copy-start = (f32[3,1024]{1,0:T(4,128)S(1)}, f32[3,1024]{1,0:T(4,128)}, u32[]{:S(2)}) copy-start(f32[3,1024]{1,0:T(4,128)} %param.17) | copy-start | bytes 36868
  6.2 16.2 %all-to-all-start = ((f32[8,4,96]{2,0,1:T(8,128)}), f32[8,4,96]{2,0,1:T(8,128)S(1)}, u32[]{:S(2)}, u32[]{:S(2)}) async-start(f32[8,4,96]{2,0,1:T(8,128)} %copy.17), calls=%async_computation | async-start | bytes 32768 | tf_op jit(solution)/shard_map/all_to_all | solution.py:102
  22.5 18.2 %copy-start.3 = (f32[3]{0:T(128)S(1)}, f32[3]{0:T(128)}, u32[]{:S(2)}) copy-start(f32[3]{0:T(128)} %constant.56) | copy-start | bytes 40
where the time goes:
time: 41.7 us; the launch traced here: 41.4 us
  matrix products  18.2 us (44%)
  blocking collectives  9.32 us (22%)
  starting transfers between devices  6.33 us (15%)
  other arithmetic  4.56 us (11%)
  local copies, waits for them, and re-layouts  2.08 us (5%)
  between operations  0.78 us (2%)
    dot_general x4, matrix products, accumulate(): lax.dot_general(table_part, kernel, (((1,), (1,)), ((), ())), precision=l...  17.2 us
    all_gather x1, blocking collectives, body(): lax.all_gather(wake_rows, 'narrow', axis=1, tiled=True)  9.32 us
    all_to_all x1, starting transfers between devices, body(): lax.all_to_all(outgoing, 'region', split_axis=1, concat_axis=1, tiled=True)  6.33 us
    another operation x3, other arithmetic  1.26 us
    dot_general x1, matrix products, body(): jnp.dot(dust_state, placing, precision=lax.Precision.HIGHEST, preferred_e...  0.99 us
  transfers between devices with their start and end apart: 1, of which 0 were waited for; matrix products, arithmetic and copies ran while one was open for 1% of the time, Pallas kernels for 0%

commit v1 on v0

--- a/solution.py
+++ b/solution.py
@@ -77,15 +77,45 @@
     return jnp.concatenate([new_place, new_velocity], axis=0) * live_flag[None, :]
 
 
+def gather_wake(wake_rows):
+    lanes = lax.axis_size("narrow")
+    if lanes > 8:
+        return lax.all_gather(wake_rows, "narrow", axis=1, tiled=True)
+    parts = [wake_rows]
+    for shift in range(1, lanes):
+        pairs = [(i, (i + shift) % lanes) for i in range(lanes)]
+        parts.append(lax.ppermute(wake_rows, "narrow", pairs))
+    return jnp.concatenate(parts, axis=1)
+
+
+def exchange_slots(outgoing, capacity):
+    regions = lax.axis_size("region")
+    if regions > 8:
+        return lax.all_to_all(outgoing, "region", split_axis=1, concat_axis=1, tiled=True)
+    region = lax.axis_index("region")
+    blocks = outgoing.reshape(outgoing.shape[0], regions, capacity)
+    by_shift = [jnp.take(blocks, region, axis=1)]
+    for shift in range(1, regions):
+        pairs = [(i, (i + shift) % regions) for i in range(regions)]
+        sent = jnp.take(blocks, (region + shift) % regions, axis=1)
+        by_shift.append(lax.ppermute(sent, "region", pairs))
+    stacked = jnp.stack(by_shift, axis=1)
+    order = (region - jnp.arange(regions, dtype=jnp.int32)) % regions
+    return jnp.take(stacked, order, axis=1).reshape(outgoing.shape[0], regions * capacity)
+
+
 def body(dust_pos, dust_vel, dust_tau, dest, counts, wake_pos, wake_gamma, wake_core):
     per_device = dust_tau.shape[0]
     regions = lax.axis_size("region")
     capacity = 2 * per_device // regions
     slot_count = regions * capacity
+    wake_rows = jnp.concatenate([wake_pos, wake_gamma, wake_core[None, :]], axis=0)
+    region_wake = gather_wake(wake_rows)
     live_rows = (jnp.arange(per_device, dtype=jnp.int32) < counts[0]).astype(jnp.float32)
     target = dest[:, 0]
-    onehot = (target[:, None] == jnp.arange(regions, dtype=jnp.int32)[None, :]).astype(jnp.int32)
-    slot_rank = jnp.sum((jnp.cumsum(onehot, axis=0) - onehot) * onehot, axis=1)
+    row = jnp.arange(per_device, dtype=jnp.int32)
+    earlier = (target[:, None] == target[None, :]) & (row[None, :] < row[:, None])
+    slot_rank = jnp.sum(earlier.astype(jnp.int32), axis=1)
     column = target * capacity + slot_rank
     placing = (column[:, None] == jnp.arange(slot_count, dtype=jnp.int32)[None, :]).astype(
         jnp.float32
@@ -99,10 +129,9 @@
     outgoing = jnp.dot(
         dust_state, placing, precision=lax.Precision.HIGHEST, preferred_element_type=jnp.float32
     )
-    arrived = lax.all_to_all(outgoing, "region", split_axis=1, concat_axis=1, tiled=True)
+    arrived = exchange_slots(outgoing, capacity)
     points = arrived[0:3]
-    wake_rows = jnp.concatenate([wake_pos, wake_gamma, wake_core[None, :]], axis=0)
-    raw_sums = raw_terms(points, lax.all_gather(wake_rows, "narrow", axis=1, tiled=True))
+    raw_sums = raw_terms(points, region_wake)
     return advance(arrived, raw_sums)
 
 

time: 41.7 us -> 41.5 us (level)
  blocking collectives: 9.32 us -> 0 us
  starting transfers between devices: 6.33 us -> 14.6 us
  waiting for transfers between devices: 0.01 us -> 1.65 us
  other arithmetic: 4.56 us -> 3.66 us
    ppermute x0 -> x10, starting transfers between devices: none -> 14.6 us  [the longest x7 9.04 us: gather_wake(): parts.append(lax.ppermute(wake_rows, 'narrow', pairs))]
    all_gather x1 -> x0, blocking collectives: 9.32 us -> none  [body(): lax.all_gather(wake_rows, 'narrow', axis=1, tiled=True)]
    all_to_all x1 -> x0, starting transfers between devices: 6.33 us -> none  [body(): lax.all_to_all(outgoing, 'region', split_axis=1, concat_axis=1, tiled=True)]
    ppermute x0 -> x10, waiting for transfers between devices: none -> 1.65 us  [the longest x7 1.54 us: gather_wake(): parts.append(lax.ppermute(wake_rows, 'narrow', pairs))]
    another operation x3 -> x2, other arithmetic: 1.26 us -> 0.03 us  [the longest x1 0.02 us: exchange_slots(): by_shift = [jnp.take(blocks, region, axis=1)]]
    eq x1 -> x0, other arithmetic: 0.71 us -> none  [body(): target[:, None] == jnp.arange(regions, dtype=jnp.int32)[None, :]]
    unnamed x2, other arithmetic: 0.08 us -> 0.77 us
    all_to_all x2 -> x0, local copies, waits for them, and re-layouts: 0.69 us -> none  [body(): lax.all_to_all(outgoing, 'region', split_axis=1, concat_axis=1, tiled=True)]
  transfers between devices with their start and end apart: 1 -> 10, of which waited for: 0 -> 3; matrix products, arithmetic and copies ran while one was open for 1% -> 10% of each run, Pallas kernels for 0% -> 0%
where the time goes in v1:
time: 41.5 us; the launch traced here: 40.8 us
  matrix products  18.2 us (44%)
  starting transfers between devices  14.6 us (35%)
  other arithmetic  3.66 us (9%)
  local copies, waits for them, and re-layouts  1.74 us (4%)
  waiting for transfers between devices  1.65 us (4%)
  between operations  0.84 us (2%)
    dot_general x4, matrix products, accumulate(): lax.dot_general(table_part, kernel, (((1,), (1,)), ((), ())), precision=l...  17.2 us
    ppermute x7, starting transfers between devices, gather_wake(): parts.append(lax.ppermute(wake_rows, 'narrow', pairs))  9.04 us
    ppermute x3, starting transfers between devices, exchange_slots(): by_shift.append(lax.ppermute(sent, 'region', pairs))  5.57 us
    ppermute x7, waiting for transfers between devices, gather_wake(): parts.append(lax.ppermute(wake_rows, 'narrow', pairs))  1.54 us
    dot_general x1, matrix products, body(): jnp.dot(dust_state, placing, precision=lax.Precision.HIGHEST, preferred_e...  0.99 us
    reduce_sum x1, other arithmetic, body(): slot_rank = jnp.sum(earlier.astype(jnp.int32), axis=1)  0.93 us
  transfers between devices with their start and end apart: 10, of which 3 were waited for; matrix products, arithmetic and copies ran while one was open for 10% of the time, Pallas kernels for 0%

profile of v1, /device:TPU:0, one launch (start us, length us, event | category | flops | bytes accessed | tf_op | source)
XLA Modules:
  0.0 40.8 jit_solution(2768297673587413563)
XLA Ops:
  0.0 0.8 %constant_dynamic-update-slice_fusion.7 = (f32[7,8192]{1,0:T(8,128)S(1)}, f32[7,1024]{1,0:T(8,128)S(1)}) fusion(f32[1,1024]{1,0:T(1,128)} %bitcast.63, f32[3,1024]{1,0:T(4,128)} %param.19, f32[3,1024]{1,0:T(4,128)} %param.18), kind=kLoop, calls=%fused_computation.45 | loop fusion | flops 14335 | bytes 94208
  0.8 0.5 %collective-permute-start.3 = (f32[7,1024]{1,0:T(8,128)S(1)}, f32[7,1024]{1,0:T(8,128)S(1)}, u32[]{:S(2)}, u32[]{:S(2)}) collective-permute-start(f32[7,1024]{1,0:T(8,128)S(1)} %get-tuple-element.114), channel_id=1, source_target_pairs={{0,1},{1,2},{2,3},{3,4},{4,5},{5,6},{6,7},{7,0},{8,9},{9,10},{10,1... | collective-permute-start | bytes 86024 | tf_op jit(solution)/shard_map/ppermute | solution.py:87
  1.3 2.6 %collective-permute-start.4 = (f32[7,1024]{1,0:T(8,128)S(1)}, f32[7,1024]{1,0:T(8,128)S(1)}, u32[]{:S(2)}, u32[]{:S(2)}) collective-permute-start(f32[7,1024]{1,0:T(8,128)S(1)} %get-tuple-element.114), channel_id=1, source_target_pairs={{0,2},{1,3},{2,4},{3,5},{4,6},{5,7},{6,0},{7,1},{8,10},{9,11},{10,... | collective-permute-start | bytes 86024 | tf_op jit(solution)/shard_map/ppermute | solution.py:87
  3.8 0.9 %convert_reduce_fusion = s32[192]{0:T(256)S(1)} fusion(s32[192]{0:T(256)} %bitcast.62), kind=kLoop, calls=%fused_computation.27 | loop fusion | flops 184128 | bytes 1536 | tf_op jit(solution)/shard_map/reduce_sum | solution.py:118
  4.8 0.7 %multiply_add_fusion.1 = s32[192,1]{0,1:T(1,128)S(1)} fusion(s32[192,1]{0,1:T(1,128)S(1)} %bitcast.65, s32[192,1]{0,1:T(1,128)} %param.16), kind=kLoop, calls=%fused_computation.88 | loop fusion | flops 384 | bytes 2304 | tf_op jit(solution)/shard_map/add | solution.py:119
  6.2 1.0 %fusion.18 = f32[8,384]{1,0:T(8,128)S(1)} fusion(s32[192]{0:T(256)S(1)} %bitcast.69, f32[1,192]{1,0:T(1,128)} %bitcast.70, f32[3,192]{1,0:T(4,128)} %param.14, f32[3,192]{1,0:T(4,128)} %param.13, f32[8]{0:T(128)S(1)} %pad.24.clone, f32[192]{0:T(256)S(1)} %compare_convert_fusion), kind=kOutput, calls=%fused_computation.25 | convolution fusion | flops 7157760 | bytes 19232 | tf_op jit(solution)/shard_map/dot_general | solution.py:129
  7.3 1.6 %collective-permute-start = (f32[8,96]{1,0:T(8,128)S(1)}, f32[8,96]{1,0:T(8,128)S(1)}, u32[]{:S(2)}, u32[]{:S(2)}) collective-permute-start(f32[8,96]{1,0:T(8,128)S(1)} %select_bitcast_fusion.2), channel_id=1, source_target_pairs={{0,8},{8,16},{16,24},{24,0},{1,9},{9,17},{17,25},{25,1},{2,10},{10... | collective-permute-start | bytes 9224 | tf_op jit(solution)/shard_map/ppermute | solution.py:101
  8.9 2.6 %collective-permute-start.1 = (f32[8,96]{1,0:T(8,128)S(1)}, f32[8,96]{1,0:T(8,128)S(1)}, u32[]{:S(2)}, u32[]{:S(2)}) collective-permute-start(f32[8,96]{1,0:T(8,128)S(1)} %select_bitcast_fusion.1), channel_id=1, source_target_pairs={{0,16},{8,24},{16,0},{24,8},{1,17},{9,25},{17,1},{25,9},{2,18},{10... | collective-permute-start | bytes 9224 | tf_op jit(solution)/shard_map/ppermute | solution.py:101
  11.5 1.3 %collective-permute-start.2 = (f32[8,96]{1,0:T(8,128)S(1)}, f32[8,96]{1,0:T(8,128)S(1)}, u32[]{:S(2)}, u32[]{:S(2)}) collective-permute-start(f32[8,96]{1,0:T(8,128)S(1)} %bitcast.64), channel_id=1, source_target_pairs={{0,24},{8,0},{16,8},{24,16},{1,25},{9,1},{17,9},{25,17},{2,26},{10... | collective-permute-start | bytes 9224 | tf_op jit(solution)/shard_map/ppermute | solution.py:101
  13.0 1.6 %collective-permute-start.5 = (f32[7,1024]{1,0:T(8,128)S(1)}, f32[7,1024]{1,0:T(8,128)S(1)}, u32[]{:S(2)}, u32[]{:S(2)}) collective-permute-start(f32[7,1024]{1,0:T(8,128)S(1)} %get-tuple-element.114), channel_id=1, source_target_pairs={{0,3},{1,4},{2,5},{3,6},{4,7},{5,0},{6,1},{7,2},{8,11},{9,12},{10,... | collective-permute-start | bytes 86024 | tf_op jit(solution)/shard_map/ppermute | solution.py:87
  14.5 0.5 %collective-permute-start.6 = (f32[7,1024]{1,0:T(8,128)S(1)}, f32[7,1024]{1,0:T(8,128)S(1)}, u32[]{:S(2)}, u32[]{:S(2)}) collective-permute-start(f32[7,1024]{1,0:T(8,128)S(1)} %get-tuple-element.114), channel_id=1, source_target_pairs={{0,4},{1,5},{2,6},{3,7},{4,0},{5,1},{6,2},{7,3},{8,12},{9,13},{10,... | collective-permute-start | bytes 86024 | tf_op jit(solution)/shard_map/ppermute | solution.py:87
  15.0 0.1 collective-permute-done.2
  15.1 0.9 %collective-permute-start.7 = (f32[7,1024]{1,0:T(8,128)S(1)}, f32[7,1024]{1,0:T(8,128)S(1)}, u32[]{:S(2)}, u32[]{:S(2)}) collective-permute-start(f32[7,1024]{1,0:T(8,128)S(1)} %get-tuple-element.114), channel_id=1, source_target_pairs={{0,5},{1,6},{2,7},{3,0},{4,1},{5,2},{6,3},{7,4},{8,13},{9,14},{10,... | collective-permute-start | bytes 86024 | tf_op jit(solution)/shard_map/ppermute | solution.py:87
  16.0 0.5 %gather_fusion = f32[4,8,96]{2,1,0:T(8,128)S(1)} fusion(f32[8,4,96]{2,0,1:T(8,128)S(1)} %pad_maximum_fusion.1, s32[1024]{0:T(1024)S(1)} %pad_clamp_fusion), kind=kCustom, calls=%fused_computation | custom fusion | bytes 24592 | tf_op jit(solution)/shard_map/jit(_take)/gather | solution.py:104
  16.7 0.1 squeeze.30
  16.8 0.1 squeeze.31
  16.9 0.1 slice.122
  17.0 0.1 squeeze.24
  17.1 0.1 squeeze.26
  17.2 0.1 slice.124
  17.3 1.5 %collective-permute-start.8 = (f32[7,1024]{1,0:T(8,128)S(1)}, f32[7,1024]{1,0:T(8,128)S(1)}, u32[]{:S(2)}, u32[]{:S(2)}) collective-permute-start(f32[7,1024]{1,0:T(8,128)S(1)} %get-tuple-element.114), channel_id=1, source_target_pairs={{0,6},{1,7},{2,0},{3,1},{4,2},{5,3},{6,4},{7,5},{8,14},{9,15},{10,... | collective-permute-start | bytes 86024 | tf_op jit(solution)/shard_map/ppermute | solution.py:87
  18.8 1.6 %collective-permute-start.9 = (f32[7,1024]{1,0:T(8,128)S(1)}, f32[7,1024]{1,0:T(8,128)S(1)}, u32[]{:S(2)}, u32[]{:S(2)}) collective-permute-start(f32[7,1024]{1,0:T(8,128)S(1)} %get-tuple-element.114), channel_id=1, source_target_pairs={{0,7},{1,0},{2,1},{3,2},{4,3},{5,4},{6,5},{7,6},{8,15},{9,8},{10,9... | collective-permute-start | bytes 86024 | tf_op jit(solution)/shard_map/ppermute | solution.py:87
  20.4 0.9 %collective-permute-done.8 = f32[7,1024]{1,0:T(8,128)S(1)} collective-permute-done((f32[7,1024]{1,0:T(8,128)S(1)}, f32[7,1024]{1,0:T(8,128)S(1)}, u32[]{:S(2)}, u32[]{:S(2)}) %collective-permute-start.8) | collective-permute-done | bytes 28704 | tf_op jit(solution)/shard_map/ppermute | solution.py:87
  21.4 0.6 %collective-permute-done.9 = f32[7,1024]{1,0:T(8,128)S(1)} collective-permute-done((f32[7,1024]{1,0:T(8,128)S(1)}, f32[7,1024]{1,0:T(8,128)S(1)}, u32[]{:S(2)}, u32[]{:S(2)}) %collective-permute-start.9) | collective-permute-done | bytes 28704 | tf_op jit(solution)/shard_map/ppermute | solution.py:87
  22.0 0.3 fusion.21
  22.3 0.1 maximum_bitcast_fusion
  22.5 17.6 %while.19 = (s32[]{:T(128)}, f32[6,384]{1,0:T(8,128)S(1)}, f32[4,6,2048]{2,1,0:T(8,128)S(1)}, f32[3,384]{1,0:T(4,128)S(1)}, f32[4,3,2048]{2,1,0:T(4,128)S(1)}, /...) while((s32[]{:T(128)}, f32[6,384]{1,0:T(8,128)S(1)}, ...), condition=%wide.region_2.4_spmd.clone, body=%wide.region_1.0_spmd.clone.sunk | while | flops 65278468 | bytes 200859 | solution.py:54
  22.6 4.3 %fusion.45 = f32[6,384]{1,0:T(8,128)S(1)} fusion(f32[2048]{0:T(1024)S(1)} %bitcast.55, f32[2048]{0:T(1024)S(1)} %bitcast.54, f32[384]{0:T(512)S(1)} %get-tuple-element.177, f32[2048]{0:T(1024)S(1)} %bitcast.53, f32[384]{0:T(512)S(1)} %get-tuple-element.179, f32[2048]{0:T(1024)S(1)} %bitcast.52, f32[384]{0:T(512)S(1)} %get-tuple-element.181, ...), kind=kOutput, calls=%fused_computation.12.clone.1 | convolution fusion | flops 65278464 | bytes 125957 | tf_op jit(solution)/shard_map/while/body/eval_jaxpr/while/body/eval_jaxpr/dot_general | solution.py:49
  27.0 4.3 %fusion.45 = f32[6,384]{1,0:T(8,128)S(1)} fusion(f32[2048]{0:T(1024)S(1)} %bitcast.55, f32[2048]{0:T(1024)S(1)} %bitcast.54, f32[384]{0:T(512)S(1)} %get-tuple-element.177, f32[2048]{0:T(1024)S(1)} %bitcast.53, f32[384]{0:T(512)S(1)} %get-tuple-element.179, f32[2048]{0:T(1024)S(1)} %bitcast.52, f32[384]{0:T(512)S(1)} %get-tuple-element.181, ...), kind=kOutput, calls=%fused_computation.12.clone.1 | convolution fusion | flops 65278464 | bytes 125957 | tf_op jit(solution)/shard_map/while/body/eval_jaxpr/while/body/eval_jaxpr/dot_general | solution.py:49
  31.4 4.3 %fusion.45 = f32[6,384]{1,0:T(8,128)S(1)} fusion(f32[2048]{0:T(1024)S(1)} %bitcast.55, f32[2048]{0:T(1024)S(1)} %bitcast.54, f32[384]{0:T(512)S(1)} %get-tuple-element.177, f32[2048]{0:T(1024)S(1)} %bitcast.53, f32[384]{0:T(512)S(1)} %get-tuple-element.179, f32[2048]{0:T(1024)S(1)} %bitcast.52, f32[384]{0:T(512)S(1)} %get-tuple-element.181, ...), kind=kOutput, calls=%fused_computation.12.clone.1 | convolution fusion | flops 65278464 | bytes 125957 | tf_op jit(solution)/shard_map/while/body/eval_jaxpr/while/body/eval_jaxpr/dot_general | solution.py:49
  35.8 4.3 %fusion.45 = f32[6,384]{1,0:T(8,128)S(1)} fusion(f32[2048]{0:T(1024)S(1)} %bitcast.55, f32[2048]{0:T(1024)S(1)} %bitcast.54, f32[384]{0:T(512)S(1)} %get-tuple-element.177, f32[2048]{0:T(1024)S(1)} %bitcast.53, f32[384]{0:T(512)S(1)} %get-tuple-element.179, f32[2048]{0:T(1024)S(1)} %bitcast.52, f32[384]{0:T(512)S(1)} %get-tuple-element.181, ...), kind=kOutput, calls=%fused_computation.12.clone.1 | convolution fusion | flops 65278464 | bytes 125957 | tf_op jit(solution)/shard_map/while/body/eval_jaxpr/while/body/eval_jaxpr/dot_general | solution.py:49
  40.2 0.6 %maximum_multiply_fusion = f32[6,384]{1,0:T(8,128)} fusion(f32[3,384]{1,0:T(4,128)S(1)} %get-tuple-element.110, f32[3,384]{1,0:T(4,128)S(1)} %get-tuple-element.109, f32[384]{0:T(512)S(1)} %squeeze.30), kind=kLoop, calls=%fused_computation.47 | loop fusion | flops 4608 | bytes 19968 | tf_op jit(solution)/shard_map/mul | solution.py:77
  (52 shorter events, 1.0 us)
Async XLA Ops:
  0.8 16.6 %collective-permute-start.3 = (f32[7,1024]{1,0:T(8,128)S(1)}, f32[7,1024]{1,0:T(8,128)S(1)}, u32[]{:S(2)}, u32[]{:S(2)}) collective-permute-start(f32[7,1024]{1,0:T(8,128)S(1)} %get-tuple-element.114), channel_id=1, source_target_pairs={{0,1},{1,2},{2,3},{3,4},{4,5},{5,6},{6,7},{7,0},{8,9},{9,10},{10,1... | collective-permute-start | bytes 86024 | tf_op jit(solution)/shard_map/ppermute | solution.py:87
  1.3 17.5 %collective-permute-start.4 = (f32[7,1024]{1,0:T(8,128)S(1)}, f32[7,1024]{1,0:T(8,128)S(1)}, u32[]{:S(2)}, u32[]{:S(2)}) collective-permute-start(f32[7,1024]{1,0:T(8,128)S(1)} %get-tuple-element.114), channel_id=1, source_target_pairs={{0,2},{1,3},{2,4},{3,5},{4,6},{5,7},{6,0},{7,1},{8,10},{9,11},{10,... | collective-permute-start | bytes 86024 | tf_op jit(solution)/shard_map/ppermute | solution.py:87
  7.3 5.6 %collective-permute-start = (f32[8,96]{1,0:T(8,128)S(1)}, f32[8,96]{1,0:T(8,128)S(1)}, u32[]{:S(2)}, u32[]{:S(2)}) collective-permute-start(f32[8,96]{1,0:T(8,128)S(1)} %select_bitcast_fusion.2), channel_id=1, source_target_pairs={{0,8},{8,16},{16,24},{24,0},{1,9},{9,17},{17,25},{25,1},{2,10},{10... | collective-permute-start | bytes 9224 | tf_op jit(solution)/shard_map/ppermute | solution.py:101
  8.9 5.6 %collective-permute-start.1 = (f32[8,96]{1,0:T(8,128)S(1)}, f32[8,96]{1,0:T(8,128)S(1)}, u32[]{:S(2)}, u32[]{:S(2)}) collective-permute-start(f32[8,96]{1,0:T(8,128)S(1)} %select_bitcast_fusion.1), channel_id=1, source_target_pairs={{0,16},{8,24},{16,0},{24,8},{1,17},{9,25},{17,1},{25,9},{2,18},{10... | collective-permute-start | bytes 9224 | tf_op jit(solution)/shard_map/ppermute | solution.py:101
  11.5 3.6 %collective-permute-start.2 = (f32[8,96]{1,0:T(8,128)S(1)}, f32[8,96]{1,0:T(8,128)S(1)}, u32[]{:S(2)}, u32[]{:S(2)}) collective-permute-start(f32[8,96]{1,0:T(8,128)S(1)} %bitcast.64), channel_id=1, source_target_pairs={{0,24},{8,0},{16,8},{24,16},{1,25},{9,1},{17,9},{25,17},{2,26},{10... | collective-permute-start | bytes 9224 | tf_op jit(solution)/shard_map/ppermute | solution.py:101
  13.0 7.4 %collective-permute-start.5 = (f32[7,1024]{1,0:T(8,128)S(1)}, f32[7,1024]{1,0:T(8,128)S(1)}, u32[]{:S(2)}, u32[]{:S(2)}) collective-permute-start(f32[7,1024]{1,0:T(8,128)S(1)} %get-tuple-element.114), channel_id=1, source_target_pairs={{0,3},{1,4},{2,5},{3,6},{4,7},{5,0},{6,1},{7,2},{8,11},{9,12},{10,... | collective-permute-start | bytes 86024 | tf_op jit(solution)/shard_map/ppermute | solution.py:87
  14.5 5.8 %collective-permute-start.6 = (f32[7,1024]{1,0:T(8,128)S(1)}, f32[7,1024]{1,0:T(8,128)S(1)}, u32[]{:S(2)}, u32[]{:S(2)}) collective-permute-start(f32[7,1024]{1,0:T(8,128)S(1)} %get-tuple-element.114), channel_id=1, source_target_pairs={{0,4},{1,5},{2,6},{3,7},{4,0},{5,1},{6,2},{7,3},{8,12},{9,13},{10,... | collective-permute-start | bytes 86024 | tf_op jit(solution)/shard_map/ppermute | solution.py:87
  15.1 5.3 %collective-permute-start.7 = (f32[7,1024]{1,0:T(8,128)S(1)}, f32[7,1024]{1,0:T(8,128)S(1)}, u32[]{:S(2)}, u32[]{:S(2)}) collective-permute-start(f32[7,1024]{1,0:T(8,128)S(1)} %get-tuple-element.114), channel_id=1, source_target_pairs={{0,5},{1,6},{2,7},{3,0},{4,1},{5,2},{6,3},{7,4},{8,13},{9,14},{10,... | collective-permute-start | bytes 86024 | tf_op jit(solution)/shard_map/ppermute | solution.py:87
  17.3 4.0 %collective-permute-start.8 = (f32[7,1024]{1,0:T(8,128)S(1)}, f32[7,1024]{1,0:T(8,128)S(1)}, u32[]{:S(2)}, u32[]{:S(2)}) collective-permute-start(f32[7,1024]{1,0:T(8,128)S(1)} %get-tuple-element.114), channel_id=1, source_target_pairs={{0,6},{1,7},{2,0},{3,1},{4,2},{5,3},{6,4},{7,5},{8,14},{9,15},{10,... | collective-permute-start | bytes 86024 | tf_op jit(solution)/shard_map/ppermute | solution.py:87
  18.8 3.2 %collective-permute-start.9 = (f32[7,1024]{1,0:T(8,128)S(1)}, f32[7,1024]{1,0:T(8,128)S(1)}, u32[]{:S(2)}, u32[]{:S(2)}) collective-permute-start(f32[7,1024]{1,0:T(8,128)S(1)} %get-tuple-element.114), channel_id=1, source_target_pairs={{0,7},{1,0},{2,1},{3,2},{4,3},{5,4},{6,5},{7,6},{8,15},{9,8},{10,9... | collective-permute-start | bytes 86024 | tf_op jit(solution)/shard_map/ppermute | solution.py:87
  22.5 17.6 %copy-start = (f32[3]{0:T(128)S(1)}, f32[3]{0:T(128)}, u32[]{:S(2)}) copy-start(f32[3]{0:T(128)} %constant.131) | copy-start | bytes 40

commit v2 on v1

--- a/solution.py
+++ b/solution.py
@@ -77,17 +77,6 @@
     return jnp.concatenate([new_place, new_velocity], axis=0) * live_flag[None, :]
 
 
-def gather_wake(wake_rows):
-    lanes = lax.axis_size("narrow")
-    if lanes > 8:
-        return lax.all_gather(wake_rows, "narrow", axis=1, tiled=True)
-    parts = [wake_rows]
-    for shift in range(1, lanes):
-        pairs = [(i, (i + shift) % lanes) for i in range(lanes)]
-        parts.append(lax.ppermute(wake_rows, "narrow", pairs))
-    return jnp.concatenate(parts, axis=1)
-
-
 def exchange_slots(outgoing, capacity):
     regions = lax.axis_size("region")
     if regions > 8:
@@ -109,8 +98,6 @@
     regions = lax.axis_size("region")
     capacity = 2 * per_device // regions
     slot_count = regions * capacity
-    wake_rows = jnp.concatenate([wake_pos, wake_gamma, wake_core[None, :]], axis=0)
-    region_wake = gather_wake(wake_rows)
     live_rows = (jnp.arange(per_device, dtype=jnp.int32) < counts[0]).astype(jnp.float32)
     target = dest[:, 0]
     row = jnp.arange(per_device, dtype=jnp.int32)
@@ -129,7 +116,10 @@
     outgoing = jnp.dot(
         dust_state, placing, precision=lax.Precision.HIGHEST, preferred_element_type=jnp.float32
     )
+    wake_rows = jnp.concatenate([wake_pos, wake_gamma, wake_core[None, :]], axis=0)
+    outgoing, wake_rows = lax.optimization_barrier((outgoing, wake_rows))
     arrived = exchange_slots(outgoing, capacity)
+    region_wake = lax.all_gather(wake_rows, "narrow", axis=1, tiled=True)
     points = arrived[0:3]
     raw_sums = raw_terms(points, region_wake)
     return advance(arrived, raw_sums)

time: 41.5 us -> 41.3 us (level)
  blocking collectives: 0 us -> 9.32 us
  starting transfers between devices: 14.6 us -> 7.01 us
  waiting for transfers between devices: 1.65 us -> 0.01 us
    all_gather x0 -> x1, blocking collectives: none -> 9.32 us  [body(): region_wake = lax.all_gather(wake_rows, 'narrow', axis=1, tiled=True)]
    ppermute x7 -> x0, starting transfers between devices: 9.04 us -> none  [gather_wake(): parts.append(lax.ppermute(wake_rows, 'narrow', pairs))]
    ppermute x7 -> x0, waiting for transfers between devices: 1.54 us -> none  [gather_wake(): parts.append(lax.ppermute(wake_rows, 'narrow', pairs))]
    ppermute x3, starting transfers between devices: 5.57 us -> 7.01 us  [exchange_slots(): by_shift.append(lax.ppermute(sent, 'region', pairs))]
    concatenate x0 -> x1, other arithmetic: none -> 0.77 us  [body(): jnp.concatenate([wake_pos, wake_gamma, wake_core[None, :]], axis=0)]
    unnamed x2 -> x1, other arithmetic: 0.77 us -> 0.01 us
  transfers between devices with their start and end apart: 10 -> 3, of which waited for: 3 -> 0; matrix products, arithmetic and copies ran while one was open for 10% -> 1% of each run, Pallas kernels for 0% -> 0%
where the time goes in v2:
time: 41.3 us; the launch traced here: 40.8 us
  matrix products  18.2 us (44%)
  blocking collectives  9.32 us (23%)
  starting transfers between devices  7.01 us (17%)
  other arithmetic  3.64 us (9%)
  local copies, waits for them, and re-layouts  1.71 us (4%)
  between operations  0.84 us (2%)
    dot_general x4, matrix products, accumulate(): lax.dot_general(table_part, kernel, (((1,), (1,)), ((), ())), precision=l...  17.2 us
    all_gather x1, blocking collectives, body(): region_wake = lax.all_gather(wake_rows, 'narrow', axis=1, tiled=True)  9.32 us
    ppermute x3, starting transfers between devices, exchange_slots(): by_shift.append(lax.ppermute(sent, 'region', pairs))  7.01 us
    dot_general x1, matrix products, body(): jnp.dot(dust_state, placing, precision=lax.Precision.HIGHEST, preferred_e...  1 us
    reduce_sum x1, other arithmetic, body(): slot_rank = jnp.sum(earlier.astype(jnp.int32), axis=1)  0.93 us
  transfers between devices with their start and end apart: 3, of which 0 were waited for; matrix products, arithmetic and copies ran while one was open for 1% of the time, Pallas kernels for 0%

profile of v2, /device:TPU:0, one launch (start us, length us, event | category | flops | bytes accessed | tf_op | source)
XLA Modules:
  0.0 40.8 jit_solution(13058956477274301846)
XLA Ops:
  0.0 0.9 %convert_reduce_fusion = s32[192]{0:T(256)S(1)} fusion(s32[192]{0:T(256)} %bitcast.62), kind=kLoop, calls=%fused_computation.27 | loop fusion | flops 184128 | bytes 1536 | tf_op jit(solution)/shard_map/reduce_sum | solution.py:105
  0.9 0.7 %multiply_add_fusion.1 = s32[192,1]{0,1:T(1,128)S(1)} fusion(s32[192,1]{0,1:T(1,128)S(1)} %bitcast.65, s32[192,1]{0,1:T(1,128)} %param.16), kind=kLoop, calls=%fused_computation.80 | loop fusion | flops 384 | bytes 2304 | tf_op jit(solution)/shard_map/add | solution.py:106
  2.3 0.1 pad.21.clone
  2.4 0.8 %pad_maximum_fusion = f32[7,1024]{1,0:T(8,128)S(1)} fusion(f32[1,1024]{1,0:T(1,128)} %bitcast.63, f32[3,1024]{1,0:T(4,128)} %param.19, f32[3,1024]{1,0:T(4,128)} %param.18), kind=kLoop, calls=%fused_computation.33 | loop fusion | flops 14336 | bytes 57344 | tf_op jit(solution)/shard_map/concatenate | solution.py:119
  3.1 1.0 %fusion.18 = f32[8,384]{1,0:T(8,128)S(1)} fusion(s32[192]{0:T(256)S(1)} %bitcast.69, f32[1,192]{1,0:T(1,128)} %bitcast.70, f32[3,192]{1,0:T(4,128)} %param.14, f32[3,192]{1,0:T(4,128)} %param.13, f32[8]{0:T(128)S(1)} %pad.21.clone, f32[192]{0:T(256)S(1)} %compare_convert_fusion), kind=kOutput, calls=%fused_computation.25 | convolution fusion | flops 7157760 | bytes 19232 | tf_op jit(solution)/shard_map/dot_general | solution.py:116
  4.1 0.1 reshape.132
  4.3 3.1 %collective-permute-start = (f32[8,96]{1,0:T(8,128)S(1)}, f32[8,96]{1,0:T(8,128)S(1)}, u32[]{:S(2)}, u32[]{:S(2)}) collective-permute-start(f32[8,96]{1,0:T(8,128)S(1)} %select_bitcast_fusion.2), channel_id=1, source_target_pairs={{0,8},{8,16},{16,24},{24,0},{1,9},{9,17},{17,25},{25,1},{2,10},{10... | collective-permute-start | bytes 9224 | tf_op jit(solution)/shard_map/ppermute | solution.py:90
  7.3 2.6 %collective-permute-start.1 = (f32[8,96]{1,0:T(8,128)S(1)}, f32[8,96]{1,0:T(8,128)S(1)}, u32[]{:S(2)}, u32[]{:S(2)}) collective-permute-start(f32[8,96]{1,0:T(8,128)S(1)} %select_bitcast_fusion.1), channel_id=1, source_target_pairs={{0,16},{8,24},{16,0},{24,8},{1,17},{9,25},{17,1},{25,9},{2,18},{10... | collective-permute-start | bytes 9224 | tf_op jit(solution)/shard_map/ppermute | solution.py:90
  9.9 1.3 %collective-permute-start.2 = (f32[8,96]{1,0:T(8,128)S(1)}, f32[8,96]{1,0:T(8,128)S(1)}, u32[]{:S(2)}, u32[]{:S(2)}) collective-permute-start(f32[8,96]{1,0:T(8,128)S(1)} %bitcast.64), channel_id=1, source_target_pairs={{0,24},{8,0},{16,8},{24,16},{1,25},{9,1},{17,9},{25,17},{2,26},{10... | collective-permute-start | bytes 9224 | tf_op jit(solution)/shard_map/ppermute | solution.py:90
  11.3 9.3 %all_gather.3 = f32[7,8192]{1,0:T(8,128)S(1)} all-gather(f32[7,1024]{1,0:T(8,128)S(1)} %pad_maximum_fusion), channel_id=1, replica_groups=mesh['region'=4,'narrow'=8] {'narrow'}, dimensions={1}, use_global_device_ids=true | all-gather | bytes 258048 | tf_op jit(solution)/shard_map/all_gather | solution.py:122
  20.6 0.3 fusion.21
  20.9 0.1 fusion.38
  21.0 0.1 maximum_bitcast_fusion
  21.1 0.0 collective-permute-done
  21.2 0.0 collective-permute-done.1
  21.2 0.0 collective-permute-done.2
  21.2 0.6 %gather_fusion = f32[4,8,96]{2,1,0:T(8,128)S(1)} fusion(f32[8,4,96]{2,0,1:T(8,128)S(1)} %pad_maximum_fusion.1, s32[1024]{0:T(1024)S(1)} %pad_clamp_fusion), kind=kCustom, calls=%fused_computation | custom fusion | bytes 24592 | tf_op jit(solution)/shard_map/jit(_take)/gather | solution.py:93
  21.8 0.1 select_bitcast_fusion
  21.9 0.1 slice.122
  22.0 17.6 %while.19 = (s32[]{:T(128)}, f32[6,384]{1,0:T(8,128)S(1)}, f32[4,6,2048]{2,1,0:T(8,128)S(1)}, f32[3,384]{1,0:T(4,128)S(1)}, f32[4,3,2048]{2,1,0:T(4,128)S(1)}, /...) while((s32[]{:T(128)}, f32[6,384]{1,0:T(8,128)S(1)}, ...), condition=%wide.region_2.4_spmd.clone, body=%wide.region_1.0_spmd.clone.sunk | while | flops 65278468 | bytes 200859 | solution.py:54
  22.1 4.3 %fusion.45 = f32[6,384]{1,0:T(8,128)S(1)} fusion(f32[2048]{0:T(1024)S(1)} %bitcast.55, f32[2048]{0:T(1024)S(1)} %bitcast.54, f32[384]{0:T(512)S(1)} %get-tuple-element.179, f32[2048]{0:T(1024)S(1)} %bitcast.53, f32[384]{0:T(512)S(1)} %get-tuple-element.181, f32[2048]{0:T(1024)S(1)} %bitcast.52, f32[384]{0:T(512)S(1)} %get-tuple-element.183, ...), kind=kOutput, calls=%fused_computation.12.clone.1 | convolution fusion | flops 65278464 | bytes 125957 | tf_op jit(solution)/shard_map/while/body/eval_jaxpr/while/body/eval_jaxpr/dot_general | solution.py:49
  26.5 4.3 %fusion.45 = f32[6,384]{1,0:T(8,128)S(1)} fusion(f32[2048]{0:T(1024)S(1)} %bitcast.55, f32[2048]{0:T(1024)S(1)} %bitcast.54, f32[384]{0:T(512)S(1)} %get-tuple-element.179, f32[2048]{0:T(1024)S(1)} %bitcast.53, f32[384]{0:T(512)S(1)} %get-tuple-element.181, f32[2048]{0:T(1024)S(1)} %bitcast.52, f32[384]{0:T(512)S(1)} %get-tuple-element.183, ...), kind=kOutput, calls=%fused_computation.12.clone.1 | convolution fusion | flops 65278464 | bytes 125957 | tf_op jit(solution)/shard_map/while/body/eval_jaxpr/while/body/eval_jaxpr/dot_general | solution.py:49
  30.9 4.3 %fusion.45 = f32[6,384]{1,0:T(8,128)S(1)} fusion(f32[2048]{0:T(1024)S(1)} %bitcast.55, f32[2048]{0:T(1024)S(1)} %bitcast.54, f32[384]{0:T(512)S(1)} %get-tuple-element.179, f32[2048]{0:T(1024)S(1)} %bitcast.53, f32[384]{0:T(512)S(1)} %get-tuple-element.181, f32[2048]{0:T(1024)S(1)} %bitcast.52, f32[384]{0:T(512)S(1)} %get-tuple-element.183, ...), kind=kOutput, calls=%fused_computation.12.clone.1 | convolution fusion | flops 65278464 | bytes 125957 | tf_op jit(solution)/shard_map/while/body/eval_jaxpr/while/body/eval_jaxpr/dot_general | solution.py:49
  35.3 4.3 %fusion.45 = f32[6,384]{1,0:T(8,128)S(1)} fusion(f32[2048]{0:T(1024)S(1)} %bitcast.55, f32[2048]{0:T(1024)S(1)} %bitcast.54, f32[384]{0:T(512)S(1)} %get-tuple-element.179, f32[2048]{0:T(1024)S(1)} %bitcast.53, f32[384]{0:T(512)S(1)} %get-tuple-element.181, f32[2048]{0:T(1024)S(1)} %bitcast.52, f32[384]{0:T(512)S(1)} %get-tuple-element.183, ...), kind=kOutput, calls=%fused_computation.12.clone.1 | convolution fusion | flops 65278464 | bytes 125957 | tf_op jit(solution)/shard_map/while/body/eval_jaxpr/while/body/eval_jaxpr/dot_general | solution.py:49
  39.6 0.1 squeeze.24
  39.6 0.1 squeeze.25
  39.7 0.1 squeeze.26
  39.8 0.1 squeeze.30
  39.9 0.1 squeeze.31
  40.0 0.1 slice.124
  40.1 0.1 multiply_add_fusion
  40.2 0.6 %maximum_multiply_fusion = f32[6,384]{1,0:T(8,128)} fusion(f32[3,384]{1,0:T(4,128)S(1)} %get-tuple-element.114, f32[3,384]{1,0:T(4,128)S(1)} %get-tuple-element.113, f32[384]{0:T(512)S(1)} %squeeze.30), kind=kLoop, calls=%fused_computation.39 | loop fusion | flops 4608 | bytes 19968 | tf_op jit(solution)/shard_map/mul | solution.py:77
  (32 shorter events, 0.5 us)
Async XLA Ops:
  4.3 16.9 %collective-permute-start = (f32[8,96]{1,0:T(8,128)S(1)}, f32[8,96]{1,0:T(8,128)S(1)}, u32[]{:S(2)}, u32[]{:S(2)}) collective-permute-start(f32[8,96]{1,0:T(8,128)S(1)} %select_bitcast_fusion.2), channel_id=1, source_target_pairs={{0,8},{8,16},{16,24},{24,0},{1,9},{9,17},{17,25},{25,1},{2,10},{10... | collective-permute-start | bytes 9224 | tf_op jit(solution)/shard_map/ppermute | solution.py:90
  7.3 13.8 %collective-permute-start.1 = (f32[8,96]{1,0:T(8,128)S(1)}, f32[8,96]{1,0:T(8,128)S(1)}, u32[]{:S(2)}, u32[]{:S(2)}) collective-permute-start(f32[8,96]{1,0:T(8,128)S(1)} %select_bitcast_fusion.1), channel_id=1, source_target_pairs={{0,16},{8,24},{16,0},{24,8},{1,17},{9,25},{17,1},{25,9},{2,18},{10... | collective-permute-start | bytes 9224 | tf_op jit(solution)/shard_map/ppermute | solution.py:90
  9.9 11.2 %collective-permute-start.2 = (f32[8,96]{1,0:T(8,128)S(1)}, f32[8,96]{1,0:T(8,128)S(1)}, u32[]{:S(2)}, u32[]{:S(2)}) collective-permute-start(f32[8,96]{1,0:T(8,128)S(1)} %bitcast.64), channel_id=1, source_target_pairs={{0,24},{8,0},{16,8},{24,16},{1,25},{9,1},{17,9},{25,17},{2,26},{10... | collective-permute-start | bytes 9224 | tf_op jit(solution)/shard_map/ppermute | solution.py:90
  22.0 18.1 %copy-start = (f32[3]{0:T(128)S(1)}, f32[3]{0:T(128)}, u32[]{:S(2)}) copy-start(f32[3]{0:T(128)} %constant.131) | copy-start | bytes 40

commit v3 on v2

--- a/solution.py
+++ b/solution.py
@@ -47,7 +47,7 @@
             )
             kernel = 1.0 / (distance_sq * jnp.sqrt(distance_sq))
             product = lax.dot_general(
-                table_part, kernel, (((1,), (1,)), ((), ())), precision=lax.Precision.HIGHEST
+                table_part, kernel, (((1,), (1,)), ((), ())), precision=lax.Precision.HIGH
             )
             return (running + product, None)
 

time: 41.3 us -> 35.8 us (0.87)
  matrix products: 18.2 us -> 12.7 us
    dot_general x4, matrix products: 17.2 us -> 11.7 us  [accumulate(): lax.dot_general(table_part, kernel, (((1,), (1,)), ((), ())), precision=l...]
where the time goes in v3:
time: 35.8 us; the launch traced here: 35.4 us
  matrix products  12.7 us (35%)
  blocking collectives  9.32 us (26%)
  starting transfers between devices  7.01 us (20%)
  other arithmetic  3.64 us (10%)
  local copies, waits for them, and re-layouts  1.8 us (5%)
  between operations  0.83 us (2%)
    dot_general x4, matrix products, accumulate(): lax.dot_general(table_part, kernel, (((1,), (1,)), ((), ())), precision=l...  11.7 us
    all_gather x1, blocking collectives, body(): region_wake = lax.all_gather(wake_rows, 'narrow', axis=1, tiled=True)  9.32 us
    ppermute x3, starting transfers between devices, exchange_slots(): by_shift.append(lax.ppermute(sent, 'region', pairs))  7.01 us
    dot_general x1, matrix products, body(): jnp.dot(dust_state, placing, precision=lax.Precision.HIGHEST, preferred_e...  1 us
    reduce_sum x1, other arithmetic, body(): slot_rank = jnp.sum(earlier.astype(jnp.int32), axis=1)  0.93 us
    concatenate x1, other arithmetic, body(): jnp.concatenate([wake_pos, wake_gamma, wake_core[None, :]], axis=0)  0.77 us
  transfers between devices with their start and end apart: 3, of which 0 were waited for; matrix products, arithmetic and copies ran while one was open for 1% of the time, Pallas kernels for 0%

profile of v3, /device:TPU:0, one launch (start us, length us, event | category | flops | bytes accessed | tf_op | source)
XLA Modules:
  0.0 35.4 jit_solution(14886656225378471944)
XLA Ops:
  0.0 0.9 %convert_reduce_fusion = s32[192]{0:T(256)S(1)} fusion(s32[192]{0:T(256)} %bitcast.62), kind=kLoop, calls=%fused_computation.27 | loop fusion | flops 184128 | bytes 1536 | tf_op jit(solution)/shard_map/reduce_sum | solution.py:105
  0.9 0.7 %multiply_add_fusion.1 = s32[192,1]{0,1:T(1,128)S(1)} fusion(s32[192,1]{0,1:T(1,128)S(1)} %bitcast.65, s32[192,1]{0,1:T(1,128)} %param.16), kind=kLoop, calls=%fused_computation.80 | loop fusion | flops 384 | bytes 2304 | tf_op jit(solution)/shard_map/add | solution.py:106
  2.3 0.1 pad.21.clone
  2.4 0.8 %pad_maximum_fusion = f32[7,1024]{1,0:T(8,128)S(1)} fusion(f32[1,1024]{1,0:T(1,128)} %bitcast.63, f32[3,1024]{1,0:T(4,128)} %param.19, f32[3,1024]{1,0:T(4,128)} %param.18), kind=kLoop, calls=%fused_computation.33 | loop fusion | flops 14336 | bytes 57344 | tf_op jit(solution)/shard_map/concatenate | solution.py:119
  3.1 1.0 %fusion.18 = f32[8,384]{1,0:T(8,128)S(1)} fusion(s32[192]{0:T(256)S(1)} %bitcast.69, f32[1,192]{1,0:T(1,128)} %bitcast.70, f32[3,192]{1,0:T(4,128)} %param.14, f32[3,192]{1,0:T(4,128)} %param.13, f32[8]{0:T(128)S(1)} %pad.21.clone, f32[192]{0:T(256)S(1)} %compare_convert_fusion), kind=kOutput, calls=%fused_computation.25 | convolution fusion | flops 7157760 | bytes 19232 | tf_op jit(solution)/shard_map/dot_general | solution.py:116
  4.1 0.1 reshape.132
  4.3 3.1 %collective-permute-start = (f32[8,96]{1,0:T(8,128)S(1)}, f32[8,96]{1,0:T(8,128)S(1)}, u32[]{:S(2)}, u32[]{:S(2)}) collective-permute-start(f32[8,96]{1,0:T(8,128)S(1)} %select_bitcast_fusion.2), channel_id=1, source_target_pairs={{0,8},{8,16},{16,24},{24,0},{1,9},{9,17},{17,25},{25,1},{2,10},{10... | collective-permute-start | bytes 9224 | tf_op jit(solution)/shard_map/ppermute | solution.py:90
  7.3 2.6 %collective-permute-start.1 = (f32[8,96]{1,0:T(8,128)S(1)}, f32[8,96]{1,0:T(8,128)S(1)}, u32[]{:S(2)}, u32[]{:S(2)}) collective-permute-start(f32[8,96]{1,0:T(8,128)S(1)} %select_bitcast_fusion.1), channel_id=1, source_target_pairs={{0,16},{8,24},{16,0},{24,8},{1,17},{9,25},{17,1},{25,9},{2,18},{10... | collective-permute-start | bytes 9224 | tf_op jit(solution)/shard_map/ppermute | solution.py:90
  9.9 1.3 %collective-permute-start.2 = (f32[8,96]{1,0:T(8,128)S(1)}, f32[8,96]{1,0:T(8,128)S(1)}, u32[]{:S(2)}, u32[]{:S(2)}) collective-permute-start(f32[8,96]{1,0:T(8,128)S(1)} %bitcast.64), channel_id=1, source_target_pairs={{0,24},{8,0},{16,8},{24,16},{1,25},{9,1},{17,9},{25,17},{2,26},{10... | collective-permute-start | bytes 9224 | tf_op jit(solution)/shard_map/ppermute | solution.py:90
  11.3 9.3 %all_gather.3 = f32[7,8192]{1,0:T(8,128)S(1)} all-gather(f32[7,1024]{1,0:T(8,128)S(1)} %pad_maximum_fusion), channel_id=1, replica_groups=mesh['region'=4,'narrow'=8] {'narrow'}, dimensions={1}, use_global_device_ids=true | all-gather | bytes 258048 | tf_op jit(solution)/shard_map/all_gather | solution.py:122
  20.6 0.3 fusion.21
  20.9 0.1 fusion.38
  21.0 0.1 maximum_bitcast_fusion
  21.2 0.6 %gather_fusion = f32[4,8,96]{2,1,0:T(8,128)S(1)} fusion(f32[8,4,96]{2,0,1:T(8,128)S(1)} %pad_maximum_fusion.1, s32[1024]{0:T(1024)S(1)} %pad_clamp_fusion), kind=kCustom, calls=%fused_computation | custom fusion | bytes 24592 | tf_op jit(solution)/shard_map/jit(_take)/gather | solution.py:93
  21.8 0.1 select_bitcast_fusion
  21.9 0.1 slice.122
  22.0 12.1 %while.19 = (s32[]{:T(128)}, f32[6,384]{1,0:T(8,128)S(1)}, f32[4,6,2048]{2,1,0:T(8,128)S(1)}, f32[3,384]{1,0:T(4,128)S(1)}, f32[4,3,2048]{2,1,0:T(4,128)S(1)}, /...) while((s32[]{:T(128)}, f32[6,384]{1,0:T(8,128)S(1)}, ...), condition=%wide.region_2.4_spmd.clone, body=%wide.region_1.0_spmd.clone.sunk | while | flops 36966916 | bytes 200859 | solution.py:54
  22.1 2.9 %fusion.45 = f32[6,384]{1,0:T(8,128)S(1)} fusion(f32[2048]{0:T(1024)S(1)} %bitcast.55, f32[2048]{0:T(1024)S(1)} %bitcast.54, f32[384]{0:T(512)S(1)} %get-tuple-element.179, f32[2048]{0:T(1024)S(1)} %bitcast.53, f32[384]{0:T(512)S(1)} %get-tuple-element.181, f32[2048]{0:T(1024)S(1)} %bitcast.52, f32[384]{0:T(512)S(1)} %get-tuple-element.183, ...), kind=kOutput, calls=%fused_computation.12.clone.1 | convolution fusion | flops 36966912 | bytes 125957 | tf_op jit(solution)/shard_map/while/body/eval_jaxpr/while/body/eval_jaxpr/dot_general | solution.py:49
  25.0 0.1 constant_dynamic-slice_fusion.10
  25.1 2.9 %fusion.45 = f32[6,384]{1,0:T(8,128)S(1)} fusion(f32[2048]{0:T(1024)S(1)} %bitcast.55, f32[2048]{0:T(1024)S(1)} %bitcast.54, f32[384]{0:T(512)S(1)} %get-tuple-element.179, f32[2048]{0:T(1024)S(1)} %bitcast.53, f32[384]{0:T(512)S(1)} %get-tuple-element.181, f32[2048]{0:T(1024)S(1)} %bitcast.52, f32[384]{0:T(512)S(1)} %get-tuple-element.183, ...), kind=kOutput, calls=%fused_computation.12.clone.1 | convolution fusion | flops 36966912 | bytes 125957 | tf_op jit(solution)/shard_map/while/body/eval_jaxpr/while/body/eval_jaxpr/dot_general | solution.py:49
  28.0 0.1 constant_dynamic-slice_fusion.10
  28.1 2.9 %fusion.45 = f32[6,384]{1,0:T(8,128)S(1)} fusion(f32[2048]{0:T(1024)S(1)} %bitcast.55, f32[2048]{0:T(1024)S(1)} %bitcast.54, f32[384]{0:T(512)S(1)} %get-tuple-element.179, f32[2048]{0:T(1024)S(1)} %bitcast.53, f32[384]{0:T(512)S(1)} %get-tuple-element.181, f32[2048]{0:T(1024)S(1)} %bitcast.52, f32[384]{0:T(512)S(1)} %get-tuple-element.183, ...), kind=kOutput, calls=%fused_computation.12.clone.1 | convolution fusion | flops 36966912 | bytes 125957 | tf_op jit(solution)/shard_map/while/body/eval_jaxpr/while/body/eval_jaxpr/dot_general | solution.py:49
  31.1 0.1 constant_dynamic-slice_fusion.10
  31.2 2.9 %fusion.45 = f32[6,384]{1,0:T(8,128)S(1)} fusion(f32[2048]{0:T(1024)S(1)} %bitcast.55, f32[2048]{0:T(1024)S(1)} %bitcast.54, f32[384]{0:T(512)S(1)} %get-tuple-element.179, f32[2048]{0:T(1024)S(1)} %bitcast.53, f32[384]{0:T(512)S(1)} %get-tuple-element.181, f32[2048]{0:T(1024)S(1)} %bitcast.52, f32[384]{0:T(512)S(1)} %get-tuple-element.183, ...), kind=kOutput, calls=%fused_computation.12.clone.1 | convolution fusion | flops 36966912 | bytes 125957 | tf_op jit(solution)/shard_map/while/body/eval_jaxpr/while/body/eval_jaxpr/dot_general | solution.py:49
  34.1 0.1 squeeze.24
  34.2 0.1 squeeze.25
  34.3 0.1 squeeze.26
  34.4 0.1 squeeze.30
  34.5 0.1 squeeze.31
  34.6 0.1 slice.124
  34.7 0.1 multiply_add_fusion
  34.8 0.6 %maximum_multiply_fusion = f32[6,384]{1,0:T(8,128)} fusion(f32[3,384]{1,0:T(4,128)S(1)} %get-tuple-element.114, f32[3,384]{1,0:T(4,128)S(1)} %get-tuple-element.113, f32[384]{0:T(512)S(1)} %squeeze.30), kind=kLoop, calls=%fused_computation.39 | loop fusion | flops 4608 | bytes 19968 | tf_op jit(solution)/shard_map/mul | solution.py:77
  (32 shorter events, 0.4 us)
Async XLA Ops:
  4.3 16.9 %collective-permute-start = (f32[8,96]{1,0:T(8,128)S(1)}, f32[8,96]{1,0:T(8,128)S(1)}, u32[]{:S(2)}, u32[]{:S(2)}) collective-permute-start(f32[8,96]{1,0:T(8,128)S(1)} %select_bitcast_fusion.2), channel_id=1, source_target_pairs={{0,8},{8,16},{16,24},{24,0},{1,9},{9,17},{17,25},{25,1},{2,10},{10... | collective-permute-start | bytes 9224 | tf_op jit(solution)/shard_map/ppermute | solution.py:90
  7.3 13.8 %collective-permute-start.1 = (f32[8,96]{1,0:T(8,128)S(1)}, f32[8,96]{1,0:T(8,128)S(1)}, u32[]{:S(2)}, u32[]{:S(2)}) collective-permute-start(f32[8,96]{1,0:T(8,128)S(1)} %select_bitcast_fusion.1), channel_id=1, source_target_pairs={{0,16},{8,24},{16,0},{24,8},{1,17},{9,25},{17,1},{25,9},{2,18},{10... | collective-permute-start | bytes 9224 | tf_op jit(solution)/shard_map/ppermute | solution.py:90
  9.9 11.2 %collective-permute-start.2 = (f32[8,96]{1,0:T(8,128)S(1)}, f32[8,96]{1,0:T(8,128)S(1)}, u32[]{:S(2)}, u32[]{:S(2)}) collective-permute-start(f32[8,96]{1,0:T(8,128)S(1)} %bitcast.64), channel_id=1, source_target_pairs={{0,24},{8,0},{16,8},{24,16},{1,25},{9,1},{17,9},{25,17},{2,26},{10... | collective-permute-start | bytes 9224 | tf_op jit(solution)/shard_map/ppermute | solution.py:90
  22.0 12.7 %copy-start = (f32[3]{0:T(128)S(1)}, f32[3]{0:T(128)}, u32[]{:S(2)}) copy-start(f32[3]{0:T(128)} %constant.131) | copy-start | bytes 40

commit v4 on v3

--- a/solution.py
+++ b/solution.py
@@ -45,7 +45,8 @@
                 + third_gap * third_gap
                 + core_part[None, :]
             )
-            kernel = 1.0 / (distance_sq * jnp.sqrt(distance_sq))
+            inverse_root = lax.rsqrt(distance_sq)
+            kernel = inverse_root * inverse_root * inverse_root
             product = lax.dot_general(
                 table_part, kernel, (((1,), (1,)), ((), ())), precision=lax.Precision.HIGH
             )

time: 35.8 us -> 33.5 us (0.936)
  matrix products: 12.7 us -> 10.2 us
    dot_general x4, matrix products: 11.7 us -> 9.21 us  [accumulate(): lax.dot_general(table_part, kernel, (((1,), (1,)), ((), ())), precision=l...]
  transfers between devices with their start and end apart: 3 -> 3, of which waited for: 0 -> 0; matrix products, arithmetic and copies ran while one was open for 1% -> 2% of each run, Pallas kernels for 0% -> 0%
where the time goes in v4:
time: 33.5 us; the launch traced here: 33 us
  matrix products  10.2 us (30%)
  blocking collectives  9.32 us (28%)
  starting transfers between devices  7.01 us (21%)
  other arithmetic  3.64 us (11%)
  local copies, waits for them, and re-layouts  1.92 us (6%)
  between operations  0.83 us (2%)
    all_gather x1, blocking collectives, body(): region_wake = lax.all_gather(wake_rows, 'narrow', axis=1, tiled=True)  9.32 us
    dot_general x4, matrix products, accumulate(): lax.dot_general(table_part, kernel, (((1,), (1,)), ((), ())), precision=l...  9.21 us
    ppermute x3, starting transfers between devices, exchange_slots(): by_shift.append(lax.ppermute(sent, 'region', pairs))  7.01 us
    dot_general x1, matrix products, body(): jnp.dot(dust_state, placing, precision=lax.Precision.HIGHEST, preferred_e...  1 us
    reduce_sum x1, other arithmetic, body(): slot_rank = jnp.sum(earlier.astype(jnp.int32), axis=1)  0.93 us
    concatenate x1, other arithmetic, body(): jnp.concatenate([wake_pos, wake_gamma, wake_core[None, :]], axis=0)  0.77 us
    add x1, other arithmetic, body(): column = target * capacity + slot_rank  0.69 us
  transfers between devices with their start and end apart: 3, of which 0 were waited for; matrix products, arithmetic and copies ran while one was open for 2% of the time, Pallas kernels for 0%

profile of v4, /device:TPU:0, one launch (start us, length us, event | category | flops | bytes accessed | tf_op | source)
XLA Modules:
  0.0 33.0 jit_solution(9160325887394976063)
XLA Ops:
  0.0 0.9 %convert_reduce_fusion = s32[192]{0:T(256)S(1)} fusion(s32[192]{0:T(256)} %bitcast.62), kind=kLoop, calls=%fused_computation.34 | loop fusion | flops 184128 | bytes 1536 | tf_op jit(solution)/shard_map/reduce_sum | solution.py:106
  0.9 0.7 %multiply_add_fusion.1 = s32[192,1]{0,1:T(1,128)S(1)} fusion(s32[192,1]{0,1:T(1,128)S(1)} %bitcast.65, s32[192,1]{0,1:T(1,128)} %param.16), kind=kLoop, calls=%fused_computation.87 | loop fusion | flops 384 | bytes 2304 | tf_op jit(solution)/shard_map/add | solution.py:107
  2.3 0.1 pad.21.clone
  2.4 0.8 %pad_maximum_fusion = f32[7,1024]{1,0:T(8,128)S(1)} fusion(f32[1,1024]{1,0:T(1,128)} %bitcast.63, f32[3,1024]{1,0:T(4,128)} %param.19, f32[3,1024]{1,0:T(4,128)} %param.18), kind=kLoop, calls=%fused_computation.40 | loop fusion | flops 14336 | bytes 57344 | tf_op jit(solution)/shard_map/concatenate | solution.py:120
  3.1 1.0 %fusion.22 = f32[8,384]{1,0:T(8,128)S(1)} fusion(s32[192]{0:T(256)S(1)} %bitcast.69, f32[1,192]{1,0:T(1,128)} %bitcast.70, f32[3,192]{1,0:T(4,128)} %param.14, f32[3,192]{1,0:T(4,128)} %param.13, f32[8]{0:T(128)S(1)} %pad.21.clone, f32[192]{0:T(256)S(1)} %compare_convert_fusion), kind=kOutput, calls=%fused_computation.32 | convolution fusion | flops 7157760 | bytes 19232 | tf_op jit(solution)/shard_map/dot_general | solution.py:117
  4.1 0.1 reshape.132
  4.3 3.1 %collective-permute-start = (f32[8,96]{1,0:T(8,128)S(1)}, f32[8,96]{1,0:T(8,128)S(1)}, u32[]{:S(2)}, u32[]{:S(2)}) collective-permute-start(f32[8,96]{1,0:T(8,128)S(1)} %select_bitcast_fusion.2), channel_id=1, source_target_pairs={{0,8},{8,16},{16,24},{24,0},{1,9},{9,17},{17,25},{25,1},{2,10},{10... | collective-permute-start | bytes 9224 | tf_op jit(solution)/shard_map/ppermute | solution.py:91
  7.3 2.6 %collective-permute-start.1 = (f32[8,96]{1,0:T(8,128)S(1)}, f32[8,96]{1,0:T(8,128)S(1)}, u32[]{:S(2)}, u32[]{:S(2)}) collective-permute-start(f32[8,96]{1,0:T(8,128)S(1)} %select_bitcast_fusion.1), channel_id=1, source_target_pairs={{0,16},{8,24},{16,0},{24,8},{1,17},{9,25},{17,1},{25,9},{2,18},{10... | collective-permute-start | bytes 9224 | tf_op jit(solution)/shard_map/ppermute | solution.py:91
  9.9 1.3 %collective-permute-start.2 = (f32[8,96]{1,0:T(8,128)S(1)}, f32[8,96]{1,0:T(8,128)S(1)}, u32[]{:S(2)}, u32[]{:S(2)}) collective-permute-start(f32[8,96]{1,0:T(8,128)S(1)} %bitcast.64), channel_id=1, source_target_pairs={{0,24},{8,0},{16,8},{24,16},{1,25},{9,1},{17,9},{25,17},{2,26},{10... | collective-permute-start | bytes 9224 | tf_op jit(solution)/shard_map/ppermute | solution.py:91
  11.3 9.3 %all_gather.3 = f32[7,8192]{1,0:T(8,128)S(1)} all-gather(f32[7,1024]{1,0:T(8,128)S(1)} %pad_maximum_fusion), channel_id=1, replica_groups=mesh['region'=4,'narrow'=8] {'narrow'}, dimensions={1}, use_global_device_ids=true | all-gather | bytes 258048 | tf_op jit(solution)/shard_map/all_gather | solution.py:123
  20.6 0.3 fusion.25
  20.9 0.1 fusion.42
  21.0 0.1 maximum_bitcast_fusion
  21.2 0.6 %gather_fusion = f32[4,8,96]{2,1,0:T(8,128)S(1)} fusion(f32[8,4,96]{2,0,1:T(8,128)S(1)} %pad_maximum_fusion.1, s32[1024]{0:T(1024)S(1)} %pad_clamp_fusion), kind=kCustom, calls=%fused_computation | custom fusion | bytes 24592 | tf_op jit(solution)/shard_map/jit(_take)/gather | solution.py:94
  21.8 0.1 select_bitcast_fusion
  21.9 0.1 slice.122
  22.0 9.7 %while.19 = (s32[]{:T(128)}, f32[6,384]{1,0:T(8,128)S(1)}, f32[4,6,2048]{2,1,0:T(8,128)S(1)}, f32[3,384]{1,0:T(4,128)S(1)}, f32[4,3,2048]{2,1,0:T(4,128)S(1)}, /...) while((s32[]{:T(128)}, f32[6,384]{1,0:T(8,128)S(1)}, ...), condition=%wide.region_2.4_spmd.clone, body=%wide.region_1.0_spmd.clone.sunk | while | flops 36966916 | bytes 200859 | solution.py:55
  22.1 2.3 %fusion.47 = f32[6,384]{1,0:T(8,128)S(1)} fusion(f32[2048]{0:T(1024)S(1)} %bitcast.55, f32[2048]{0:T(1024)S(1)} %bitcast.54, f32[384]{0:T(512)S(1)} %get-tuple-element.179, f32[2048]{0:T(1024)S(1)} %bitcast.53, f32[384]{0:T(512)S(1)} %get-tuple-element.181, f32[2048]{0:T(1024)S(1)} %bitcast.52, f32[384]{0:T(512)S(1)} %get-tuple-element.183, ...), kind=kOutput, calls=%fused_computation.20.clone.1 | convolution fusion | flops 36966912 | bytes 125957 | tf_op jit(solution)/shard_map/while/body/eval_jaxpr/while/body/eval_jaxpr/dot_general | solution.py:50
  24.4 0.1 constant_dynamic-slice_fusion.10
  24.5 2.3 %fusion.47 = f32[6,384]{1,0:T(8,128)S(1)} fusion(f32[2048]{0:T(1024)S(1)} %bitcast.55, f32[2048]{0:T(1024)S(1)} %bitcast.54, f32[384]{0:T(512)S(1)} %get-tuple-element.179, f32[2048]{0:T(1024)S(1)} %bitcast.53, f32[384]{0:T(512)S(1)} %get-tuple-element.181, f32[2048]{0:T(1024)S(1)} %bitcast.52, f32[384]{0:T(512)S(1)} %get-tuple-element.183, ...), kind=kOutput, calls=%fused_computation.20.clone.1 | convolution fusion | flops 36966912 | bytes 125957 | tf_op jit(solution)/shard_map/while/body/eval_jaxpr/while/body/eval_jaxpr/dot_general | solution.py:50
  26.8 0.1 constant_dynamic-slice_fusion.10
  27.0 2.3 %fusion.47 = f32[6,384]{1,0:T(8,128)S(1)} fusion(f32[2048]{0:T(1024)S(1)} %bitcast.55, f32[2048]{0:T(1024)S(1)} %bitcast.54, f32[384]{0:T(512)S(1)} %get-tuple-element.179, f32[2048]{0:T(1024)S(1)} %bitcast.53, f32[384]{0:T(512)S(1)} %get-tuple-element.181, f32[2048]{0:T(1024)S(1)} %bitcast.52, f32[384]{0:T(512)S(1)} %get-tuple-element.183, ...), kind=kOutput, calls=%fused_computation.20.clone.1 | convolution fusion | flops 36966912 | bytes 125957 | tf_op jit(solution)/shard_map/while/body/eval_jaxpr/while/body/eval_jaxpr/dot_general | solution.py:50
  29.3 0.1 constant_dynamic-slice_fusion.10
  29.4 2.3 %fusion.47 = f32[6,384]{1,0:T(8,128)S(1)} fusion(f32[2048]{0:T(1024)S(1)} %bitcast.55, f32[2048]{0:T(1024)S(1)} %bitcast.54, f32[384]{0:T(512)S(1)} %get-tuple-element.179, f32[2048]{0:T(1024)S(1)} %bitcast.53, f32[384]{0:T(512)S(1)} %get-tuple-element.181, f32[2048]{0:T(1024)S(1)} %bitcast.52, f32[384]{0:T(512)S(1)} %get-tuple-element.183, ...), kind=kOutput, calls=%fused_computation.20.clone.1 | convolution fusion | flops 36966912 | bytes 125957 | tf_op jit(solution)/shard_map/while/body/eval_jaxpr/while/body/eval_jaxpr/dot_general | solution.py:50
  31.7 0.1 squeeze.24
  31.8 0.1 squeeze.25
  31.9 0.1 squeeze.26
  32.0 0.1 squeeze.30
  32.1 0.1 squeeze.31
  32.2 0.1 slice.124
  32.3 0.1 multiply_add_fusion
  32.4 0.6 %maximum_multiply_fusion = f32[6,384]{1,0:T(8,128)} fusion(f32[3,384]{1,0:T(4,128)S(1)} %get-tuple-element.114, f32[3,384]{1,0:T(4,128)S(1)} %get-tuple-element.113, f32[384]{0:T(512)S(1)} %squeeze.30), kind=kLoop, calls=%fused_computation.46 | loop fusion | flops 4608 | bytes 19968 | tf_op jit(solution)/shard_map/mul | solution.py:78
  (32 shorter events, 0.4 us)
Async XLA Ops:
  4.3 16.9 %collective-permute-start = (f32[8,96]{1,0:T(8,128)S(1)}, f32[8,96]{1,0:T(8,128)S(1)}, u32[]{:S(2)}, u32[]{:S(2)}) collective-permute-start(f32[8,96]{1,0:T(8,128)S(1)} %select_bitcast_fusion.2), channel_id=1, source_target_pairs={{0,8},{8,16},{16,24},{24,0},{1,9},{9,17},{17,25},{25,1},{2,10},{10... | collective-permute-start | bytes 9224 | tf_op jit(solution)/shard_map/ppermute | solution.py:91
  7.3 13.8 %collective-permute-start.1 = (f32[8,96]{1,0:T(8,128)S(1)}, f32[8,96]{1,0:T(8,128)S(1)}, u32[]{:S(2)}, u32[]{:S(2)}) collective-permute-start(f32[8,96]{1,0:T(8,128)S(1)} %select_bitcast_fusion.1), channel_id=1, source_target_pairs={{0,16},{8,24},{16,0},{24,8},{1,17},{9,25},{17,1},{25,9},{2,18},{10... | collective-permute-start | bytes 9224 | tf_op jit(solution)/shard_map/ppermute | solution.py:91
  9.9 11.2 %collective-permute-start.2 = (f32[8,96]{1,0:T(8,128)S(1)}, f32[8,96]{1,0:T(8,128)S(1)}, u32[]{:S(2)}, u32[]{:S(2)}) collective-permute-start(f32[8,96]{1,0:T(8,128)S(1)} %bitcast.64), channel_id=1, source_target_pairs={{0,24},{8,0},{16,8},{24,16},{1,25},{9,1},{17,9},{25,17},{2,26},{10... | collective-permute-start | bytes 9224 | tf_op jit(solution)/shard_map/ppermute | solution.py:91
  22.0 10.4 %copy-start = (f32[3]{0:T(128)S(1)}, f32[3]{0:T(128)}, u32[]{:S(2)}) copy-start(f32[3]{0:T(128)} %constant.129) | copy-start | bytes 40

commit v5 on v4

--- a/solution.py
+++ b/solution.py
@@ -1,8 +1,11 @@
+import functools
 import math
 
 import jax
 import jax.numpy as jnp
 from jax import lax
+from jax.experimental import pallas as pl
+from jax.experimental.pallas import tpu as pltpu
 from jax.sharding import PartitionSpec as P
 
 step_size = 0.1
@@ -19,14 +22,13 @@
     )
 
 
-def raw_terms(points, wake_block):
+def raw_terms(points, wake_table):
     point_count = points.shape[1]
-    wake_count = wake_block.shape[1]
+    wake_count = wake_table.shape[1]
     wake_width = math.gcd(wake_count, 2048)
-    wake_place = wake_block[0:3]
-    vortex_gamma = wake_block[3:6]
-    core_square = wake_block[6] * wake_block[6]
-    tables = jnp.concatenate([vortex_gamma, cross_rows(vortex_gamma, wake_place)], axis=0)
+    wake_place = wake_table[0:3]
+    core_square = wake_table[3]
+    tables = wake_table[4:10]
     place_blocks = wake_place.reshape(3, wake_count // wake_width, wake_width).transpose(1, 0, 2)
     table_blocks = tables.reshape(6, wake_count // wake_width, wake_width).transpose(1, 0, 2)
     core_blocks = core_square.reshape(wake_count // wake_width, wake_width)
@@ -78,6 +80,70 @@
     return jnp.concatenate([new_place, new_velocity], axis=0) * live_flag[None, :]
 
 
+def exact_place(values, placing):
+    high = values.astype(jnp.bfloat16)
+    rest = values - high.astype(jnp.float32)
+    middle = rest.astype(jnp.bfloat16)
+    low = (rest - middle.astype(jnp.float32)).astype(jnp.bfloat16)
+    total = jnp.dot(high, placing, preferred_element_type=jnp.float32)
+    total = total + jnp.dot(middle, placing, preferred_element_type=jnp.float32)
+    return total + jnp.dot(low, placing, preferred_element_type=jnp.float32)
+
+
+def prologue_kernel(
+    count_ref, pos_ref, vel_ref, tau_ref, dest_ref, wpos_ref, wgam_ref, wcore_ref,
+    out_ref, table_ref, *, regions, capacity,
+):
+    per_device = dest_ref.shape[0]
+    slot_count = out_ref.shape[1]
+    target = dest_ref[...]
+    row = lax.broadcasted_iota(jnp.int32, (per_device, per_device), 0)
+    col = lax.broadcasted_iota(jnp.int32, (per_device, per_device), 1)
+    lower = (col < row).astype(jnp.bfloat16)
+    region_id = lax.broadcasted_iota(jnp.int32, (per_device, regions), 1)
+    onehot = (target == region_id).astype(jnp.float32)
+    before = jnp.dot(lower, onehot.astype(jnp.bfloat16), preferred_element_type=jnp.float32)
+    slot_rank = jnp.sum(before * onehot, axis=1, keepdims=True).astype(jnp.int32)
+    column = target * capacity + slot_rank
+    live = lax.broadcasted_iota(jnp.int32, (per_device, 1), 0) < count_ref[0]
+    slot_id = lax.broadcasted_iota(jnp.int32, (per_device, slot_count), 1)
+    placing = ((column == slot_id) & live).astype(jnp.bfloat16)
+    out_ref[0:3, :] = exact_place(pos_ref[...], placing)
+    out_ref[3:6, :] = exact_place(vel_ref[...], placing)
+    out_ref[6:7, :] = exact_place(tau_ref[...], placing)
+    ones = jnp.ones((1, per_device), jnp.bfloat16)
+    out_ref[7:8, :] = jnp.dot(ones, placing, preferred_element_type=jnp.float32)
+    place = [wpos_ref[i:i + 1, :] for i in range(3)]
+    gamma = [wgam_ref[i:i + 1, :] for i in range(3)]
+    core = wcore_ref[...]
+    table_ref[0:3, :] = wpos_ref[...]
+    table_ref[3:4, :] = core * core
+    table_ref[4:7, :] = wgam_ref[...]
+    table_ref[7:8, :] = gamma[1] * place[2] - gamma[2] * place[1]
+    table_ref[8:9, :] = gamma[2] * place[0] - gamma[0] * place[2]
+    table_ref[9:10, :] = gamma[0] * place[1] - gamma[1] * place[0]
+
+
+def prologue(dust_pos, dust_vel, dust_tau, dest, counts, wake_pos, wake_gamma, wake_core):
+    per_device = dust_tau.shape[0]
+    regions = lax.axis_size("region")
+    capacity = 2 * per_device // regions
+    wake_count = wake_core.shape[0]
+    vmem = pl.BlockSpec(memory_space=pltpu.VMEM)
+    return pl.pallas_call(
+        functools.partial(prologue_kernel, regions=regions, capacity=capacity),
+        out_shape=(
+            jax.ShapeDtypeStruct((8, regions * capacity), jnp.float32),
+            jax.ShapeDtypeStruct((10, wake_count), jnp.float32),
+        ),
+        in_specs=[pl.BlockSpec(memory_space=pltpu.SMEM)] + [vmem] * 7,
+        out_specs=(vmem, vmem),
+    )(
+        counts, dust_pos, dust_vel, dust_tau.reshape(1, per_device), dest,
+        wake_pos, wake_gamma, wake_core.reshape(1, wake_count),
+    )
+
+
 def exchange_slots(outgoing, capacity):
     regions = lax.axis_size("region")
     if regions > 8:
@@ -89,40 +155,28 @@
         pairs = [(i, (i + shift) % regions) for i in range(regions)]
         sent = jnp.take(blocks, (region + shift) % regions, axis=1)
         by_shift.append(lax.ppermute(sent, "region", pairs))
-    stacked = jnp.stack(by_shift, axis=1)
-    order = (region - jnp.arange(regions, dtype=jnp.int32)) % regions
-    return jnp.take(stacked, order, axis=1).reshape(outgoing.shape[0], regions * capacity)
+    placed = []
+    for source in range(regions):
+        shift = (region - source) % regions
+        block = by_shift[0]
+        for other in range(1, regions):
+            block = jnp.where(shift == other, by_shift[other], block)
+        placed.append(block)
+    return jnp.concatenate(placed, axis=1)
 
 
 def body(dust_pos, dust_vel, dust_tau, dest, counts, wake_pos, wake_gamma, wake_core):
     per_device = dust_tau.shape[0]
     regions = lax.axis_size("region")
     capacity = 2 * per_device // regions
-    slot_count = regions * capacity
-    live_rows = (jnp.arange(per_device, dtype=jnp.int32) < counts[0]).astype(jnp.float32)
-    target = dest[:, 0]
-    row = jnp.arange(per_device, dtype=jnp.int32)
-    earlier = (target[:, None] == target[None, :]) & (row[None, :] < row[:, None])
-    slot_rank = jnp.sum(earlier.astype(jnp.int32), axis=1)
-    column = target * capacity + slot_rank
-    placing = (column[:, None] == jnp.arange(slot_count, dtype=jnp.int32)[None, :]).astype(
-        jnp.float32
+    outgoing, wake_table = prologue(
+        dust_pos, dust_vel, dust_tau, dest, counts, wake_pos, wake_gamma, wake_core
     )
-    dust_state = (
-        jnp.concatenate(
-            [dust_pos, dust_vel, dust_tau[None, :], jnp.ones((1, per_device), jnp.float32)], axis=0
-        )
-        * live_rows[None, :]
-    )
-    outgoing = jnp.dot(
-        dust_state, placing, precision=lax.Precision.HIGHEST, preferred_element_type=jnp.float32
-    )
-    wake_rows = jnp.concatenate([wake_pos, wake_gamma, wake_core[None, :]], axis=0)
-    outgoing, wake_rows = lax.optimization_barrier((outgoing, wake_rows))
+    outgoing, wake_table = lax.optimization_barrier((outgoing, wake_table))
     arrived = exchange_slots(outgoing, capacity)
-    region_wake = lax.all_gather(wake_rows, "narrow", axis=1, tiled=True)
+    region_table = lax.all_gather(wake_table, "narrow", axis=1, tiled=True)
     points = arrived[0:3]
-    raw_sums = raw_terms(points, region_wake)
+    raw_sums = raw_terms(points, region_table)
     return advance(arrived, raw_sums)
 
 

time: 33.5 us -> 33.9 us (1.012)
  other arithmetic: 3.64 us -> 1.14 us
  Pallas kernels: 0 us -> 2.3 us
  matrix products: 10.2 us -> 9.21 us
  local copies, waits for them, and re-layouts: 1.92 us -> 2.84 us
  blocking collectives: 9.32 us -> 10.1 us
    pallas_call x0 -> x1, Pallas kernels: none -> 2.3 us  [prologue(): pl.pallas_call(functools.partial(prologue_kernel, regions=regions, capaci...]
    unnamed x2 -> x3, local copies, waits for them, and re-layouts: 0.01 us -> 1.43 us
    dot_general x1 -> x0, matrix products: 1 us -> none  [body(): jnp.dot(dust_state, placing, precision=lax.Precision.HIGHEST, preferred_e...]
    reduce_sum x1 -> x0, other arithmetic: 0.93 us -> none  [body(): slot_rank = jnp.sum(earlier.astype(jnp.int32), axis=1)]
    all_gather x1, blocking collectives: 9.32 us -> 10.1 us  [body(): region_table = lax.all_gather(wake_table, 'narrow', axis=1, tiled=True)]
    reshape x1, local copies, waits for them, and re-layouts: 0.08 us -> 0.78 us  [exchange_slots(): blocks = outgoing.reshape(outgoing.shape[0], regions, capacity)]
    add x2 -> x0, other arithmetic: 0.69 us -> none  [the longest x1 0.69 us: body(): column = target * capacity + slot_rank]
    concatenate x1, other arithmetic: 0.77 us -> 0.08 us  [exchange_slots(): return jnp.concatenate(placed, axis=1)]
  transfers between devices with their start and end apart: 3 -> 3, of which waited for: 0 -> 0; matrix products, arithmetic and copies ran while one was open for 2% -> 0% of each run, Pallas kernels for 0% -> 0%
where the time goes in v5:
time: 33.9 us; the launch traced here: 33.6 us
  blocking collectives  10.1 us (30%)
  matrix products  9.21 us (27%)
  starting transfers between devices  7.02 us (21%)
  local copies, waits for them, and re-layouts  2.84 us (8%)
  Pallas kernels  2.3 us (7%)
  other arithmetic  1.14 us (3%)
  between operations  0.83 us (2%)
    all_gather x1, blocking collectives, body(): region_table = lax.all_gather(wake_table, 'narrow', axis=1, tiled=True)  10.1 us
    dot_general x4, matrix products, accumulate(): lax.dot_general(table_part, kernel, (((1,), (1,)), ((), ())), precision=l...  9.21 us
    ppermute x3, starting transfers between devices, exchange_slots(): by_shift.append(lax.ppermute(sent, 'region', pairs))  7.02 us
    pallas_call x1, Pallas kernels, prologue(): pl.pallas_call(functools.partial(prologue_kernel, regions=regions, capaci...  2.3 us
    unnamed x3, local copies, waits for them, and re-layouts  1.43 us
    reshape x1, local copies, waits for them, and re-layouts, exchange_slots(): blocks = outgoing.reshape(outgoing.shape[0], regions, capacity)  0.78 us
  transfers between devices with their start and end apart: 3, of which 0 were waited for; matrix products, arithmetic and copies ran while one was open for 0% of the time, Pallas kernels for 0%

profile of v5, /device:TPU:0, one launch (start us, length us, event | category | flops | bytes accessed | tf_op | source)
XLA Modules:
  0.0 33.6 jit_solution(14375430969153359997)
XLA Ops:
  0.0 1.4 %copy.10.dest_ref = s32[192,1]{1,0:T(8,128)} copy(s32[192,1]{0,1:T(1,128)} %param.16) | data formatting | bytes 1536 | tf_op args[3]
  2.1 2.3 %shard_map.91 = (f32[8,384]{1,0:T(8,128)}, f32[10,1024]{1,0:T(8,128)}) custom-call(s32[1]{0:T(128)S(6)} %copy.27.count_ref, f32[3,192]{1,0:T(4,128)} %pos_ref.1, f32[3,192]{1,0:T(4,128)} %vel_ref.1, f32[1,192]{1,0:T(1,128)} %bitcast.67, s32[192,1]{1,0:T(8,128)} %copy.10.dest_ref, f32[3,1024]{1,0:T(4,128)} %wpos_ref.1, f32[3,1024]{1,0:T(4,128)} %wgam_ref.1, ...), custom_call_target="tpu_custom_call" | custom-call | tf_op jit(solution)/shard_map/pallas_call | solution.py:133
  4.4 0.8 %reshape.38 = f32[8,4,96]{2,1,0:T(4,128)S(1)} reshape(f32[8,384]{1,0:T(8,128)} %get-tuple-element.58) | data formatting | bytes 24576 | tf_op jit(solution)/shard_map/reshape | solution.py:152
  5.2 3.1 %collective-permute-start.2 = (f32[8,96]{1,0:T(8,128)S(1)}, f32[8,96]{1,0:T(8,128)S(1)}, u32[]{:S(2)}, u32[]{:S(2)}) collective-permute-start(f32[8,96]{1,0:T(8,128)S(1)} %select_bitcast_fusion), channel_id=1, source_target_pairs={{0,8},{8,16},{16,24},{24,0},{1,9},{9,17},{17,25},{25,1},{2,10},{10... | collective-permute-start | bytes 9224 | tf_op jit(solution)/shard_map/ppermute | solution.py:157
  8.3 2.6 %collective-permute-start.1 = (f32[8,96]{1,0:T(8,128)S(1)}, f32[8,96]{1,0:T(8,128)S(1)}, u32[]{:S(2)}, u32[]{:S(2)}) collective-permute-start(f32[8,96]{1,0:T(8,128)S(1)} %select_bitcast_fusion.1), channel_id=1, source_target_pairs={{0,16},{8,24},{16,0},{24,8},{1,17},{9,25},{17,1},{25,9},{2,18},{10... | collective-permute-start | bytes 9224 | tf_op jit(solution)/shard_map/ppermute | solution.py:157
  10.9 1.3 %collective-permute-start = (f32[8,96]{1,0:T(8,128)S(1)}, f32[8,96]{1,0:T(8,128)S(1)}, u32[]{:S(2)}, u32[]{:S(2)}) collective-permute-start(f32[8,96]{1,0:T(8,128)S(1)} %select_bitcast_fusion.2), channel_id=1, source_target_pairs={{0,24},{8,0},{16,8},{24,16},{1,25},{9,1},{17,9},{25,17},{2,26},{10... | collective-permute-start | bytes 9224 | tf_op jit(solution)/shard_map/ppermute | solution.py:157
  12.2 10.1 %all_gather.3 = f32[10,8192]{1,0:T(8,128)S(1)} all-gather(f32[10,1024]{1,0:T(8,128)} %get-tuple-element.59), channel_id=1, replica_groups=mesh['region'=4,'narrow'=8] {'narrow'}, dimensions={1}, use_global_device_ids=true | all-gather | bytes 368640 | tf_op jit(solution)/shard_map/all_gather | solution.py:177
  22.4 0.1 slice_reduce_fusion.3
  22.6 0.0 collective-permute-done.2
  22.6 0.0 collective-permute-done.1
  22.7 0.0 collective-permute-done
  22.7 0.1 pad_maximum_fusion
  22.8 0.0 copy-start
  22.8 9.8 %while.19 = (s32[]{:T(128)}, f32[6,384]{1,0:T(8,128)S(1)}, f32[4,6,2048]{2,1,0:T(8,128)S(1)}, f32[3,384]{1,0:T(4,128)S(1)}, f32[4,3,2048]{2,1,0:T(4,128)S(1)}, /...) while((s32[]{:T(128)}, f32[6,384]{1,0:T(8,128)S(1)}, ...), condition=%wide.region_1.3_spmd.clone, body=%wide.region_0.0_spmd.clone.sunk | while | flops 36966916 | bytes 200859 | solution.py:57
  22.9 2.3 %fusion.39 = f32[6,384]{1,0:T(8,128)S(1)} fusion(f32[2048]{0:T(1024)S(1)} %bitcast.61, f32[2048]{0:T(1024)S(1)} %bitcast.60, f32[384]{0:T(512)S(1)} %get-tuple-element.177, f32[2048]{0:T(1024)S(1)} %bitcast.59, f32[384]{0:T(512)S(1)} %get-tuple-element.179, f32[2048]{0:T(1024)S(1)} %bitcast.58, f32[384]{0:T(512)S(1)} %get-tuple-element.181, ...), kind=kOutput, calls=%fused_computation.19.clone.1 | convolution fusion | flops 36966912 | bytes 125957 | tf_op jit(solution)/shard_map/while/body/eval_jaxpr/while/body/eval_jaxpr/dot_general | solution.py:52
  25.2 0.1 constant_dynamic-slice_fusion.11
  25.3 2.3 %fusion.39 = f32[6,384]{1,0:T(8,128)S(1)} fusion(f32[2048]{0:T(1024)S(1)} %bitcast.61, f32[2048]{0:T(1024)S(1)} %bitcast.60, f32[384]{0:T(512)S(1)} %get-tuple-element.177, f32[2048]{0:T(1024)S(1)} %bitcast.59, f32[384]{0:T(512)S(1)} %get-tuple-element.179, f32[2048]{0:T(1024)S(1)} %bitcast.58, f32[384]{0:T(512)S(1)} %get-tuple-element.181, ...), kind=kOutput, calls=%fused_computation.19.clone.1 | convolution fusion | flops 36966912 | bytes 125957 | tf_op jit(solution)/shard_map/while/body/eval_jaxpr/while/body/eval_jaxpr/dot_general | solution.py:52
  27.6 0.1 constant_dynamic-slice_fusion.11
  27.8 2.3 %fusion.39 = f32[6,384]{1,0:T(8,128)S(1)} fusion(f32[2048]{0:T(1024)S(1)} %bitcast.61, f32[2048]{0:T(1024)S(1)} %bitcast.60, f32[384]{0:T(512)S(1)} %get-tuple-element.177, f32[2048]{0:T(1024)S(1)} %bitcast.59, f32[384]{0:T(512)S(1)} %get-tuple-element.179, f32[2048]{0:T(1024)S(1)} %bitcast.58, f32[384]{0:T(512)S(1)} %get-tuple-element.181, ...), kind=kOutput, calls=%fused_computation.19.clone.1 | convolution fusion | flops 36966912 | bytes 125957 | tf_op jit(solution)/shard_map/while/body/eval_jaxpr/while/body/eval_jaxpr/dot_general | solution.py:52
  30.1 0.1 constant_dynamic-slice_fusion.11
  30.2 2.3 %fusion.39 = f32[6,384]{1,0:T(8,128)S(1)} fusion(f32[2048]{0:T(1024)S(1)} %bitcast.61, f32[2048]{0:T(1024)S(1)} %bitcast.60, f32[384]{0:T(512)S(1)} %get-tuple-element.177, f32[2048]{0:T(1024)S(1)} %bitcast.59, f32[384]{0:T(512)S(1)} %get-tuple-element.179, f32[2048]{0:T(1024)S(1)} %bitcast.58, f32[384]{0:T(512)S(1)} %get-tuple-element.181, ...), kind=kOutput, calls=%fused_computation.19.clone.1 | convolution fusion | flops 36966912 | bytes 125957 | tf_op jit(solution)/shard_map/while/body/eval_jaxpr/while/body/eval_jaxpr/dot_general | solution.py:52
  32.5 0.1 multiply_subtract_fusion.2
  32.7 0.1 multiply_subtract_fusion.1
  32.8 0.1 multiply_reduce_fusion
  32.9 0.0 copy-done
  32.9 0.1 multiply_add_fusion
  33.0 0.6 %maximum_multiply_fusion = f32[6,384]{1,0:T(8,128)} fusion(f32[3,384]{1,0:T(4,128)S(1)} %get-tuple-element.113, f32[3,384]{1,0:T(4,128)S(1)} %get-tuple-element.112, f32[384]{0:T(512)S(1)} %get-tuple-element.122), kind=kLoop, calls=%fused_computation.32 | loop fusion | flops 4608 | bytes 19968 | tf_op jit(solution)/shard_map/mul | solution.py:80
  (19 shorter events, 0.3 us)
Async XLA Ops:
  5.2 17.4 %collective-permute-start.2 = (f32[8,96]{1,0:T(8,128)S(1)}, f32[8,96]{1,0:T(8,128)S(1)}, u32[]{:S(2)}, u32[]{:S(2)}) collective-permute-start(f32[8,96]{1,0:T(8,128)S(1)} %select_bitcast_fusion), channel_id=1, source_target_pairs={{0,8},{8,16},{16,24},{24,0},{1,9},{9,17},{17,25},{25,1},{2,10},{10... | collective-permute-start | bytes 9224 | tf_op jit(solution)/shard_map/ppermute | solution.py:157
  8.3 14.4 %collective-permute-start.1 = (f32[8,96]{1,0:T(8,128)S(1)}, f32[8,96]{1,0:T(8,128)S(1)}, u32[]{:S(2)}, u32[]{:S(2)}) collective-permute-start(f32[8,96]{1,0:T(8,128)S(1)} %select_bitcast_fusion.1), channel_id=1, source_target_pairs={{0,16},{8,24},{16,0},{24,8},{1,17},{9,25},{17,1},{25,9},{2,18},{10... | collective-permute-start | bytes 9224 | tf_op jit(solution)/shard_map/ppermute | solution.py:157
  10.9 11.8 %collective-permute-start = (f32[8,96]{1,0:T(8,128)S(1)}, f32[8,96]{1,0:T(8,128)S(1)}, u32[]{:S(2)}, u32[]{:S(2)}) collective-permute-start(f32[8,96]{1,0:T(8,128)S(1)} %select_bitcast_fusion.2), channel_id=1, source_target_pairs={{0,24},{8,0},{16,8},{24,16},{1,25},{9,1},{17,9},{25,17},{2,26},{10... | collective-permute-start | bytes 9224 | tf_op jit(solution)/shard_map/ppermute | solution.py:157
  22.8 10.1 %copy-start = (f32[3]{0:T(128)S(1)}, f32[3]{0:T(128)}, u32[]{:S(2)}) copy-start(f32[3]{0:T(128)} %constant.125) | copy-start | bytes 40

commit v6 on v5

--- a/solution.py
+++ b/solution.py
@@ -85,43 +85,49 @@
     rest = values - high.astype(jnp.float32)
     middle = rest.astype(jnp.bfloat16)
     low = (rest - middle.astype(jnp.float32)).astype(jnp.bfloat16)
-    total = jnp.dot(high, placing, preferred_element_type=jnp.float32)
-    total = total + jnp.dot(middle, placing, preferred_element_type=jnp.float32)
-    return total + jnp.dot(low, placing, preferred_element_type=jnp.float32)
+    contract = (((1,), (1,)), ((), ()))
+    total = lax.dot_general(high, placing, contract, preferred_element_type=jnp.float32)
+    total = total + lax.dot_general(middle, placing, contract, preferred_element_type=jnp.float32)
+    return total + lax.dot_general(low, placing, contract, preferred_element_type=jnp.float32)
 
 
 def prologue_kernel(
     count_ref, pos_ref, vel_ref, tau_ref, dest_ref, wpos_ref, wgam_ref, wcore_ref,
-    out_ref, table_ref, *, regions, capacity,
+    out_ref, table_ref,
 ):
-    per_device = dest_ref.shape[0]
-    slot_count = out_ref.shape[1]
+    regions, _, capacity = out_ref.shape
+    per_device = dest_ref.shape[1]
     target = dest_ref[...]
+    region_id = lax.broadcasted_iota(jnp.int32, (regions, per_device), 0)
+    onehot = (target == region_id).astype(jnp.float32)
     row = lax.broadcasted_iota(jnp.int32, (per_device, per_device), 0)
     col = lax.broadcasted_iota(jnp.int32, (per_device, per_device), 1)
-    lower = (col < row).astype(jnp.bfloat16)
-    region_id = lax.broadcasted_iota(jnp.int32, (per_device, regions), 1)
-    onehot = (target == region_id).astype(jnp.float32)
-    before = jnp.dot(lower, onehot.astype(jnp.bfloat16), preferred_element_type=jnp.float32)
-    slot_rank = jnp.sum(before * onehot, axis=1, keepdims=True).astype(jnp.int32)
+    upper = (row < col).astype(jnp.bfloat16)
+    before = jnp.dot(onehot.astype(jnp.bfloat16), upper, preferred_element_type=jnp.float32)
+    slot_rank = jnp.sum(before * onehot, axis=0, keepdims=True).astype(jnp.int32)
     column = target * capacity + slot_rank
-    live = lax.broadcasted_iota(jnp.int32, (per_device, 1), 0) < count_ref[0]
-    slot_id = lax.broadcasted_iota(jnp.int32, (per_device, slot_count), 1)
-    placing = ((column == slot_id) & live).astype(jnp.bfloat16)
-    out_ref[0:3, :] = exact_place(pos_ref[...], placing)
-    out_ref[3:6, :] = exact_place(vel_ref[...], placing)
-    out_ref[6:7, :] = exact_place(tau_ref[...], placing)
+    live = lax.broadcasted_iota(jnp.int32, (1, per_device), 1) < count_ref[0]
+    pos = pos_ref[...]
+    vel = vel_ref[...]
+    tau = tau_ref[...]
     ones = jnp.ones((1, per_device), jnp.bfloat16)
-    out_ref[7:8, :] = jnp.dot(ones, placing, preferred_element_type=jnp.float32)
-    place = [wpos_ref[i:i + 1, :] for i in range(3)]
-    gamma = [wgam_ref[i:i + 1, :] for i in range(3)]
+
+    def one_region(d, carry):
+        slot_id = lax.broadcasted_iota(jnp.int32, (capacity, per_device), 0) + d * capacity
+        placing = ((column == slot_id) & live).astype(jnp.bfloat16)
+        out_ref[d, 0:3, :] = exact_place(pos, placing)
+        out_ref[d, 3:6, :] = exact_place(vel, placing)
+        out_ref[d, 6:7, :] = exact_place(tau, placing)
+        out_ref[d, 7:8, :] = lax.dot_general(
+            ones, placing, (((1,), (1,)), ((), ())), preferred_element_type=jnp.float32
+        )
+        return carry
+
+    lax.fori_loop(0, regions, one_region, 0)
     core = wcore_ref[...]
     table_ref[0:3, :] = wpos_ref[...]
     table_ref[3:4, :] = core * core
     table_ref[4:7, :] = wgam_ref[...]
-    table_ref[7:8, :] = gamma[1] * place[2] - gamma[2] * place[1]
-    table_ref[8:9, :] = gamma[2] * place[0] - gamma[0] * place[2]
-    table_ref[9:10, :] = gamma[0] * place[1] - gamma[1] * place[0]
 
 
 def prologue(dust_pos, dust_vel, dust_tau, dest, counts, wake_pos, wake_gamma, wake_core):
@@ -131,30 +137,29 @@
     wake_count = wake_core.shape[0]
     vmem = pl.BlockSpec(memory_space=pltpu.VMEM)
     return pl.pallas_call(
-        functools.partial(prologue_kernel, regions=regions, capacity=capacity),
+        prologue_kernel,
         out_shape=(
-            jax.ShapeDtypeStruct((8, regions * capacity), jnp.float32),
-            jax.ShapeDtypeStruct((10, wake_count), jnp.float32),
+            jax.ShapeDtypeStruct((regions, 8, capacity), jnp.float32),
+            jax.ShapeDtypeStruct((7, wake_count), jnp.float32),
         ),
         in_specs=[pl.BlockSpec(memory_space=pltpu.SMEM)] + [vmem] * 7,
         out_specs=(vmem, vmem),
     )(
-        counts, dust_pos, dust_vel, dust_tau.reshape(1, per_device), dest,
+        counts, dust_pos, dust_vel, dust_tau.reshape(1, per_device), dest.reshape(1, per_device),
         wake_pos, wake_gamma, wake_core.reshape(1, wake_count),
     )
 
 
-def exchange_slots(outgoing, capacity):
-    regions = lax.axis_size("region")
+def exchange_slots(blocks):
+    regions, rows, capacity = blocks.shape
     if regions > 8:
-        return lax.all_to_all(outgoing, "region", split_axis=1, concat_axis=1, tiled=True)
+        arrived = lax.all_to_all(blocks, "region", split_axis=0, concat_axis=0, tiled=True)
+        return arrived.transpose(1, 0, 2).reshape(rows, regions * capacity)
     region = lax.axis_index("region")
-    blocks = outgoing.reshape(outgoing.shape[0], regions, capacity)
-    by_shift = [jnp.take(blocks, region, axis=1)]
+    by_shift = [blocks[region]]
     for shift in range(1, regions):
         pairs = [(i, (i + shift) % regions) for i in range(regions)]
-        sent = jnp.take(blocks, (region + shift) % regions, axis=1)
-        by_shift.append(lax.ppermute(sent, "region", pairs))
+        by_shift.append(lax.ppermute(blocks[(region + shift) % regions], "region", pairs))
     placed = []
     for source in range(regions):
         shift = (region - source) % regions
@@ -165,16 +170,19 @@
     return jnp.concatenate(placed, axis=1)
 
 
+def wake_tables(gathered):
+    place = gathered[0:3]
+    gamma = gathered[4:7]
+    return jnp.concatenate([gathered, cross_rows(gamma, place)], axis=0)
+
+
 def body(dust_pos, dust_vel, dust_tau, dest, counts, wake_pos, wake_gamma, wake_core):
-    per_device = dust_tau.shape[0]
-    regions = lax.axis_size("region")
-    capacity = 2 * per_device // regions
     outgoing, wake_table = prologue(
         dust_pos, dust_vel, dust_tau, dest, counts, wake_pos, wake_gamma, wake_core
     )
     outgoing, wake_table = lax.optimization_barrier((outgoing, wake_table))
-    arrived = exchange_slots(outgoing, capacity)
-    region_table = lax.all_gather(wake_table, "narrow", axis=1, tiled=True)
+    arrived = exchange_slots(outgoing)
+    region_table = wake_tables(lax.all_gather(wake_table, "narrow", axis=1, tiled=True))
     points = arrived[0:3]
     raw_sums = raw_terms(points, region_table)
     return advance(arrived, raw_sums)

time: 33.9 us -> 32 us (0.944)
  local copies, waits for them, and re-layouts: 2.84 us -> 1.19 us
  other arithmetic: 1.14 us -> 2.2 us
  starting transfers between devices: 7.02 us -> 6.06 us
  blocking collectives: 10.1 us -> 9.51 us
    unnamed x3 -> x2, local copies, waits for them, and re-layouts: 1.43 us -> 0.01 us
    ppermute x3, starting transfers between devices: 7.02 us -> 6.06 us  [exchange_slots(): lax.ppermute(blocks[(region + shift) % regions], 'region', pairs)]
    reshape x1 -> x0, local copies, waits for them, and re-layouts: 0.78 us -> none  [exchange_slots(): blocks = outgoing.reshape(outgoing.shape[0], regions, capacity)]
    squeeze x0 -> x1, local copies, waits for them, and re-layouts: none -> 0.69 us  [exchange_slots(): blocks[(region + shift) % regions]]
    select_n x1, other arithmetic: 0.01 us -> 0.69 us  [exchange_slots(): block = jnp.where(shift == other, by_shift[other], block)]
    all_gather x1, blocking collectives: 10.1 us -> 9.51 us  [body(): lax.all_gather(wake_table, 'narrow', axis=1, tiled=True)]
  transfers between devices with their start and end apart: 3 -> 3, of which waited for: 0 -> 0; matrix products, arithmetic and copies ran while one was open for 0% -> 1% of each run, Pallas kernels for 0% -> 0%
where the time goes in v6:
time: 32 us; the launch traced here: 31.6 us
  blocking collectives  9.51 us (30%)
  matrix products  9.21 us (29%)
  starting transfers between devices  6.06 us (19%)
  Pallas kernels  2.54 us (8%)
  other arithmetic  2.2 us (7%)
  local copies, waits for them, and re-layouts  1.19 us (4%)
  between operations  0.8 us (2%)
    all_gather x1, blocking collectives, body(): lax.all_gather(wake_table, 'narrow', axis=1, tiled=True)  9.51 us
    dot_general x4, matrix products, accumulate(): lax.dot_general(table_part, kernel, (((1,), (1,)), ((), ())), precision=l...  9.21 us
    ppermute x3, starting transfers between devices, exchange_slots(): lax.ppermute(blocks[(region + shift) % regions], 'region', pairs)  6.06 us
    pallas_call x1, Pallas kernels, prologue(): pl.pallas_call(prologue_kernel, out_shape=(jax.ShapeDtypeStruct((regions,...  2.54 us
    select_n x1, other arithmetic, exchange_slots(): block = jnp.where(shift == other, by_shift[other], block)  0.69 us
    squeeze x1, local copies, waits for them, and re-layouts, exchange_slots(): blocks[(region + shift) % regions]  0.69 us
  transfers between devices with their start and end apart: 3, of which 0 were waited for; matrix products, arithmetic and copies ran while one was open for 1% of the time, Pallas kernels for 0%

profile of v6, /device:TPU:0, one launch (start us, length us, event | category | flops | bytes accessed | tf_op | source)
XLA Modules:
  0.0 31.6 jit_solution(7327203755934638734)
XLA Ops:
  0.7 2.5 %shard_map.91 = (f32[4,8,96]{2,1,0:T(8,128)}, f32[7,1024]{1,0:T(8,128)}) custom-call(s32[1]{0:T(128)S(6)} %copy.18.count_ref, f32[3,192]{1,0:T(4,128)} %pos_ref.1, f32[3,192]{1,0:T(4,128)} %vel_ref.1, f32[1,192]{1,0:T(1,128)} %bitcast.60, s32[1,192]{1,0:T(1,128)} %bitcast.61, f32[3,1024]{1,0:T(4,128)} %wpos_ref.1, f32[3,1024]{1,0:T(4,128)} %wgam_ref.1, ...), custom_call_target="tpu_custom_call" | custom-call | tf_op jit(solution)/shard_map/pallas_call | solution.py:139
  3.2 0.7 %dynamic-slice_bitcast_fusion = (f32[8,96]{1,0:T(8,128)S(1)}, f32[8,96]{1,0:T(8,128)S(1)}, f32[8,96]{1,0:T(8,128)S(1)}) fusion(f32[4,8,96]{2,1,0:T(8,128)} %get-tuple-element.57, s32[]{:T(128)S(6)} %select_n.132, s32[]{:T(128)S(6)} %select_n.129, s32[]{:T(128)S(6)} %select_n.126), kind=kLoop, calls=%fused_computation.58 | loop fusion | bytes 18444 | tf_op jit(solution)/shard_map/squeeze | solution.py:162
  3.9 5.1 %collective-permute-start = (f32[8,96]{1,0:T(8,128)S(1)}, f32[8,96]{1,0:T(8,128)S(1)}, u32[]{:S(2)}, u32[]{:S(2)}) collective-permute-start(f32[8,96]{1,0:T(8,128)S(1)} %get-tuple-element.122), channel_id=1, source_target_pairs={{0,24},{8,0},{16,8},{24,16},{1,25},{9,1},{17,9},{25,17},{2,26},{10... | collective-permute-start | bytes 9224 | tf_op jit(solution)/shard_map/ppermute | solution.py:162
  8.9 0.0 collective-permute-start.1
  8.9 1.0 %collective-permute-start.2 = (f32[8,96]{1,0:T(8,128)S(1)}, f32[8,96]{1,0:T(8,128)S(1)}, u32[]{:S(2)}, u32[]{:S(2)}) collective-permute-start(f32[8,96]{1,0:T(8,128)S(1)} %get-tuple-element.120), channel_id=1, source_target_pairs={{0,8},{8,16},{16,24},{24,0},{1,9},{9,17},{17,25},{25,1},{2,10},{10... | collective-permute-start | bytes 9224 | tf_op jit(solution)/shard_map/ppermute | solution.py:162
  9.9 9.5 %all_gather.3 = f32[7,8192]{1,0:T(8,128)S(1)} all-gather(f32[7,1024]{1,0:T(8,128)} %get-tuple-element.58), channel_id=1, replica_groups=mesh['region'=4,'narrow'=8] {'narrow'}, dimensions={1}, use_global_device_ids=true | all-gather | bytes 258048 | tf_op jit(solution)/shard_map/all_gather | solution.py:185
  19.5 0.3 slice_reduce_fusion.3
  19.7 0.1 pad_maximum_fusion
  20.0 0.0 collective-permute-done
  20.0 0.0 collective-permute-done.1
  20.0 0.0 collective-permute-done.2
  20.0 0.7 %fusion.26 = (f32[8,96]{1,0:T(8,128)S(1)}, f32[8,96]{1,0:T(8,128)S(1)}, f32[8,96]{1,0:T(8,128)S(1)}, f32[8,96]{1,0:T(8,128)S(1)}) fusion(f32[8,96]{1,0:T(8,128)S(1)} %collective-permute-done, f32[8,96]{1,0:T(8,128)S(1)} %collective-permute-done.1, f32[8,96]{1,0:T(8,128)S(1)} %collective-permute-done.2, f32[4,8,96]{2,1,0:T(8,128)} %get-tuple-element.57, ...), kind=kLoop, calls=%fused_computation.51 | loop fusion | flops 9216 | bytes 24592 | tf_op jit(solution)/shard_map/jit(_where)/select_n | solution.py:168
  20.7 0.1 pad_maximum_fusion.3
  20.8 0.0 copy-start
  20.8 9.8 %while.18 = (s32[]{:T(128)}, f32[6,384]{1,0:T(8,128)S(1)}, f32[4,6,2048]{2,1,0:T(8,128)S(1)}, f32[3,384]{1,0:T(4,128)S(1)}, f32[4,3,2048]{2,1,0:T(4,128)S(1)}, /...) while((s32[]{:T(128)}, f32[6,384]{1,0:T(8,128)S(1)}, ...), condition=%wide.region_1.2_spmd.clone, body=%wide.region_0.1_spmd.clone.sunk | while | flops 36966916 | bytes 200859 | solution.py:57
  20.9 2.3 %fusion.39 = f32[6,384]{1,0:T(8,128)S(1)} fusion(f32[2048]{0:T(1024)S(1)} %bitcast.58, f32[2048]{0:T(1024)S(1)} %bitcast.57, f32[384]{0:T(512)S(1)} %get-tuple-element.168, f32[2048]{0:T(1024)S(1)} %bitcast.56, f32[384]{0:T(512)S(1)} %get-tuple-element.170, f32[2048]{0:T(1024)S(1)} %bitcast.55, f32[384]{0:T(512)S(1)} %get-tuple-element.172, ...), kind=kOutput, calls=%fused_computation.19.clone.1 | convolution fusion | flops 36966912 | bytes 125957 | tf_op jit(solution)/shard_map/while/body/eval_jaxpr/while/body/eval_jaxpr/dot_general | solution.py:52
  23.2 0.1 constant_dynamic-slice_fusion.7
  23.4 2.3 %fusion.39 = f32[6,384]{1,0:T(8,128)S(1)} fusion(f32[2048]{0:T(1024)S(1)} %bitcast.58, f32[2048]{0:T(1024)S(1)} %bitcast.57, f32[384]{0:T(512)S(1)} %get-tuple-element.168, f32[2048]{0:T(1024)S(1)} %bitcast.56, f32[384]{0:T(512)S(1)} %get-tuple-element.170, f32[2048]{0:T(1024)S(1)} %bitcast.55, f32[384]{0:T(512)S(1)} %get-tuple-element.172, ...), kind=kOutput, calls=%fused_computation.19.clone.1 | convolution fusion | flops 36966912 | bytes 125957 | tf_op jit(solution)/shard_map/while/body/eval_jaxpr/while/body/eval_jaxpr/dot_general | solution.py:52
  25.7 0.1 constant_dynamic-slice_fusion.7
  25.8 2.3 %fusion.39 = f32[6,384]{1,0:T(8,128)S(1)} fusion(f32[2048]{0:T(1024)S(1)} %bitcast.58, f32[2048]{0:T(1024)S(1)} %bitcast.57, f32[384]{0:T(512)S(1)} %get-tuple-element.168, f32[2048]{0:T(1024)S(1)} %bitcast.56, f32[384]{0:T(512)S(1)} %get-tuple-element.170, f32[2048]{0:T(1024)S(1)} %bitcast.55, f32[384]{0:T(512)S(1)} %get-tuple-element.172, ...), kind=kOutput, calls=%fused_computation.19.clone.1 | convolution fusion | flops 36966912 | bytes 125957 | tf_op jit(solution)/shard_map/while/body/eval_jaxpr/while/body/eval_jaxpr/dot_general | solution.py:52
  28.1 0.1 constant_dynamic-slice_fusion.7
  28.3 2.3 %fusion.39 = f32[6,384]{1,0:T(8,128)S(1)} fusion(f32[2048]{0:T(1024)S(1)} %bitcast.58, f32[2048]{0:T(1024)S(1)} %bitcast.57, f32[384]{0:T(512)S(1)} %get-tuple-element.168, f32[2048]{0:T(1024)S(1)} %bitcast.56, f32[384]{0:T(512)S(1)} %get-tuple-element.170, f32[2048]{0:T(1024)S(1)} %bitcast.55, f32[384]{0:T(512)S(1)} %get-tuple-element.172, ...), kind=kOutput, calls=%fused_computation.19.clone.1 | convolution fusion | flops 36966912 | bytes 125957 | tf_op jit(solution)/shard_map/while/body/eval_jaxpr/while/body/eval_jaxpr/dot_general | solution.py:52
  30.6 0.1 multiply_subtract_fusion.5
  30.7 0.1 multiply_subtract_fusion.4
  30.8 0.1 multiply_reduce_fusion
  30.9 0.0 copy-done
  30.9 0.1 multiply_add_fusion
  31.0 0.6 %maximum_multiply_fusion = f32[6,384]{1,0:T(8,128)} fusion(f32[3,384]{1,0:T(4,128)S(1)} %get-tuple-element.101, f32[3,384]{1,0:T(4,128)S(1)} %get-tuple-element.100, f32[384]{0:T(512)S(1)} %get-tuple-element.118), kind=kLoop, calls=%fused_computation.38 | loop fusion | flops 4608 | bytes 19968 | tf_op jit(solution)/shard_map/mul | solution.py:80
  (13 shorter events, 0.3 us)
Async XLA Ops:
  3.9 16.1 %collective-permute-start = (f32[8,96]{1,0:T(8,128)S(1)}, f32[8,96]{1,0:T(8,128)S(1)}, u32[]{:S(2)}, u32[]{:S(2)}) collective-permute-start(f32[8,96]{1,0:T(8,128)S(1)} %get-tuple-element.122), channel_id=1, source_target_pairs={{0,24},{8,0},{16,8},{24,16},{1,25},{9,1},{17,9},{25,17},{2,26},{10... | collective-permute-start | bytes 9224 | tf_op jit(solution)/shard_map/ppermute | solution.py:162
  8.9 11.1 %collective-permute-start.1 = (f32[8,96]{1,0:T(8,128)S(1)}, f32[8,96]{1,0:T(8,128)S(1)}, u32[]{:S(2)}, u32[]{:S(2)}) collective-permute-start(f32[8,96]{1,0:T(8,128)S(1)} %get-tuple-element.121), channel_id=1, source_target_pairs={{0,16},{8,24},{16,0},{24,8},{1,17},{9,25},{17,1},{25,9},{2,18},{10... | collective-permute-start | bytes 9224 | tf_op jit(solution)/shard_map/ppermute | solution.py:162
  8.9 11.1 %collective-permute-start.2 = (f32[8,96]{1,0:T(8,128)S(1)}, f32[8,96]{1,0:T(8,128)S(1)}, u32[]{:S(2)}, u32[]{:S(2)}) collective-permute-start(f32[8,96]{1,0:T(8,128)S(1)} %get-tuple-element.120), channel_id=1, source_target_pairs={{0,8},{8,16},{16,24},{24,0},{1,9},{9,17},{17,25},{25,1},{2,10},{10... | collective-permute-start | bytes 9224 | tf_op jit(solution)/shard_map/ppermute | solution.py:162
  20.8 10.1 %copy-start = (f32[3]{0:T(128)S(1)}, f32[3]{0:T(128)}, u32[]{:S(2)}) copy-start(f32[3]{0:T(128)} %constant.95) | copy-start | bytes 40

commit v7 on v6

--- a/solution.py
+++ b/solution.py
@@ -25,7 +25,7 @@
 def raw_terms(points, wake_table):
     point_count = points.shape[1]
     wake_count = wake_table.shape[1]
-    wake_width = math.gcd(wake_count, 2048)
+    wake_width = wake_count
     wake_place = wake_table[0:3]
     core_square = wake_table[3]
     tables = wake_table[4:10]

time: 32 us -> 31.8 us (level)
  starting transfers between devices: 6.06 us -> 6.96 us
  local copies, waits for them, and re-layouts: 1.19 us -> 0.69 us
    ppermute x3, starting transfers between devices: 6.06 us -> 6.96 us  [exchange_slots(): lax.ppermute(blocks[(region + shift) % regions], 'region', pairs)]
    slice x10 -> x0, local copies, waits for them, and re-layouts: 0.43 us -> none  [the longest x8 0.4 us: accumulate(): first_gap = point_group[0][:, None] - place_part[0][None, :]]
    dot_general x4 -> x1, matrix products: 9.21 us -> 9.11 us  [accumulate(): lax.dot_general(table_part, kernel, (((1,), (1,)), ((), ())), precision=l...]
where the time goes in v7:
time: 31.8 us; the launch traced here: 31.5 us
  blocking collectives  9.51 us (30%)
  matrix products  9.11 us (29%)
  starting transfers between devices  6.96 us (22%)
  Pallas kernels  2.54 us (8%)
  other arithmetic  1.89 us (6%)
  between operations  0.79 us (2%)
  local copies, waits for them, and re-layouts  0.69 us (2%)
    all_gather x1, blocking collectives, body(): lax.all_gather(wake_table, 'narrow', axis=1, tiled=True)  9.51 us
    dot_general x1, matrix products, accumulate(): lax.dot_general(table_part, kernel, (((1,), (1,)), ((), ())), precision=l...  9.11 us
    ppermute x3, starting transfers between devices, exchange_slots(): lax.ppermute(blocks[(region + shift) % regions], 'region', pairs)  6.96 us
    pallas_call x1, Pallas kernels, prologue(): pl.pallas_call(prologue_kernel, out_shape=(jax.ShapeDtypeStruct((regions,...  2.54 us
    squeeze x1, local copies, waits for them, and re-layouts, exchange_slots(): blocks[(region + shift) % regions]  0.69 us
    select_n x1, other arithmetic, exchange_slots(): block = jnp.where(shift == other, by_shift[other], block)  0.68 us
  transfers between devices with their start and end apart: 3, of which 0 were waited for; matrix products, arithmetic and copies ran while one was open for 1% of the time, Pallas kernels for 0%

profile of v7, /device:TPU:0, one launch (start us, length us, event | category | flops | bytes accessed | tf_op | source)
XLA Modules:
  0.0 31.5 jit_solution(10547654981604601509)
XLA Ops:
  0.7 2.5 %shard_map.91 = (f32[4,8,96]{2,1,0:T(8,128)}, f32[7,1024]{1,0:T(8,128)}) custom-call(s32[1]{0:T(128)S(6)} %copy.10.count_ref, f32[3,192]{1,0:T(4,128)} %pos_ref.1, f32[3,192]{1,0:T(4,128)} %vel_ref.1, f32[1,192]{1,0:T(1,128)} %bitcast.39, s32[1,192]{1,0:T(1,128)} %bitcast.40, f32[3,1024]{1,0:T(4,128)} %wpos_ref.1, f32[3,1024]{1,0:T(4,128)} %wgam_ref.1, ...), custom_call_target="tpu_custom_call" | custom-call | tf_op jit(solution)/shard_map/pallas_call | solution.py:139
  3.2 0.7 %dynamic-slice_bitcast_fusion = (f32[8,96]{1,0:T(8,128)S(1)}, f32[8,96]{1,0:T(8,128)S(1)}, f32[8,96]{1,0:T(8,128)S(1)}) fusion(f32[4,8,96]{2,1,0:T(8,128)} %get-tuple-element.41, s32[]{:T(128)S(6)} %select_n.132, s32[]{:T(128)S(6)} %select_n.129, s32[]{:T(128)S(6)} %select_n.126), kind=kLoop, calls=%fused_computation.47 | loop fusion | bytes 18444 | tf_op jit(solution)/shard_map/squeeze | solution.py:162
  3.9 3.0 %collective-permute-start.2 = (f32[8,96]{1,0:T(8,128)S(1)}, f32[8,96]{1,0:T(8,128)S(1)}, u32[]{:S(2)}, u32[]{:S(2)}) collective-permute-start(f32[8,96]{1,0:T(8,128)S(1)} %get-tuple-element.79), channel_id=1, source_target_pairs={{0,8},{8,16},{16,24},{24,0},{1,9},{9,17},{17,25},{25,1},{2,10},{10... | collective-permute-start | bytes 9224 | tf_op jit(solution)/shard_map/ppermute | solution.py:162
  6.9 2.6 %collective-permute-start.1 = (f32[8,96]{1,0:T(8,128)S(1)}, f32[8,96]{1,0:T(8,128)S(1)}, u32[]{:S(2)}, u32[]{:S(2)}) collective-permute-start(f32[8,96]{1,0:T(8,128)S(1)} %get-tuple-element.80), channel_id=1, source_target_pairs={{0,16},{8,24},{16,0},{24,8},{1,17},{9,25},{17,1},{25,9},{2,18},{10... | collective-permute-start | bytes 9224 | tf_op jit(solution)/shard_map/ppermute | solution.py:162
  9.5 1.3 %collective-permute-start = (f32[8,96]{1,0:T(8,128)S(1)}, f32[8,96]{1,0:T(8,128)S(1)}, u32[]{:S(2)}, u32[]{:S(2)}) collective-permute-start(f32[8,96]{1,0:T(8,128)S(1)} %get-tuple-element.81), channel_id=1, source_target_pairs={{0,24},{8,0},{16,8},{24,16},{1,25},{9,1},{17,9},{25,17},{2,26},{10... | collective-permute-start | bytes 9224 | tf_op jit(solution)/shard_map/ppermute | solution.py:162
  10.8 9.5 %all_gather.3 = f32[7,8192]{1,0:T(8,128)S(1)} all-gather(f32[7,1024]{1,0:T(8,128)} %get-tuple-element.48), channel_id=1, replica_groups=mesh['region'=4,'narrow'=8] {'narrow'}, dimensions={1}, use_global_device_ids=true | all-gather | bytes 258048 | tf_op jit(solution)/shard_map/all_gather | solution.py:185
  20.4 0.2 multiply_subtract_fusion.2
  20.6 0.0 collective-permute-done.2
  20.6 0.0 collective-permute-done.1
  20.7 0.0 collective-permute-done
  20.7 0.7 %fusion.24 = (f32[8,96]{1,0:T(8,128)S(1)}, f32[8,96]{1,0:T(8,128)S(1)}, f32[8,96]{1,0:T(8,128)S(1)}, f32[8,96]{1,0:T(8,128)S(1)}) fusion(f32[8,96]{1,0:T(8,128)S(1)} %collective-permute-done, f32[8,96]{1,0:T(8,128)S(1)} %collective-permute-done.1, f32[8,96]{1,0:T(8,128)S(1)} %collective-permute-done.2, f32[4,8,96]{2,1,0:T(8,128)} %get-tuple-element.41, ...), kind=kLoop, calls=%fused_computation.40 | loop fusion | flops 9216 | bytes 24592 | tf_op jit(solution)/shard_map/jit(_where)/select_n | solution.py:168
  21.3 0.1 fusion.33
  21.4 0.1 pad_maximum_fusion.6
  21.5 0.1 fusion.35
  21.6 0.0 copy-start
  21.7 9.1 %fusion = f32[6,384]{1,0:T(8,128)S(1)} fusion(f32[8192]{0:T(1024)S(1)} %bitcast.34, f32[8192]{0:T(1024)S(1)} %bitcast.37, f32[384]{0:T(512)S(1)} %get-tuple-element.75, f32[8192]{0:T(1024)S(1)} %bitcast.36, f32[384]{0:T(512)S(1)} %get-tuple-element.77, f32[8192]{0:T(1024)S(1)} %bitcast.35, f32[384]{0:T(512)S(1)} %get-tuple-element.57, ...), kind=kOutput, calls=%fused_computation.1 | convolution fusion | flops 147996672 | bytes 472576 | tf_op jit(solution)/shard_map/while/body/eval_jaxpr/while/body/eval_jaxpr/dot_general | solution.py:52
  30.8 0.0 copy-done
  30.8 0.1 slice_add_fusion
  30.9 0.6 %maximum_multiply_fusion = f32[6,384]{1,0:T(8,128)} fusion(f32[3,384]{1,0:T(4,128)S(1)} %get-tuple-element.56, f32[3,384]{1,0:T(4,128)S(1)} %get-tuple-element.55, f32[384]{0:T(512)S(1)} %get-tuple-element.53), kind=kLoop, calls=%fused_computation.27 | loop fusion | flops 4608 | bytes 19968 | tf_op jit(solution)/shard_map/mul | solution.py:80
  (2 shorter events, 0.1 us)
Async XLA Ops:
  3.9 16.8 %collective-permute-start.2 = (f32[8,96]{1,0:T(8,128)S(1)}, f32[8,96]{1,0:T(8,128)S(1)}, u32[]{:S(2)}, u32[]{:S(2)}) collective-permute-start(f32[8,96]{1,0:T(8,128)S(1)} %get-tuple-element.79), channel_id=1, source_target_pairs={{0,8},{8,16},{16,24},{24,0},{1,9},{9,17},{17,25},{25,1},{2,10},{10... | collective-permute-start | bytes 9224 | tf_op jit(solution)/shard_map/ppermute | solution.py:162
  6.9 13.7 %collective-permute-start.1 = (f32[8,96]{1,0:T(8,128)S(1)}, f32[8,96]{1,0:T(8,128)S(1)}, u32[]{:S(2)}, u32[]{:S(2)}) collective-permute-start(f32[8,96]{1,0:T(8,128)S(1)} %get-tuple-element.80), channel_id=1, source_target_pairs={{0,16},{8,24},{16,0},{24,8},{1,17},{9,25},{17,1},{25,9},{2,18},{10... | collective-permute-start | bytes 9224 | tf_op jit(solution)/shard_map/ppermute | solution.py:162
  9.5 11.2 %collective-permute-start = (f32[8,96]{1,0:T(8,128)S(1)}, f32[8,96]{1,0:T(8,128)S(1)}, u32[]{:S(2)}, u32[]{:S(2)}) collective-permute-start(f32[8,96]{1,0:T(8,128)S(1)} %get-tuple-element.81), channel_id=1, source_target_pairs={{0,24},{8,0},{16,8},{24,16},{1,25},{9,1},{17,9},{25,17},{2,26},{10... | collective-permute-start | bytes 9224 | tf_op jit(solution)/shard_map/ppermute | solution.py:162
  21.6 9.2 %copy-start = (f32[3]{0:T(128)S(1)}, f32[3]{0:T(128)}, u32[]{:S(2)}) copy-start(f32[3]{0:T(128)} %constant.95) | copy-start | bytes 40

commit v8 on v6

--- a/solution.py
+++ b/solution.py
@@ -93,7 +93,7 @@
 
 def prologue_kernel(
     count_ref, pos_ref, vel_ref, tau_ref, dest_ref, wpos_ref, wgam_ref, wcore_ref,
-    out_ref, table_ref,
+    out_ref, table_ref, state_ref,
 ):
     regions, _, capacity = out_ref.shape
     per_device = dest_ref.shape[1]
@@ -107,23 +107,21 @@
     slot_rank = jnp.sum(before * onehot, axis=0, keepdims=True).astype(jnp.int32)
     column = target * capacity + slot_rank
     live = lax.broadcasted_iota(jnp.int32, (1, per_device), 1) < count_ref[0]
-    pos = pos_ref[...]
-    vel = vel_ref[...]
-    tau = tau_ref[...]
-    ones = jnp.ones((1, per_device), jnp.bfloat16)
-
-    def one_region(d, carry):
-        slot_id = lax.broadcasted_iota(jnp.int32, (capacity, per_device), 0) + d * capacity
+    state_ref[0:3, :] = pos_ref[...]
+    state_ref[3:6, :] = vel_ref[...]
+    state_ref[6:7, :] = tau_ref[...]
+    state_ref[7:8, :] = jnp.ones((1, per_device), jnp.float32)
+    state = state_ref[...]
+    region = lax.axis_index("region")
+
+    def one_shift(shift, carry):
+        dest_region = (region + shift) % regions
+        slot_id = lax.broadcasted_iota(jnp.int32, (capacity, per_device), 0) + dest_region * capacity
         placing = ((column == slot_id) & live).astype(jnp.bfloat16)
-        out_ref[d, 0:3, :] = exact_place(pos, placing)
-        out_ref[d, 3:6, :] = exact_place(vel, placing)
-        out_ref[d, 6:7, :] = exact_place(tau, placing)
-        out_ref[d, 7:8, :] = lax.dot_general(
-            ones, placing, (((1,), (1,)), ((), ())), preferred_element_type=jnp.float32
-        )
+        out_ref[shift] = exact_place(state, placing)
         return carry
 
-    lax.fori_loop(0, regions, one_region, 0)
+    lax.fori_loop(0, regions, one_shift, 0)
     core = wcore_ref[...]
     table_ref[0:3, :] = wpos_ref[...]
     table_ref[3:4, :] = core * core
@@ -144,22 +142,25 @@
         ),
         in_specs=[pl.BlockSpec(memory_space=pltpu.SMEM)] + [vmem] * 7,
         out_specs=(vmem, vmem),
+        scratch_shapes=[pltpu.VMEM((8, per_device), jnp.float32)],
     )(
         counts, dust_pos, dust_vel, dust_tau.reshape(1, per_device), dest.reshape(1, per_device),
         wake_pos, wake_gamma, wake_core.reshape(1, wake_count),
     )
 
 
-def exchange_slots(blocks):
-    regions, rows, capacity = blocks.shape
+def exchange_slots(by_offset):
+    regions, rows, capacity = by_offset.shape
+    region = lax.axis_index("region")
     if regions > 8:
+        back = (jnp.arange(regions, dtype=jnp.int32) - region) % regions
+        blocks = jnp.take(by_offset, back, axis=0)
         arrived = lax.all_to_all(blocks, "region", split_axis=0, concat_axis=0, tiled=True)
         return arrived.transpose(1, 0, 2).reshape(rows, regions * capacity)
-    region = lax.axis_index("region")
-    by_shift = [blocks[region]]
+    by_shift = [by_offset[0]]
     for shift in range(1, regions):
         pairs = [(i, (i + shift) % regions) for i in range(regions)]
-        by_shift.append(lax.ppermute(blocks[(region + shift) % regions], "region", pairs))
+        by_shift.append(lax.ppermute(by_offset[shift], "region", pairs))
     placed = []
     for source in range(regions):
         shift = (region - source) % regions

time: 32 us -> 31.7 us (level)
  no operation moved by 1% of the time
where the time goes in v8:
time: 31.7 us; the launch traced here: 31.3 us
  blocking collectives  9.51 us (30%)
  matrix products  9.21 us (29%)
  starting transfers between devices  6.06 us (19%)
  Pallas kernels  2.26 us (7%)
  other arithmetic  2.2 us (7%)
  local copies, waits for them, and re-layouts  1.19 us (4%)
  between operations  0.8 us (3%)
    all_gather x1, blocking collectives, body(): lax.all_gather(wake_table, 'narrow', axis=1, tiled=True)  9.51 us
    dot_general x4, matrix products, accumulate(): lax.dot_general(table_part, kernel, (((1,), (1,)), ((), ())), precision=l...  9.21 us
    ppermute x3, starting transfers between devices, exchange_slots(): by_shift.append(lax.ppermute(by_offset[shift], 'region', pairs))  6.06 us
    pallas_call x1, Pallas kernels, prologue(): pl.pallas_call(prologue_kernel, out_shape=(jax.ShapeDtypeStruct((regions,...  2.26 us
    squeeze x1, local copies, waits for them, and re-layouts, exchange_slots(): by_shift.append(lax.ppermute(by_offset[shift], 'region', pairs))  0.69 us
    select_n x1, other arithmetic, exchange_slots(): block = jnp.where(shift == other, by_shift[other], block)  0.68 us
  transfers between devices with their start and end apart: 3, of which 0 were waited for; matrix products, arithmetic and copies ran while one was open for 1% of the time, Pallas kernels for 0%

profile of v8, /device:TPU:0, one launch (start us, length us, event | category | flops | bytes accessed | tf_op | source)
XLA Modules:
  0.0 31.3 jit_solution(2406893361780204095)
XLA Ops:
  0.7 2.3 %shard_map.91 = (f32[4,8,96]{2,1,0:T(8,128)}, f32[7,1024]{1,0:T(8,128)}) custom-call(s32[1]{0:T(128)S(6)} %copy.18.count_ref, f32[3,192]{1,0:T(4,128)} %pos_ref.1, f32[3,192]{1,0:T(4,128)} %vel_ref.1, f32[1,192]{1,0:T(1,128)} %bitcast.60, s32[1,192]{1,0:T(1,128)} %bitcast.61, f32[3,1024]{1,0:T(4,128)} %wpos_ref.1, f32[3,1024]{1,0:T(4,128)} %wgam_ref.1, ...), custom_call_target="tpu_custom_call" | custom-call | tf_op jit(solution)/shard_map/pallas_call | solution.py:137
  2.9 0.7 %slice_bitcast_fusion = (f32[8,96]{1,0:T(8,128)S(1)}, f32[8,96]{1,0:T(8,128)S(1)}, f32[8,96]{1,0:T(8,128)S(1)}) fusion(f32[4,8,96]{2,1,0:T(8,128)} %get-tuple-element.57), kind=kLoop, calls=%fused_computation.58 | loop fusion | bytes 18432 | tf_op jit(solution)/shard_map/squeeze | solution.py:163
  3.6 5.0 %collective-permute-start = (f32[8,96]{1,0:T(8,128)S(1)}, f32[8,96]{1,0:T(8,128)S(1)}, u32[]{:S(2)}, u32[]{:S(2)}) collective-permute-start(f32[8,96]{1,0:T(8,128)S(1)} %get-tuple-element.122), channel_id=1, source_target_pairs={{0,24},{8,0},{16,8},{24,16},{1,25},{9,1},{17,9},{25,17},{2,26},{10... | collective-permute-start | bytes 9224 | tf_op jit(solution)/shard_map/ppermute | solution.py:163
  8.6 0.0 collective-permute-start.1
  8.7 1.0 %collective-permute-start.2 = (f32[8,96]{1,0:T(8,128)S(1)}, f32[8,96]{1,0:T(8,128)S(1)}, u32[]{:S(2)}, u32[]{:S(2)}) collective-permute-start(f32[8,96]{1,0:T(8,128)S(1)} %get-tuple-element.120), channel_id=1, source_target_pairs={{0,8},{8,16},{16,24},{24,0},{1,9},{9,17},{17,25},{25,1},{2,10},{10... | collective-permute-start | bytes 9224 | tf_op jit(solution)/shard_map/ppermute | solution.py:163
  9.7 9.5 %all_gather.3 = f32[7,8192]{1,0:T(8,128)S(1)} all-gather(f32[7,1024]{1,0:T(8,128)} %get-tuple-element.58), channel_id=1, replica_groups=mesh['region'=4,'narrow'=8] {'narrow'}, dimensions={1}, use_global_device_ids=true | all-gather | bytes 258048 | tf_op jit(solution)/shard_map/all_gather | solution.py:186
  19.2 0.3 slice_reduce_fusion.3
  19.4 0.1 pad_maximum_fusion
  19.7 0.0 collective-permute-done
  19.7 0.0 collective-permute-done.1
  19.7 0.0 collective-permute-done.2
  19.8 0.7 %fusion.26 = (f32[8,96]{1,0:T(8,128)S(1)}, f32[8,96]{1,0:T(8,128)S(1)}, f32[8,96]{1,0:T(8,128)S(1)}, f32[8,96]{1,0:T(8,128)S(1)}) fusion(f32[8,96]{1,0:T(8,128)S(1)} %collective-permute-done, f32[8,96]{1,0:T(8,128)S(1)} %collective-permute-done.1, f32[8,96]{1,0:T(8,128)S(1)} %collective-permute-done.2, f32[4,8,96]{2,1,0:T(8,128)} %get-tuple-element.57, ...), kind=kLoop, calls=%fused_computation.51 | loop fusion | flops 9216 | bytes 24588 | tf_op jit(solution)/shard_map/jit(_where)/select_n | solution.py:169
  20.4 0.1 pad_maximum_fusion.3
  20.5 0.0 copy-start
  20.5 9.8 %while.18 = (s32[]{:T(128)}, f32[6,384]{1,0:T(8,128)S(1)}, f32[4,6,2048]{2,1,0:T(8,128)S(1)}, f32[3,384]{1,0:T(4,128)S(1)}, f32[4,3,2048]{2,1,0:T(4,128)S(1)}, /...) while((s32[]{:T(128)}, f32[6,384]{1,0:T(8,128)S(1)}, ...), condition=%wide.region_1.2_spmd.clone, body=%wide.region_0.1_spmd.clone.sunk | while | flops 36966916 | bytes 200859 | solution.py:57
  20.6 2.3 %fusion.39 = f32[6,384]{1,0:T(8,128)S(1)} fusion(f32[2048]{0:T(1024)S(1)} %bitcast.58, f32[2048]{0:T(1024)S(1)} %bitcast.57, f32[384]{0:T(512)S(1)} %get-tuple-element.168, f32[2048]{0:T(1024)S(1)} %bitcast.56, f32[384]{0:T(512)S(1)} %get-tuple-element.170, f32[2048]{0:T(1024)S(1)} %bitcast.55, f32[384]{0:T(512)S(1)} %get-tuple-element.172, ...), kind=kOutput, calls=%fused_computation.19.clone.1 | convolution fusion | flops 36966912 | bytes 125957 | tf_op jit(solution)/shard_map/while/body/eval_jaxpr/while/body/eval_jaxpr/dot_general | solution.py:52
  22.9 0.1 constant_dynamic-slice_fusion.7
  23.1 2.3 %fusion.39 = f32[6,384]{1,0:T(8,128)S(1)} fusion(f32[2048]{0:T(1024)S(1)} %bitcast.58, f32[2048]{0:T(1024)S(1)} %bitcast.57, f32[384]{0:T(512)S(1)} %get-tuple-element.168, f32[2048]{0:T(1024)S(1)} %bitcast.56, f32[384]{0:T(512)S(1)} %get-tuple-element.170, f32[2048]{0:T(1024)S(1)} %bitcast.55, f32[384]{0:T(512)S(1)} %get-tuple-element.172, ...), kind=kOutput, calls=%fused_computation.19.clone.1 | convolution fusion | flops 36966912 | bytes 125957 | tf_op jit(solution)/shard_map/while/body/eval_jaxpr/while/body/eval_jaxpr/dot_general | solution.py:52
  25.4 0.1 constant_dynamic-slice_fusion.7
  25.5 2.3 %fusion.39 = f32[6,384]{1,0:T(8,128)S(1)} fusion(f32[2048]{0:T(1024)S(1)} %bitcast.58, f32[2048]{0:T(1024)S(1)} %bitcast.57, f32[384]{0:T(512)S(1)} %get-tuple-element.168, f32[2048]{0:T(1024)S(1)} %bitcast.56, f32[384]{0:T(512)S(1)} %get-tuple-element.170, f32[2048]{0:T(1024)S(1)} %bitcast.55, f32[384]{0:T(512)S(1)} %get-tuple-element.172, ...), kind=kOutput, calls=%fused_computation.19.clone.1 | convolution fusion | flops 36966912 | bytes 125957 | tf_op jit(solution)/shard_map/while/body/eval_jaxpr/while/body/eval_jaxpr/dot_general | solution.py:52
  27.8 0.1 constant_dynamic-slice_fusion.7
  28.0 2.3 %fusion.39 = f32[6,384]{1,0:T(8,128)S(1)} fusion(f32[2048]{0:T(1024)S(1)} %bitcast.58, f32[2048]{0:T(1024)S(1)} %bitcast.57, f32[384]{0:T(512)S(1)} %get-tuple-element.168, f32[2048]{0:T(1024)S(1)} %bitcast.56, f32[384]{0:T(512)S(1)} %get-tuple-element.170, f32[2048]{0:T(1024)S(1)} %bitcast.55, f32[384]{0:T(512)S(1)} %get-tuple-element.172, ...), kind=kOutput, calls=%fused_computation.19.clone.1 | convolution fusion | flops 36966912 | bytes 125957 | tf_op jit(solution)/shard_map/while/body/eval_jaxpr/while/body/eval_jaxpr/dot_general | solution.py:52
  30.3 0.1 multiply_subtract_fusion.5
  30.4 0.1 multiply_subtract_fusion.4
  30.5 0.1 multiply_reduce_fusion
  30.6 0.0 copy-done
  30.6 0.1 multiply_add_fusion
  30.7 0.6 %maximum_multiply_fusion = f32[6,384]{1,0:T(8,128)} fusion(f32[3,384]{1,0:T(4,128)S(1)} %get-tuple-element.101, f32[3,384]{1,0:T(4,128)S(1)} %get-tuple-element.100, f32[384]{0:T(512)S(1)} %get-tuple-element.118), kind=kLoop, calls=%fused_computation.38 | loop fusion | flops 4608 | bytes 19968 | tf_op jit(solution)/shard_map/mul | solution.py:80
  (13 shorter events, 0.2 us)
Async XLA Ops:
  3.6 16.1 %collective-permute-start = (f32[8,96]{1,0:T(8,128)S(1)}, f32[8,96]{1,0:T(8,128)S(1)}, u32[]{:S(2)}, u32[]{:S(2)}) collective-permute-start(f32[8,96]{1,0:T(8,128)S(1)} %get-tuple-element.122), channel_id=1, source_target_pairs={{0,24},{8,0},{16,8},{24,16},{1,25},{9,1},{17,9},{25,17},{2,26},{10... | collective-permute-start | bytes 9224 | tf_op jit(solution)/shard_map/ppermute | solution.py:163
  8.6 11.1 %collective-permute-start.1 = (f32[8,96]{1,0:T(8,128)S(1)}, f32[8,96]{1,0:T(8,128)S(1)}, u32[]{:S(2)}, u32[]{:S(2)}) collective-permute-start(f32[8,96]{1,0:T(8,128)S(1)} %get-tuple-element.121), channel_id=1, source_target_pairs={{0,16},{8,24},{16,0},{24,8},{1,17},{9,25},{17,1},{25,9},{2,18},{10... | collective-permute-start | bytes 9224 | tf_op jit(solution)/shard_map/ppermute | solution.py:163
  8.7 11.1 %collective-permute-start.2 = (f32[8,96]{1,0:T(8,128)S(1)}, f32[8,96]{1,0:T(8,128)S(1)}, u32[]{:S(2)}, u32[]{:S(2)}) collective-permute-start(f32[8,96]{1,0:T(8,128)S(1)} %get-tuple-element.120), channel_id=1, source_target_pairs={{0,8},{8,16},{16,24},{24,0},{1,9},{9,17},{17,25},{25,1},{2,10},{10... | collective-permute-start | bytes 9224 | tf_op jit(solution)/shard_map/ppermute | solution.py:163
  20.5 10.1 %copy-start = (f32[3]{0:T(128)S(1)}, f32[3]{0:T(128)}, u32[]{:S(2)}) copy-start(f32[3]{0:T(128)} %constant.83) | copy-start | bytes 40

commit v9 on v8

--- a/solution.py
+++ b/solution.py
@@ -92,10 +92,12 @@
 
 
 def prologue_kernel(
-    count_ref, pos_ref, vel_ref, tau_ref, dest_ref, wpos_ref, wgam_ref, wcore_ref,
-    out_ref, table_ref, state_ref,
+    count_ref, pos_ref, vel_ref, tau_ref, dest_ref, wpos_ref, wgam_ref, wcore_ref, *refs
 ):
-    regions, _, capacity = out_ref.shape
+    out_refs = refs[:-2]
+    table_ref, state_ref = refs[-2:]
+    regions = len(out_refs)
+    capacity = out_refs[0].shape[1]
     per_device = dest_ref.shape[1]
     target = dest_ref[...]
     region_id = lax.broadcasted_iota(jnp.int32, (regions, per_device), 0)
@@ -114,14 +116,11 @@
     state = state_ref[...]
     region = lax.axis_index("region")
 
-    def one_shift(shift, carry):
+    for shift, out_ref in enumerate(out_refs):
         dest_region = (region + shift) % regions
         slot_id = lax.broadcasted_iota(jnp.int32, (capacity, per_device), 0) + dest_region * capacity
         placing = ((column == slot_id) & live).astype(jnp.bfloat16)
-        out_ref[shift] = exact_place(state, placing)
-        return carry
-
-    lax.fori_loop(0, regions, one_shift, 0)
+        out_ref[...] = exact_place(state, placing)
     core = wcore_ref[...]
     table_ref[0:3, :] = wpos_ref[...]
     table_ref[3:4, :] = core * core
@@ -136,12 +135,12 @@
     vmem = pl.BlockSpec(memory_space=pltpu.VMEM)
     return pl.pallas_call(
         prologue_kernel,
-        out_shape=(
-            jax.ShapeDtypeStruct((regions, 8, capacity), jnp.float32),
-            jax.ShapeDtypeStruct((7, wake_count), jnp.float32),
+        out_shape=tuple(
+            [jax.ShapeDtypeStruct((8, capacity), jnp.float32)] * regions
+            + [jax.ShapeDtypeStruct((7, wake_count), jnp.float32)]
         ),
         in_specs=[pl.BlockSpec(memory_space=pltpu.SMEM)] + [vmem] * 7,
-        out_specs=(vmem, vmem),
+        out_specs=tuple([vmem] * (regions + 1)),
         scratch_shapes=[pltpu.VMEM((8, per_device), jnp.float32)],
     )(
         counts, dust_pos, dust_vel, dust_tau.reshape(1, per_device), dest.reshape(1, per_device),
@@ -150,9 +149,11 @@
 
 
 def exchange_slots(by_offset):
-    regions, rows, capacity = by_offset.shape
+    regions = len(by_offset)
+    rows, capacity = by_offset[0].shape
     region = lax.axis_index("region")
     if regions > 8:
+        by_offset = jnp.stack(by_offset)
         back = (jnp.arange(regions, dtype=jnp.int32) - region) % regions
         blocks = jnp.take(by_offset, back, axis=0)
         arrived = lax.all_to_all(blocks, "region", split_axis=0, concat_axis=0, tiled=True)
@@ -178,10 +179,10 @@
 
 
 def body(dust_pos, dust_vel, dust_tau, dest, counts, wake_pos, wake_gamma, wake_core):
-    outgoing, wake_table = prologue(
+    *outgoing, wake_table = prologue(
         dust_pos, dust_vel, dust_tau, dest, counts, wake_pos, wake_gamma, wake_core
     )
-    outgoing, wake_table = lax.optimization_barrier((outgoing, wake_table))
+    outgoing, wake_table = lax.optimization_barrier((tuple(outgoing), wake_table))
     arrived = exchange_slots(outgoing)
     region_table = wake_tables(lax.all_gather(wake_table, "narrow", axis=1, tiled=True))
     points = arrived[0:3]

time: 31.7 us -> 30.4 us (0.959)
  other arithmetic: 2.2 us -> 1.52 us
  Pallas kernels: 2.26 us -> 1.84 us
    squeeze x1 -> x0, local copies, waits for them, and re-layouts: 0.69 us -> none  [exchange_slots(): by_shift.append(lax.ppermute(by_offset[shift], 'region', pairs))]
    select_n x1, other arithmetic: 0.68 us -> 0.01 us  [exchange_slots(): block = jnp.where(shift == other, by_shift[other], block)]
    unnamed x2 -> x4, local copies, waits for them, and re-layouts: 0.01 us -> 0.51 us
    pallas_call x1, Pallas kernels: 2.26 us -> 1.84 us  [prologue(): pl.pallas_call(prologue_kernel, out_shape=tuple([jax.ShapeDtypeStruct((8,...]
where the time goes in v9:
time: 30.4 us; the launch traced here: 30.1 us
  blocking collectives  9.51 us (31%)
  matrix products  9.21 us (30%)
  starting transfers between devices  6.06 us (20%)
  Pallas kernels  1.84 us (6%)
  other arithmetic  1.52 us (5%)
  local copies, waits for them, and re-layouts  1.02 us (3%)
  between operations  0.81 us (3%)
    all_gather x1, blocking collectives, body(): lax.all_gather(wake_table, 'narrow', axis=1, tiled=True)  9.51 us
    dot_general x4, matrix products, accumulate(): lax.dot_general(table_part, kernel, (((1,), (1,)), ((), ())), precision=l...  9.21 us
    ppermute x3, starting transfers between devices, exchange_slots(): by_shift.append(lax.ppermute(by_offset[shift], 'region', pairs))  6.06 us
    pallas_call x1, Pallas kernels, prologue(): pl.pallas_call(prologue_kernel, out_shape=tuple([jax.ShapeDtypeStruct((8,...  1.84 us
    mul x1, other arithmetic, advance(): jnp.concatenate([new_place, new_velocity], axis=0) * live_flag[None, :]  0.61 us
  transfers between devices with their start and end apart: 3, of which 0 were waited for; matrix products, arithmetic and copies ran while one was open for 1% of the time, Pallas kernels for 0%

profile of v9, /device:TPU:0, one launch (start us, length us, event | category | flops | bytes accessed | tf_op | source)
XLA Modules:
  0.0 30.1 jit_solution(4259974863033655106)
XLA Ops:
  0.7 1.8 %shard_map.91 = (f32[8,96]{1,0:T(8,128)}, f32[8,96]{1,0:T(8,128)}, f32[8,96]{1,0:T(8,128)}, f32[8,96]{1,0:T(8,128)}, f32[7,1024]{1,0:T(8,128)}) custom-call(s32[1]{0:T(128)S(6)} %copy.18.count_ref, f32[3,192]{1,0:T(4,128)} %pos_ref.1, f32[3,192]{1,0:T(4,128)} %vel_ref.1, f32[1,192]{1,0:T(1,128)} %bitcast.33, s32[1,192]{1,0:T(1,128)} %bitcast.34, ...), custom_call_target="tpu_custom_call" | custom-call | tf_op jit(solution)/shard_map/pallas_call | solution.py:136
  2.5 5.0 %collective-permute-start = (f32[8,96]{1,0:T(8,128)}, f32[8,96]{1,0:T(8,128)S(1)}, u32[]{:S(2)}, u32[]{:S(2)}) collective-permute-start(f32[8,96]{1,0:T(8,128)} %get-tuple-element.60), channel_id=1, source_target_pairs={{0,24},{8,0},{16,8},{24,16},{1,25},{9,1},{17,9},{25,17},{2,26},{10... | collective-permute-start | bytes 9224 | tf_op jit(solution)/shard_map/ppermute | solution.py:164
  7.5 0.0 collective-permute-start.1
  7.5 1.0 %collective-permute-start.2 = (f32[8,96]{1,0:T(8,128)}, f32[8,96]{1,0:T(8,128)S(1)}, u32[]{:S(2)}, u32[]{:S(2)}) collective-permute-start(f32[8,96]{1,0:T(8,128)} %get-tuple-element.62), channel_id=1, source_target_pairs={{0,8},{8,16},{16,24},{24,0},{1,9},{9,17},{17,25},{25,1},{2,10},{10... | collective-permute-start | bytes 9224 | tf_op jit(solution)/shard_map/ppermute | solution.py:164
  8.6 9.5 %all_gather.3 = f32[7,8192]{1,0:T(8,128)S(1)} all-gather(f32[7,1024]{1,0:T(8,128)} %get-tuple-element.64), channel_id=1, replica_groups=mesh['region'=4,'narrow'=8] {'narrow'}, dimensions={1}, use_global_device_ids=true | all-gather | bytes 258048 | tf_op jit(solution)/shard_map/all_gather | solution.py:187
  18.1 0.3 slice_reduce_fusion.3
  18.3 0.1 pad_maximum_fusion
  18.5 0.0 copy-start
  18.6 0.0 collective-permute-done
  18.6 0.0 collective-permute-done.1
  18.6 0.0 collective-permute-done.2
  18.7 0.5 %copy-done = f32[8,96]{1,0:T(8,128)S(1)} copy-done((f32[8,96]{1,0:T(8,128)S(1)}, f32[8,96]{1,0:T(8,128)}, u32[]{:S(2)}) %copy-start) | copy-done | bytes 3096
  19.2 0.1 pad_maximum_fusion.3
  19.3 0.0 copy-start.1
  19.3 9.8 %while.18 = (s32[]{:T(128)}, f32[6,384]{1,0:T(8,128)S(1)}, f32[4,6,2048]{2,1,0:T(8,128)S(1)}, f32[3,384]{1,0:T(4,128)S(1)}, f32[4,3,2048]{2,1,0:T(4,128)S(1)}, /...) while((s32[]{:T(128)}, f32[6,384]{1,0:T(8,128)S(1)}, ...), condition=%wide.region_1.2_spmd.clone, body=%wide.region_0.1_spmd.clone.sunk | while | flops 36966916 | bytes 200859 | solution.py:57
  19.4 2.3 %fusion.31 = f32[6,384]{1,0:T(8,128)S(1)} fusion(f32[2048]{0:T(1024)S(1)} %bitcast.31, f32[2048]{0:T(1024)S(1)} %bitcast.30, f32[384]{0:T(512)S(1)} %get-tuple-element.171, f32[2048]{0:T(1024)S(1)} %bitcast.29, f32[384]{0:T(512)S(1)} %get-tuple-element.173, f32[2048]{0:T(1024)S(1)} %bitcast.28, f32[384]{0:T(512)S(1)} %get-tuple-element.175, ...), kind=kOutput, calls=%fused_computation.19.clone.1 | convolution fusion | flops 36966912 | bytes 125957 | tf_op jit(solution)/shard_map/while/body/eval_jaxpr/while/body/eval_jaxpr/dot_general | solution.py:52
  21.7 0.1 constant_dynamic-slice_fusion.7
  21.8 2.3 %fusion.31 = f32[6,384]{1,0:T(8,128)S(1)} fusion(f32[2048]{0:T(1024)S(1)} %bitcast.31, f32[2048]{0:T(1024)S(1)} %bitcast.30, f32[384]{0:T(512)S(1)} %get-tuple-element.171, f32[2048]{0:T(1024)S(1)} %bitcast.29, f32[384]{0:T(512)S(1)} %get-tuple-element.173, f32[2048]{0:T(1024)S(1)} %bitcast.28, f32[384]{0:T(512)S(1)} %get-tuple-element.175, ...), kind=kOutput, calls=%fused_computation.19.clone.1 | convolution fusion | flops 36966912 | bytes 125957 | tf_op jit(solution)/shard_map/while/body/eval_jaxpr/while/body/eval_jaxpr/dot_general | solution.py:52
  24.1 0.1 constant_dynamic-slice_fusion.7
  24.3 2.3 %fusion.31 = f32[6,384]{1,0:T(8,128)S(1)} fusion(f32[2048]{0:T(1024)S(1)} %bitcast.31, f32[2048]{0:T(1024)S(1)} %bitcast.30, f32[384]{0:T(512)S(1)} %get-tuple-element.171, f32[2048]{0:T(1024)S(1)} %bitcast.29, f32[384]{0:T(512)S(1)} %get-tuple-element.173, f32[2048]{0:T(1024)S(1)} %bitcast.28, f32[384]{0:T(512)S(1)} %get-tuple-element.175, ...), kind=kOutput, calls=%fused_computation.19.clone.1 | convolution fusion | flops 36966912 | bytes 125957 | tf_op jit(solution)/shard_map/while/body/eval_jaxpr/while/body/eval_jaxpr/dot_general | solution.py:52
  26.6 0.1 constant_dynamic-slice_fusion.7
  26.7 2.3 %fusion.31 = f32[6,384]{1,0:T(8,128)S(1)} fusion(f32[2048]{0:T(1024)S(1)} %bitcast.31, f32[2048]{0:T(1024)S(1)} %bitcast.30, f32[384]{0:T(512)S(1)} %get-tuple-element.171, f32[2048]{0:T(1024)S(1)} %bitcast.29, f32[384]{0:T(512)S(1)} %get-tuple-element.173, f32[2048]{0:T(1024)S(1)} %bitcast.28, f32[384]{0:T(512)S(1)} %get-tuple-element.175, ...), kind=kOutput, calls=%fused_computation.19.clone.1 | convolution fusion | flops 36966912 | bytes 125957 | tf_op jit(solution)/shard_map/while/body/eval_jaxpr/while/body/eval_jaxpr/dot_general | solution.py:52
  29.0 0.1 multiply_subtract_fusion.5
  29.2 0.1 multiply_subtract_fusion.4
  29.3 0.1 multiply_reduce_fusion
  29.4 0.0 copy-done.1
  29.4 0.1 multiply_add_fusion
  29.5 0.6 %maximum_multiply_fusion = f32[6,384]{1,0:T(8,128)} fusion(f32[3,384]{1,0:T(4,128)S(1)} %get-tuple-element.107, f32[3,384]{1,0:T(4,128)S(1)} %get-tuple-element.106, f32[384]{0:T(512)S(1)} %get-tuple-element.120), kind=kLoop, calls=%fused_computation.38 | loop fusion | flops 4608 | bytes 19968 | tf_op jit(solution)/shard_map/mul | solution.py:80
  (14 shorter events, 0.3 us)
Async XLA Ops:
  2.5 16.1 %collective-permute-start = (f32[8,96]{1,0:T(8,128)}, f32[8,96]{1,0:T(8,128)S(1)}, u32[]{:S(2)}, u32[]{:S(2)}) collective-permute-start(f32[8,96]{1,0:T(8,128)} %get-tuple-element.60), channel_id=1, source_target_pairs={{0,24},{8,0},{16,8},{24,16},{1,25},{9,1},{17,9},{25,17},{2,26},{10... | collective-permute-start | bytes 9224 | tf_op jit(solution)/shard_map/ppermute | solution.py:164
  7.5 11.1 %collective-permute-start.1 = (f32[8,96]{1,0:T(8,128)}, f32[8,96]{1,0:T(8,128)S(1)}, u32[]{:S(2)}, u32[]{:S(2)}) collective-permute-start(f32[8,96]{1,0:T(8,128)} %get-tuple-element.61), channel_id=1, source_target_pairs={{0,16},{8,24},{16,0},{24,8},{1,17},{9,25},{17,1},{25,9},{2,18},{10... | collective-permute-start | bytes 9224 | tf_op jit(solution)/shard_map/ppermute | solution.py:164
  7.5 11.1 %collective-permute-start.2 = (f32[8,96]{1,0:T(8,128)}, f32[8,96]{1,0:T(8,128)S(1)}, u32[]{:S(2)}, u32[]{:S(2)}) collective-permute-start(f32[8,96]{1,0:T(8,128)} %get-tuple-element.62), channel_id=1, source_target_pairs={{0,8},{8,16},{16,24},{24,0},{1,9},{9,17},{17,25},{25,1},{2,10},{10... | collective-permute-start | bytes 9224 | tf_op jit(solution)/shard_map/ppermute | solution.py:164
  18.5 0.7 %copy-start = (f32[8,96]{1,0:T(8,128)S(1)}, f32[8,96]{1,0:T(8,128)}, u32[]{:S(2)}) copy-start(f32[8,96]{1,0:T(8,128)} %get-tuple-element.63) | copy-start | bytes 9220
  19.3 10.1 %copy-start.1 = (f32[3]{0:T(128)S(1)}, f32[3]{0:T(128)}, u32[]{:S(2)}) copy-start(f32[3]{0:T(128)} %constant.83) | copy-start | bytes 40

commit v10 on v9

--- a/solution.py
+++ b/solution.py
@@ -50,16 +50,16 @@
             inverse_root = lax.rsqrt(distance_sq)
             kernel = inverse_root * inverse_root * inverse_root
             product = lax.dot_general(
-                table_part, kernel, (((1,), (1,)), ((), ())), precision=lax.Precision.HIGH
+                kernel, table_part, (((1,), (1,)), ((), ())), precision=lax.Precision.HIGH
             )
             return (running + product, None)
 
         total, _ = lax.scan(
             accumulate,
-            jnp.zeros((6, point_count), jnp.float32),
+            jnp.zeros((point_count, 6), jnp.float32),
             (place_blocks, table_blocks, core_blocks),
         )
-        return total
+        return total.T
 
     result = lax.map(one_block, point_blocks)
     return result.transpose(1, 0, 2).reshape(6, point_count)

time: 30.4 us -> 30.6 us (level)
  matrix products: 9.21 us -> 9.63 us
    dot_general x4, matrix products: 9.21 us -> 9.63 us  [accumulate(): lax.dot_general(kernel, table_part, (((1,), (1,)), ((), ())), precision=l...]
where the time goes in v10:
time: 30.6 us; the launch traced here: 30.3 us
  matrix products  9.63 us (31%)
  blocking collectives  9.51 us (31%)
  starting transfers between devices  6.06 us (20%)
  Pallas kernels  1.84 us (6%)
  other arithmetic  1.47 us (5%)
  local copies, waits for them, and re-layouts  0.89 us (3%)
  between operations  0.81 us (3%)
    dot_general x4, matrix products, accumulate(): lax.dot_general(kernel, table_part, (((1,), (1,)), ((), ())), precision=l...  9.63 us
    all_gather x1, blocking collectives, body(): lax.all_gather(wake_table, 'narrow', axis=1, tiled=True)  9.51 us
    ppermute x3, starting transfers between devices, exchange_slots(): by_shift.append(lax.ppermute(by_offset[shift], 'region', pairs))  6.06 us
    pallas_call x1, Pallas kernels, prologue(): pl.pallas_call(prologue_kernel, out_shape=tuple([jax.ShapeDtypeStruct((8,...  1.84 us
  transfers between devices with their start and end apart: 3, of which 0 were waited for; matrix products, arithmetic and copies ran while one was open for 1% of the time, Pallas kernels for 0%

profile of v10, /device:TPU:0, one launch (start us, length us, event | category | flops | bytes accessed | tf_op | source)
XLA Modules:
  0.0 30.3 jit_solution(12819806189020402660)
XLA Ops:
  0.7 1.8 %shard_map.91 = (f32[8,96]{1,0:T(8,128)}, f32[8,96]{1,0:T(8,128)}, f32[8,96]{1,0:T(8,128)}, f32[8,96]{1,0:T(8,128)}, f32[7,1024]{1,0:T(8,128)}) custom-call(s32[1]{0:T(128)S(6)} %copy.18.count_ref, f32[3,192]{1,0:T(4,128)} %pos_ref.1, f32[3,192]{1,0:T(4,128)} %vel_ref.1, f32[1,192]{1,0:T(1,128)} %bitcast.38, s32[1,192]{1,0:T(1,128)} %bitcast.39, ...), custom_call_target="tpu_custom_call" | custom-call | tf_op jit(solution)/shard_map/pallas_call | solution.py:136
  2.5 5.0 %collective-permute-start = (f32[8,96]{1,0:T(8,128)}, f32[8,96]{1,0:T(8,128)S(1)}, u32[]{:S(2)}, u32[]{:S(2)}) collective-permute-start(f32[8,96]{1,0:T(8,128)} %get-tuple-element.60), channel_id=1, source_target_pairs={{0,24},{8,0},{16,8},{24,16},{1,25},{9,1},{17,9},{25,17},{2,26},{10... | collective-permute-start | bytes 9224 | tf_op jit(solution)/shard_map/ppermute | solution.py:164
  7.5 0.0 collective-permute-start.1
  7.5 1.0 %collective-permute-start.2 = (f32[8,96]{1,0:T(8,128)}, f32[8,96]{1,0:T(8,128)S(1)}, u32[]{:S(2)}, u32[]{:S(2)}) collective-permute-start(f32[8,96]{1,0:T(8,128)} %get-tuple-element.62), channel_id=1, source_target_pairs={{0,8},{8,16},{16,24},{24,0},{1,9},{9,17},{17,25},{25,1},{2,10},{10... | collective-permute-start | bytes 9224 | tf_op jit(solution)/shard_map/ppermute | solution.py:164
  8.6 9.5 %all_gather.3 = f32[7,8192]{1,0:T(8,128)S(1)} all-gather(f32[7,1024]{1,0:T(8,128)} %get-tuple-element.64), channel_id=1, replica_groups=mesh['region'=4,'narrow'=8] {'narrow'}, dimensions={1}, use_global_device_ids=true | all-gather | bytes 258048 | tf_op jit(solution)/shard_map/all_gather | solution.py:187
  18.1 0.3 multiply_subtract_fusion.2
  18.3 0.1 pad_maximum_fusion
  18.5 0.0 copy-start
  18.6 0.0 collective-permute-done
  18.6 0.0 collective-permute-done.1
  18.6 0.0 collective-permute-done.2
  18.7 0.5 %copy-done = f32[8,96]{1,0:T(8,128)S(1)} copy-done((f32[8,96]{1,0:T(8,128)S(1)}, f32[8,96]{1,0:T(8,128)}, u32[]{:S(2)}) %copy-start) | copy-done | bytes 3096
  19.2 0.1 pad_maximum_fusion.3
  19.3 0.0 copy-start.1
  19.3 10.0 %while.18 = (s32[]{:T(128)}, f32[384,6]{0,1:T(8,128)S(1)}, f32[3,384]{1,0:T(4,128)S(1)}, f32[4,3,2048]{2,1,0:T(4,128)S(1)}, f32[4,2048]{1,0:T(4,128)S(1)}, /*ind...) while((s32[]{:T(128)}, f32[384,6]{0,1:T(8,128)S(1)}, f32[3,384]{1,0:T(4,128)S(1)}, ...), condition=%wide.region_1.2_spmd.clone, body=%wide.region_0.1_spmd.clone.sunk | while | flops 36966916 | bytes 200859 | solution.py:57
  19.4 2.4 %fusion.32 = f32[384,6]{0,1:T(8,128)S(1)} fusion(f32[2048]{0:T(1024)S(1)} %bitcast.32, f32[2048]{0:T(1024)S(1)} %bitcast.31, f32[384]{0:T(512)S(1)} %get-tuple-element.171, f32[2048]{0:T(1024)S(1)} %bitcast.30, f32[384]{0:T(512)S(1)} %get-tuple-element.173, f32[2048]{0:T(1024)S(1)} %bitcast.29, f32[384]{0:T(512)S(1)} %get-tuple-element.175, ...), kind=kOutput, calls=%fused_computation.19.clone.1 | convolution fusion | flops 36966912 | bytes 125957 | tf_op jit(solution)/shard_map/while/body/eval_jaxpr/while/body/eval_jaxpr/dot_general | solution.py:52
  21.9 2.4 %fusion.32 = f32[384,6]{0,1:T(8,128)S(1)} fusion(f32[2048]{0:T(1024)S(1)} %bitcast.32, f32[2048]{0:T(1024)S(1)} %bitcast.31, f32[384]{0:T(512)S(1)} %get-tuple-element.171, f32[2048]{0:T(1024)S(1)} %bitcast.30, f32[384]{0:T(512)S(1)} %get-tuple-element.173, f32[2048]{0:T(1024)S(1)} %bitcast.29, f32[384]{0:T(512)S(1)} %get-tuple-element.175, ...), kind=kOutput, calls=%fused_computation.19.clone.1 | convolution fusion | flops 36966912 | bytes 125957 | tf_op jit(solution)/shard_map/while/body/eval_jaxpr/while/body/eval_jaxpr/dot_general | solution.py:52
  24.4 2.4 %fusion.32 = f32[384,6]{0,1:T(8,128)S(1)} fusion(f32[2048]{0:T(1024)S(1)} %bitcast.32, f32[2048]{0:T(1024)S(1)} %bitcast.31, f32[384]{0:T(512)S(1)} %get-tuple-element.171, f32[2048]{0:T(1024)S(1)} %bitcast.30, f32[384]{0:T(512)S(1)} %get-tuple-element.173, f32[2048]{0:T(1024)S(1)} %bitcast.29, f32[384]{0:T(512)S(1)} %get-tuple-element.175, ...), kind=kOutput, calls=%fused_computation.19.clone.1 | convolution fusion | flops 36966912 | bytes 125957 | tf_op jit(solution)/shard_map/while/body/eval_jaxpr/while/body/eval_jaxpr/dot_general | solution.py:52
  26.9 2.4 %fusion.32 = f32[384,6]{0,1:T(8,128)S(1)} fusion(f32[2048]{0:T(1024)S(1)} %bitcast.32, f32[2048]{0:T(1024)S(1)} %bitcast.31, f32[384]{0:T(512)S(1)} %get-tuple-element.171, f32[2048]{0:T(1024)S(1)} %bitcast.30, f32[384]{0:T(512)S(1)} %get-tuple-element.173, f32[2048]{0:T(1024)S(1)} %bitcast.29, f32[384]{0:T(512)S(1)} %get-tuple-element.175, ...), kind=kOutput, calls=%fused_computation.19.clone.1 | convolution fusion | flops 36966912 | bytes 125957 | tf_op jit(solution)/shard_map/while/body/eval_jaxpr/while/body/eval_jaxpr/dot_general | solution.py:52
  29.3 0.1 multiply_subtract_fusion.5
  29.4 0.1 multiply_subtract_fusion.4
  29.5 0.1 multiply_reduce_fusion
  29.6 0.0 copy-done.1
  29.6 0.1 multiply_add_fusion
  29.7 0.6 %maximum_multiply_fusion = f32[6,384]{1,0:T(8,128)} fusion(f32[3,384]{1,0:T(4,128)S(1)} %get-tuple-element.107, f32[3,384]{1,0:T(4,128)S(1)} %get-tuple-element.106, f32[384]{0:T(512)S(1)} %get-tuple-element.120), kind=kLoop, calls=%fused_computation.38 | loop fusion | flops 4608 | bytes 19968 | tf_op jit(solution)/shard_map/mul | solution.py:80
  (17 shorter events, 0.4 us)
Async XLA Ops:
  2.5 16.1 %collective-permute-start = (f32[8,96]{1,0:T(8,128)}, f32[8,96]{1,0:T(8,128)S(1)}, u32[]{:S(2)}, u32[]{:S(2)}) collective-permute-start(f32[8,96]{1,0:T(8,128)} %get-tuple-element.60), channel_id=1, source_target_pairs={{0,24},{8,0},{16,8},{24,16},{1,25},{9,1},{17,9},{25,17},{2,26},{10... | collective-permute-start | bytes 9224 | tf_op jit(solution)/shard_map/ppermute | solution.py:164
  7.5 11.1 %collective-permute-start.1 = (f32[8,96]{1,0:T(8,128)}, f32[8,96]{1,0:T(8,128)S(1)}, u32[]{:S(2)}, u32[]{:S(2)}) collective-permute-start(f32[8,96]{1,0:T(8,128)} %get-tuple-element.61), channel_id=1, source_target_pairs={{0,16},{8,24},{16,0},{24,8},{1,17},{9,25},{17,1},{25,9},{2,18},{10... | collective-permute-start | bytes 9224 | tf_op jit(solution)/shard_map/ppermute | solution.py:164
  7.5 11.1 %collective-permute-start.2 = (f32[8,96]{1,0:T(8,128)}, f32[8,96]{1,0:T(8,128)S(1)}, u32[]{:S(2)}, u32[]{:S(2)}) collective-permute-start(f32[8,96]{1,0:T(8,128)} %get-tuple-element.62), channel_id=1, source_target_pairs={{0,8},{8,16},{16,24},{24,0},{1,9},{9,17},{17,25},{25,1},{2,10},{10... | collective-permute-start | bytes 9224 | tf_op jit(solution)/shard_map/ppermute | solution.py:164
  18.5 0.7 %copy-start = (f32[8,96]{1,0:T(8,128)S(1)}, f32[8,96]{1,0:T(8,128)}, u32[]{:S(2)}) copy-start(f32[8,96]{1,0:T(8,128)} %get-tuple-element.63) | copy-start | bytes 9220
  19.3 10.4 %copy-start.1 = (f32[3]{0:T(128)S(1)}, f32[3]{0:T(128)}, u32[]{:S(2)}) copy-start(f32[3]{0:T(128)} %constant.83) | copy-start | bytes 40

commit v11 on v9

--- a/solution.py
+++ b/solution.py
@@ -29,23 +29,31 @@
     wake_place = wake_table[0:3]
     core_square = wake_table[3]
     tables = wake_table[4:10]
-    place_blocks = wake_place.reshape(3, wake_count // wake_width, wake_width).transpose(1, 0, 2)
+    wake_offset = (
+        wake_place[0] * wake_place[0]
+        + wake_place[1] * wake_place[1]
+        + wake_place[2] * wake_place[2]
+        + core_square
+    )
+    place_blocks = (-2.0 * wake_place).reshape(3, wake_count // wake_width, wake_width).transpose(1, 0, 2)
     table_blocks = tables.reshape(6, wake_count // wake_width, wake_width).transpose(1, 0, 2)
-    core_blocks = core_square.reshape(wake_count // wake_width, wake_width)
+    core_blocks = wake_offset.reshape(wake_count // wake_width, wake_width)
     point_blocks = points.reshape(3, point_count // point_count, point_count).transpose(1, 0, 2)
 
     def one_block(point_group):
+        point_sq = (
+            point_group[0] * point_group[0]
+            + point_group[1] * point_group[1]
+            + point_group[2] * point_group[2]
+        )
 
         def accumulate(running, parts):
-            place_part, table_part, core_part = parts
-            first_gap = point_group[0][:, None] - place_part[0][None, :]
-            second_gap = point_group[1][:, None] - place_part[1][None, :]
-            third_gap = point_group[2][:, None] - place_part[2][None, :]
+            scaled_place, table_part, offset_part = parts
             distance_sq = (
-                first_gap * first_gap
-                + second_gap * second_gap
-                + third_gap * third_gap
-                + core_part[None, :]
+                (point_sq[:, None] + offset_part[None, :])
+                + point_group[0][:, None] * scaled_place[0][None, :]
+                + point_group[1][:, None] * scaled_place[1][None, :]
+                + point_group[2][:, None] * scaled_place[2][None, :]
             )
             inverse_root = lax.rsqrt(distance_sq)
             kernel = inverse_root * inverse_root * inverse_root

time: 30.4 us -> 29.5 us (0.970)
  matrix products: 9.21 us -> 8.57 us
    dot_general x4, matrix products: 9.21 us -> 8.57 us  [accumulate(): lax.dot_general(table_part, kernel, (((1,), (1,)), ((), ())), precision=l...]
    add x0 -> x2, other arithmetic: none -> 0.41 us  [the longest x1 0.3 us: raw_terms(): wake_place[0] * wake_place[0] + wake_place[1] * wake_place[1]]
  transfers between devices with their start and end apart: 3 -> 3, of which waited for: 0 -> 0; matrix products, arithmetic and copies ran while one was open for 1% -> 2% of each run, Pallas kernels for 0% -> 0%
where the time goes in v11:
time: 29.5 us; the launch traced here: 29.2 us
  blocking collectives  9.51 us (32%)
  matrix products  8.57 us (29%)
  starting transfers between devices  6.06 us (21%)
  Pallas kernels  1.84 us (6%)
  other arithmetic  1.5 us (5%)
  between operations  0.84 us (3%)
  local copies, waits for them, and re-layouts  0.78 us (3%)
    all_gather x1, blocking collectives, body(): lax.all_gather(wake_table, 'narrow', axis=1, tiled=True)  9.51 us
    dot_general x4, matrix products, accumulate(): lax.dot_general(table_part, kernel, (((1,), (1,)), ((), ())), precision=l...  8.57 us
    ppermute x3, starting transfers between devices, exchange_slots(): by_shift.append(lax.ppermute(by_offset[shift], 'region', pairs))  6.06 us
    pallas_call x1, Pallas kernels, prologue(): pl.pallas_call(prologue_kernel, out_shape=tuple([jax.ShapeDtypeStruct((8,...  1.84 us
    mul x1, other arithmetic, advance(): jnp.concatenate([new_place, new_velocity], axis=0) * live_flag[None, :]  0.61 us
  transfers between devices with their start and end apart: 3, of which 0 were waited for; matrix products, arithmetic and copies ran while one was open for 2% of the time, Pallas kernels for 0%

profile of v11, /device:TPU:0, one launch (start us, length us, event | category | flops | bytes accessed | tf_op | source)
XLA Modules:
  0.0 29.2 jit_solution(9612902481672881304)
XLA Ops:
  0.7 1.8 %shard_map.91 = (f32[8,96]{1,0:T(8,128)}, f32[8,96]{1,0:T(8,128)}, f32[8,96]{1,0:T(8,128)}, f32[8,96]{1,0:T(8,128)}, f32[7,1024]{1,0:T(8,128)}) custom-call(s32[1]{0:T(128)S(6)} %copy.18.count_ref, f32[3,192]{1,0:T(4,128)} %pos_ref.1, f32[3,192]{1,0:T(4,128)} %vel_ref.1, f32[1,192]{1,0:T(1,128)} %bitcast.33, s32[1,192]{1,0:T(1,128)} %bitcast.34, ...), custom_call_target="tpu_custom_call" | custom-call | tf_op jit(solution)/shard_map/pallas_call | solution.py:144
  2.5 5.0 %collective-permute-start = (f32[8,96]{1,0:T(8,128)}, f32[8,96]{1,0:T(8,128)S(1)}, u32[]{:S(2)}, u32[]{:S(2)}) collective-permute-start(f32[8,96]{1,0:T(8,128)} %get-tuple-element.65), channel_id=1, source_target_pairs={{0,24},{8,0},{16,8},{24,16},{1,25},{9,1},{17,9},{25,17},{2,26},{10... | collective-permute-start | bytes 9224 | tf_op jit(solution)/shard_map/ppermute | solution.py:172
  7.5 0.0 collective-permute-start.1
  7.5 1.0 %collective-permute-start.2 = (f32[8,96]{1,0:T(8,128)}, f32[8,96]{1,0:T(8,128)S(1)}, u32[]{:S(2)}, u32[]{:S(2)}) collective-permute-start(f32[8,96]{1,0:T(8,128)} %get-tuple-element.67), channel_id=1, source_target_pairs={{0,8},{8,16},{16,24},{24,0},{1,9},{9,17},{17,25},{25,1},{2,10},{10... | collective-permute-start | bytes 9224 | tf_op jit(solution)/shard_map/ppermute | solution.py:172
  8.6 9.5 %all_gather.3 = f32[7,8192]{1,0:T(8,128)S(1)} all-gather(f32[7,1024]{1,0:T(8,128)} %get-tuple-element.69), channel_id=1, replica_groups=mesh['region'=4,'narrow'=8] {'narrow'}, dimensions={1}, use_global_device_ids=true | all-gather | bytes 258048 | tf_op jit(solution)/shard_map/all_gather | solution.py:195
  18.1 0.3 %fusion.21 = (f32[8192]{0:T(1024)S(1)}, f32[1,8192]{1,0:T(1,128)S(1)}, f32[1,8192]{1,0:T(1,128)S(1)}, f32[1,8192]{1,0:T(1,128)S(1)}) fusion(f32[7,8192]{1,0:T(8,128)S(1)} %all_gather.3), kind=kLoop, calls=%fused_computation.34 | loop fusion | flops 122880 | bytes 360448 | tf_op jit(solution)/shard_map/add | solution.py:33
  18.4 0.0 copy-start
  18.4 0.1 pad_maximum_fusion
  18.7 0.0 collective-permute-done
  18.7 0.0 collective-permute-done.1
  18.7 0.0 collective-permute-done.2
  18.7 0.4 %copy-done = f32[8,96]{1,0:T(8,128)S(1)} copy-done((f32[8,96]{1,0:T(8,128)S(1)}, f32[8,96]{1,0:T(8,128)}, u32[]{:S(2)}) %copy-start) | copy-done | bytes 3096
  19.1 0.1 fusion.26
  19.2 0.1 pad_maximum_fusion.3
  19.3 0.1 add_reduce_fusion.1
  19.4 0.0 copy-start.1
  19.4 9.0 %while.18 = (s32[]{:T(128)}, f32[6,384]{1,0:T(8,128)S(1)}, f32[4,6,2048]{2,1,0:T(8,128)S(1)}, f32[384]{0:T(512)S(1)}, f32[4,2048]{1,0:T(4,128)S(1)}, /*index=5*/...) while((s32[]{:T(128)}, f32[6,384]{1,0:T(8,128)S(1)}, ...), condition=%wide.region_1.2_spmd.clone, body=%wide.region_0.1_spmd.clone.sunk | while | flops 35394052 | bytes 202915 | solution.py:65
  19.5 2.1 %fusion.31 = f32[6,384]{1,0:T(8,128)S(1)} fusion(f32[2048]{0:T(1024)S(1)} %bitcast.30, f32[384]{0:T(512)S(1)} %get-tuple-element.190, f32[2048]{0:T(1024)S(1)} %bitcast.29, f32[384]{0:T(512)S(1)} %get-tuple-element.192, f32[2048]{0:T(1024)S(1)} %bitcast.28, f32[384]{0:T(512)S(1)} %get-tuple-element.194, f32[2048]{0:T(1024)S(1)} %bitcast.31, ...), kind=kOutput, calls=%fused_computation.18.clone.1 | convolution fusion | flops 35394048 | bytes 128005 | tf_op jit(solution)/shard_map/while/body/eval_jaxpr/while/body/eval_jaxpr/dot_general | solution.py:60
  21.7 0.1 constant_dynamic-slice_fusion.6
  21.8 2.1 %fusion.31 = f32[6,384]{1,0:T(8,128)S(1)} fusion(f32[2048]{0:T(1024)S(1)} %bitcast.30, f32[384]{0:T(512)S(1)} %get-tuple-element.190, f32[2048]{0:T(1024)S(1)} %bitcast.29, f32[384]{0:T(512)S(1)} %get-tuple-element.192, f32[2048]{0:T(1024)S(1)} %bitcast.28, f32[384]{0:T(512)S(1)} %get-tuple-element.194, f32[2048]{0:T(1024)S(1)} %bitcast.31, ...), kind=kOutput, calls=%fused_computation.18.clone.1 | convolution fusion | flops 35394048 | bytes 128005 | tf_op jit(solution)/shard_map/while/body/eval_jaxpr/while/body/eval_jaxpr/dot_general | solution.py:60
  23.9 0.1 constant_dynamic-slice_fusion.6
  24.1 2.1 %fusion.31 = f32[6,384]{1,0:T(8,128)S(1)} fusion(f32[2048]{0:T(1024)S(1)} %bitcast.30, f32[384]{0:T(512)S(1)} %get-tuple-element.190, f32[2048]{0:T(1024)S(1)} %bitcast.29, f32[384]{0:T(512)S(1)} %get-tuple-element.192, f32[2048]{0:T(1024)S(1)} %bitcast.28, f32[384]{0:T(512)S(1)} %get-tuple-element.194, f32[2048]{0:T(1024)S(1)} %bitcast.31, ...), kind=kOutput, calls=%fused_computation.18.clone.1 | convolution fusion | flops 35394048 | bytes 128005 | tf_op jit(solution)/shard_map/while/body/eval_jaxpr/while/body/eval_jaxpr/dot_general | solution.py:60
  26.2 0.1 constant_dynamic-slice_fusion.6
  26.3 2.1 %fusion.31 = f32[6,384]{1,0:T(8,128)S(1)} fusion(f32[2048]{0:T(1024)S(1)} %bitcast.30, f32[384]{0:T(512)S(1)} %get-tuple-element.190, f32[2048]{0:T(1024)S(1)} %bitcast.29, f32[384]{0:T(512)S(1)} %get-tuple-element.192, f32[2048]{0:T(1024)S(1)} %bitcast.28, f32[384]{0:T(512)S(1)} %get-tuple-element.194, f32[2048]{0:T(1024)S(1)} %bitcast.31, ...), kind=kOutput, calls=%fused_computation.18.clone.1 | convolution fusion | flops 35394048 | bytes 128005 | tf_op jit(solution)/shard_map/while/body/eval_jaxpr/while/body/eval_jaxpr/dot_general | solution.py:60
  28.5 0.1 multiply_reduce_fusion
  28.5 0.0 copy-done.1
  28.5 0.1 multiply_add_fusion
  28.6 0.6 %maximum_multiply_fusion = f32[6,384]{1,0:T(8,128)} fusion(f32[3,384]{1,0:T(4,128)S(1)} %get-tuple-element.117, f32[3,384]{1,0:T(4,128)S(1)} %get-tuple-element.116, f32[384]{0:T(512)S(1)} %get-tuple-element.114), kind=kLoop, calls=%fused_computation.39 | loop fusion | flops 4608 | bytes 19968 | tf_op jit(solution)/shard_map/mul | solution.py:88
  (14 shorter events, 0.3 us)
Async XLA Ops:
  2.5 16.2 %collective-permute-start = (f32[8,96]{1,0:T(8,128)}, f32[8,96]{1,0:T(8,128)S(1)}, u32[]{:S(2)}, u32[]{:S(2)}) collective-permute-start(f32[8,96]{1,0:T(8,128)} %get-tuple-element.65), channel_id=1, source_target_pairs={{0,24},{8,0},{16,8},{24,16},{1,25},{9,1},{17,9},{25,17},{2,26},{10... | collective-permute-start | bytes 9224 | tf_op jit(solution)/shard_map/ppermute | solution.py:172
  7.5 11.2 %collective-permute-start.1 = (f32[8,96]{1,0:T(8,128)}, f32[8,96]{1,0:T(8,128)S(1)}, u32[]{:S(2)}, u32[]{:S(2)}) collective-permute-start(f32[8,96]{1,0:T(8,128)} %get-tuple-element.66), channel_id=1, source_target_pairs={{0,16},{8,24},{16,0},{24,8},{1,17},{9,25},{17,1},{25,9},{2,18},{10... | collective-permute-start | bytes 9224 | tf_op jit(solution)/shard_map/ppermute | solution.py:172
  7.5 11.2 %collective-permute-start.2 = (f32[8,96]{1,0:T(8,128)}, f32[8,96]{1,0:T(8,128)S(1)}, u32[]{:S(2)}, u32[]{:S(2)}) collective-permute-start(f32[8,96]{1,0:T(8,128)} %get-tuple-element.67), channel_id=1, source_target_pairs={{0,8},{8,16},{16,24},{24,0},{1,9},{9,17},{17,25},{25,1},{2,10},{10... | collective-permute-start | bytes 9224 | tf_op jit(solution)/shard_map/ppermute | solution.py:172
  18.4 0.7 %copy-start = (f32[8,96]{1,0:T(8,128)S(1)}, f32[8,96]{1,0:T(8,128)}, u32[]{:S(2)}) copy-start(f32[8,96]{1,0:T(8,128)} %get-tuple-element.68) | copy-start | bytes 9220
  19.4 9.1 %copy-start.1 = (f32[3]{0:T(128)S(1)}, f32[3]{0:T(128)}, u32[]{:S(2)}) copy-start(f32[3]{0:T(128)} %constant.85) | copy-start | bytes 40

commit v12 on v11

--- a/solution.py
+++ b/solution.py
@@ -25,7 +25,7 @@
 def raw_terms(points, wake_table):
     point_count = points.shape[1]
     wake_count = wake_table.shape[1]
-    wake_width = math.gcd(wake_count, 2048)
+    wake_width = math.gcd(wake_count, 4096)
     wake_place = wake_table[0:3]
     core_square = wake_table[3]
     tables = wake_table[4:10]

time: 29.5 us -> 28.9 us (0.980)
  matrix products: 8.57 us -> 8.15 us
    dot_general x4 -> x2, matrix products: 8.57 us -> 8.15 us  [accumulate(): lax.dot_general(table_part, kernel, (((1,), (1,)), ((), ())), precision=l...]
where the time goes in v12:
time: 28.9 us; the launch traced here: 28.6 us
  blocking collectives  9.51 us (33%)
  matrix products  8.15 us (28%)
  starting transfers between devices  6.06 us (21%)
  Pallas kernels  1.84 us (6%)
  other arithmetic  1.51 us (5%)
  between operations  0.85 us (3%)
  local copies, waits for them, and re-layouts  0.65 us (2%)
    all_gather x1, blocking collectives, body(): lax.all_gather(wake_table, 'narrow', axis=1, tiled=True)  9.51 us
    dot_general x2, matrix products, accumulate(): lax.dot_general(table_part, kernel, (((1,), (1,)), ((), ())), precision=l...  8.15 us
    ppermute x3, starting transfers between devices, exchange_slots(): by_shift.append(lax.ppermute(by_offset[shift], 'region', pairs))  6.06 us
    pallas_call x1, Pallas kernels, prologue(): pl.pallas_call(prologue_kernel, out_shape=tuple([jax.ShapeDtypeStruct((8,...  1.84 us
    mul x1, other arithmetic, advance(): jnp.concatenate([new_place, new_velocity], axis=0) * live_flag[None, :]  0.61 us
  transfers between devices with their start and end apart: 3, of which 0 were waited for; matrix products, arithmetic and copies ran while one was open for 2% of the time, Pallas kernels for 0%

profile of v12, /device:TPU:0, one launch (start us, length us, event | category | flops | bytes accessed | tf_op | source)
XLA Modules:
  0.0 28.6 jit_solution(2236580943160821618)
XLA Ops:
  0.7 1.8 %shard_map.91 = (f32[8,96]{1,0:T(8,128)}, f32[8,96]{1,0:T(8,128)}, f32[8,96]{1,0:T(8,128)}, f32[8,96]{1,0:T(8,128)}, f32[7,1024]{1,0:T(8,128)}) custom-call(s32[1]{0:T(128)S(6)} %copy.18.count_ref, f32[3,192]{1,0:T(4,128)} %pos_ref.1, f32[3,192]{1,0:T(4,128)} %vel_ref.1, f32[1,192]{1,0:T(1,128)} %bitcast.33, s32[1,192]{1,0:T(1,128)} %bitcast.34, ...), custom_call_target="tpu_custom_call" | custom-call | tf_op jit(solution)/shard_map/pallas_call | solution.py:144
  2.5 5.0 %collective-permute-start = (f32[8,96]{1,0:T(8,128)}, f32[8,96]{1,0:T(8,128)S(1)}, u32[]{:S(2)}, u32[]{:S(2)}) collective-permute-start(f32[8,96]{1,0:T(8,128)} %get-tuple-element.65), channel_id=1, source_target_pairs={{0,24},{8,0},{16,8},{24,16},{1,25},{9,1},{17,9},{25,17},{2,26},{10... | collective-permute-start | bytes 9224 | tf_op jit(solution)/shard_map/ppermute | solution.py:172
  7.5 0.0 collective-permute-start.1
  7.5 1.0 %collective-permute-start.2 = (f32[8,96]{1,0:T(8,128)}, f32[8,96]{1,0:T(8,128)S(1)}, u32[]{:S(2)}, u32[]{:S(2)}) collective-permute-start(f32[8,96]{1,0:T(8,128)} %get-tuple-element.67), channel_id=1, source_target_pairs={{0,8},{8,16},{16,24},{24,0},{1,9},{9,17},{17,25},{25,1},{2,10},{10... | collective-permute-start | bytes 9224 | tf_op jit(solution)/shard_map/ppermute | solution.py:172
  8.6 9.5 %all_gather.3 = f32[7,8192]{1,0:T(8,128)S(1)} all-gather(f32[7,1024]{1,0:T(8,128)} %get-tuple-element.69), channel_id=1, replica_groups=mesh['region'=4,'narrow'=8] {'narrow'}, dimensions={1}, use_global_device_ids=true | all-gather | bytes 258048 | tf_op jit(solution)/shard_map/all_gather | solution.py:195
  18.1 0.3 %fusion.21 = (f32[8192]{0:T(1024)S(1)}, f32[1,8192]{1,0:T(1,128)S(1)}, f32[1,8192]{1,0:T(1,128)S(1)}, f32[1,8192]{1,0:T(1,128)S(1)}) fusion(f32[7,8192]{1,0:T(8,128)S(1)} %all_gather.3), kind=kLoop, calls=%fused_computation.34 | loop fusion | flops 122880 | bytes 360448 | tf_op jit(solution)/shard_map/add | solution.py:33
  18.4 0.0 copy-start
  18.4 0.1 pad_maximum_fusion
  18.7 0.0 collective-permute-done
  18.7 0.0 collective-permute-done.1
  18.7 0.0 collective-permute-done.2
  18.7 0.4 %copy-done = f32[8,96]{1,0:T(8,128)S(1)} copy-done((f32[8,96]{1,0:T(8,128)S(1)}, f32[8,96]{1,0:T(8,128)}, u32[]{:S(2)}) %copy-start) | copy-done | bytes 3096
  19.1 0.1 fusion.26
  19.2 0.1 pad_maximum_fusion.3
  19.3 0.1 add_reduce_fusion.1
  19.4 0.0 copy-start.1
  19.4 8.4 %while.18 = (s32[]{:T(128)}, f32[6,384]{1,0:T(8,128)S(1)}, f32[2,6,4096]{2,1,0:T(8,128)S(1)}, f32[384]{0:T(512)S(1)}, f32[2,4096]{1,0:T(2,128)S(1)}, /*index=5*/...) while((s32[]{:T(128)}, f32[6,384]{1,0:T(8,128)S(1)}, ...), condition=%wide.region_1.2_spmd.clone, body=%wide.region_0.1_spmd.clone.sunk | while | flops 70783488 | bytes 366755 | solution.py:65
  19.4 0.1 constant_dynamic-slice_fusion.6
  19.6 4.1 %fusion.31 = f32[6,384]{1,0:T(8,128)S(1)} fusion(f32[4096]{0:T(1024)S(1)} %bitcast.29, f32[384]{0:T(512)S(1)} %get-tuple-element.190, f32[4096]{0:T(1024)S(1)} %bitcast.28, f32[384]{0:T(512)S(1)} %get-tuple-element.192, f32[4096]{0:T(1024)S(1)} %bitcast.27, f32[384]{0:T(512)S(1)} %get-tuple-element.194, f32[4096]{0:T(1024)S(1)} %bitcast.30, ...), kind=kOutput, calls=%fused_computation.18.clone.1 | convolution fusion | flops 70783488 | bytes 226309 | tf_op jit(solution)/shard_map/while/body/eval_jaxpr/while/body/eval_jaxpr/dot_general | solution.py:60
  23.6 0.1 constant_dynamic-slice_fusion.6
  23.8 4.1 %fusion.31 = f32[6,384]{1,0:T(8,128)S(1)} fusion(f32[4096]{0:T(1024)S(1)} %bitcast.29, f32[384]{0:T(512)S(1)} %get-tuple-element.190, f32[4096]{0:T(1024)S(1)} %bitcast.28, f32[384]{0:T(512)S(1)} %get-tuple-element.192, f32[4096]{0:T(1024)S(1)} %bitcast.27, f32[384]{0:T(512)S(1)} %get-tuple-element.194, f32[4096]{0:T(1024)S(1)} %bitcast.30, ...), kind=kOutput, calls=%fused_computation.18.clone.1 | convolution fusion | flops 70783488 | bytes 226309 | tf_op jit(solution)/shard_map/while/body/eval_jaxpr/while/body/eval_jaxpr/dot_general | solution.py:60
  27.9 0.1 multiply_reduce_fusion
  27.9 0.0 copy-done.1
  27.9 0.1 multiply_add_fusion
  28.0 0.6 %maximum_multiply_fusion = f32[6,384]{1,0:T(8,128)} fusion(f32[3,384]{1,0:T(4,128)S(1)} %get-tuple-element.117, f32[3,384]{1,0:T(4,128)S(1)} %get-tuple-element.116, f32[384]{0:T(512)S(1)} %get-tuple-element.114), kind=kLoop, calls=%fused_computation.39 | loop fusion | flops 4608 | bytes 19968 | tf_op jit(solution)/shard_map/mul | solution.py:88
  (9 shorter events, 0.2 us)
Async XLA Ops:
  2.5 16.2 %collective-permute-start = (f32[8,96]{1,0:T(8,128)}, f32[8,96]{1,0:T(8,128)S(1)}, u32[]{:S(2)}, u32[]{:S(2)}) collective-permute-start(f32[8,96]{1,0:T(8,128)} %get-tuple-element.65), channel_id=1, source_target_pairs={{0,24},{8,0},{16,8},{24,16},{1,25},{9,1},{17,9},{25,17},{2,26},{10... | collective-permute-start | bytes 9224 | tf_op jit(solution)/shard_map/ppermute | solution.py:172
  7.5 11.2 %collective-permute-start.1 = (f32[8,96]{1,0:T(8,128)}, f32[8,96]{1,0:T(8,128)S(1)}, u32[]{:S(2)}, u32[]{:S(2)}) collective-permute-start(f32[8,96]{1,0:T(8,128)} %get-tuple-element.66), channel_id=1, source_target_pairs={{0,16},{8,24},{16,0},{24,8},{1,17},{9,25},{17,1},{25,9},{2,18},{10... | collective-permute-start | bytes 9224 | tf_op jit(solution)/shard_map/ppermute | solution.py:172
  7.5 11.2 %collective-permute-start.2 = (f32[8,96]{1,0:T(8,128)}, f32[8,96]{1,0:T(8,128)S(1)}, u32[]{:S(2)}, u32[]{:S(2)}) collective-permute-start(f32[8,96]{1,0:T(8,128)} %get-tuple-element.67), channel_id=1, source_target_pairs={{0,8},{8,16},{16,24},{24,0},{1,9},{9,17},{17,25},{25,1},{2,10},{10... | collective-permute-start | bytes 9224 | tf_op jit(solution)/shard_map/ppermute | solution.py:172
  18.4 0.7 %copy-start = (f32[8,96]{1,0:T(8,128)S(1)}, f32[8,96]{1,0:T(8,128)}, u32[]{:S(2)}) copy-start(f32[8,96]{1,0:T(8,128)} %get-tuple-element.68) | copy-start | bytes 9220
  19.4 8.5 %copy-start.1 = (f32[3]{0:T(128)S(1)}, f32[3]{0:T(128)}, u32[]{:S(2)}) copy-start(f32[3]{0:T(128)} %constant.85) | copy-start | bytes 40

commit v13 on v12

--- a/solution.py
+++ b/solution.py
@@ -25,7 +25,7 @@
 def raw_terms(points, wake_table):
     point_count = points.shape[1]
     wake_count = wake_table.shape[1]
-    wake_width = math.gcd(wake_count, 4096)
+    wake_width = math.gcd(wake_count, 8192)
     wake_place = wake_table[0:3]
     core_square = wake_table[3]
     tables = wake_table[4:10]

time: 28.9 us -> 28.5 us (0.986)
  local copies, waits for them, and re-layouts: 0.65 us -> 0.32 us
    add x1 -> x0, other arithmetic: 0.3 us -> none  [raw_terms(): wake_place[0] * wake_place[0] + wake_place[1] * wake_place[1]]
    dot_general x2 -> x1, matrix products: 8.15 us -> 8.32 us  [accumulate(): lax.dot_general(table_part, kernel, (((1,), (1,)), ((), ())), precision=l...]
  transfers between devices with their start and end apart: 3 -> 3, of which waited for: 0 -> 0; matrix products, arithmetic and copies ran while one was open for 2% -> 1% of each run, Pallas kernels for 0% -> 0%
where the time goes in v13:
time: 28.5 us; the launch traced here: 28.2 us
  blocking collectives  9.51 us (33%)
  matrix products  8.32 us (29%)
  starting transfers between devices  6.06 us (21%)
  Pallas kernels  1.84 us (6%)
  other arithmetic  1.29 us (5%)
  between operations  0.83 us (3%)
  local copies, waits for them, and re-layouts  0.32 us (1%)
    all_gather x1, blocking collectives, body(): lax.all_gather(wake_table, 'narrow', axis=1, tiled=True)  9.51 us
    dot_general x1, matrix products, accumulate(): lax.dot_general(table_part, kernel, (((1,), (1,)), ((), ())), precision=l...  8.32 us
    ppermute x3, starting transfers between devices, exchange_slots(): by_shift.append(lax.ppermute(by_offset[shift], 'region', pairs))  6.06 us
    pallas_call x1, Pallas kernels, prologue(): pl.pallas_call(prologue_kernel, out_shape=tuple([jax.ShapeDtypeStruct((8,...  1.84 us
    mul x1, other arithmetic, advance(): jnp.concatenate([new_place, new_velocity], axis=0) * live_flag[None, :]  0.61 us
  transfers between devices with their start and end apart: 3, of which 0 were waited for; matrix products, arithmetic and copies ran while one was open for 1% of the time, Pallas kernels for 0%

profile of v13, /device:TPU:0, one launch (start us, length us, event | category | flops | bytes accessed | tf_op | source)
XLA Modules:
  0.0 28.2 jit_solution(16688702133700979884)
XLA Ops:
  0.7 1.8 %shard_map.91 = (f32[8,96]{1,0:T(8,128)}, f32[8,96]{1,0:T(8,128)}, f32[8,96]{1,0:T(8,128)}, f32[8,96]{1,0:T(8,128)}, f32[7,1024]{1,0:T(8,128)}) custom-call(s32[1]{0:T(128)S(6)} %copy.10.count_ref, f32[3,192]{1,0:T(4,128)} %pos_ref.1, f32[3,192]{1,0:T(4,128)} %vel_ref.1, f32[1,192]{1,0:T(1,128)} %bitcast.12, s32[1,192]{1,0:T(1,128)} %bitcast.13, ...), custom_call_target="tpu_custom_call" | custom-call | tf_op jit(solution)/shard_map/pallas_call | solution.py:144
  2.5 5.0 %collective-permute-start = (f32[8,96]{1,0:T(8,128)}, f32[8,96]{1,0:T(8,128)S(1)}, u32[]{:S(2)}, u32[]{:S(2)}) collective-permute-start(f32[8,96]{1,0:T(8,128)} %get-tuple-element.56), channel_id=1, source_target_pairs={{0,24},{8,0},{16,8},{24,16},{1,25},{9,1},{17,9},{25,17},{2,26},{10... | collective-permute-start | bytes 9224 | tf_op jit(solution)/shard_map/ppermute | solution.py:172
  7.5 0.0 collective-permute-start.1
  7.5 1.0 %collective-permute-start.2 = (f32[8,96]{1,0:T(8,128)}, f32[8,96]{1,0:T(8,128)S(1)}, u32[]{:S(2)}, u32[]{:S(2)}) collective-permute-start(f32[8,96]{1,0:T(8,128)} %get-tuple-element.58), channel_id=1, source_target_pairs={{0,8},{8,16},{16,24},{24,0},{1,9},{9,17},{17,25},{25,1},{2,10},{10... | collective-permute-start | bytes 9224 | tf_op jit(solution)/shard_map/ppermute | solution.py:172
  8.6 9.5 %all_gather.3 = f32[7,8192]{1,0:T(8,128)S(1)} all-gather(f32[7,1024]{1,0:T(8,128)} %get-tuple-element.60), channel_id=1, replica_groups=mesh['region'=4,'narrow'=8] {'narrow'}, dimensions={1}, use_global_device_ids=true | all-gather | bytes 258048 | tf_op jit(solution)/shard_map/all_gather | solution.py:195
  18.1 0.0 copy-start
  18.1 0.2 multiply_subtract_fusion.2
  18.4 0.1 fusion.29
  18.5 0.0 collective-permute-done
  18.5 0.0 collective-permute-done.1
  18.5 0.0 collective-permute-done.2
  18.5 0.2 copy-done
  18.8 0.1 fusion.24
  18.9 0.1 pad_maximum_fusion.6
  19.0 0.1 fusion.26
  19.1 0.0 copy-start.1
  19.1 8.3 %fusion = f32[6,384]{1,0:T(8,128)S(1)} fusion(f32[8192]{0:T(1024)S(1)} %bitcast.8, f32[384]{0:T(512)S(1)} %get-tuple-element.81, f32[8192]{0:T(1024)S(1)} %bitcast.9, f32[384]{0:T(512)S(1)} %get-tuple-element.83, f32[8192]{0:T(1024)S(1)} %bitcast.7, f32[384]{0:T(512)S(1)} %get-tuple-element.67, f32[8192]{0:T(1024)S(1)} %bitcast.10, ...), kind=kOutput, calls=%fused_computation.1 | convolution fusion | flops 141705216 | bytes 474112 | tf_op jit(solution)/shard_map/while/body/eval_jaxpr/while/body/eval_jaxpr/dot_general | solution.py:60
  27.5 0.0 copy-done.1
  27.5 0.1 slice_add_fusion.1
  27.6 0.6 %maximum_multiply_fusion = f32[6,384]{1,0:T(8,128)} fusion(f32[3,384]{1,0:T(4,128)S(1)} %get-tuple-element.66, f32[3,384]{1,0:T(4,128)S(1)} %get-tuple-element.65, f32[384]{0:T(512)S(1)} %get-tuple-element.63), kind=kLoop, calls=%fused_computation.28 | loop fusion | flops 4608 | bytes 19968 | tf_op jit(solution)/shard_map/mul | solution.py:88
  (5 shorter events, 0.1 us)
Async XLA Ops:
  2.5 16.0 %collective-permute-start = (f32[8,96]{1,0:T(8,128)}, f32[8,96]{1,0:T(8,128)S(1)}, u32[]{:S(2)}, u32[]{:S(2)}) collective-permute-start(f32[8,96]{1,0:T(8,128)} %get-tuple-element.56), channel_id=1, source_target_pairs={{0,24},{8,0},{16,8},{24,16},{1,25},{9,1},{17,9},{25,17},{2,26},{10... | collective-permute-start | bytes 9224 | tf_op jit(solution)/shard_map/ppermute | solution.py:172
  7.5 11.0 %collective-permute-start.1 = (f32[8,96]{1,0:T(8,128)}, f32[8,96]{1,0:T(8,128)S(1)}, u32[]{:S(2)}, u32[]{:S(2)}) collective-permute-start(f32[8,96]{1,0:T(8,128)} %get-tuple-element.57), channel_id=1, source_target_pairs={{0,16},{8,24},{16,0},{24,8},{1,17},{9,25},{17,1},{25,9},{2,18},{10... | collective-permute-start | bytes 9224 | tf_op jit(solution)/shard_map/ppermute | solution.py:172
  7.5 11.0 %collective-permute-start.2 = (f32[8,96]{1,0:T(8,128)}, f32[8,96]{1,0:T(8,128)S(1)}, u32[]{:S(2)}, u32[]{:S(2)}) collective-permute-start(f32[8,96]{1,0:T(8,128)} %get-tuple-element.58), channel_id=1, source_target_pairs={{0,8},{8,16},{16,24},{24,0},{1,9},{9,17},{17,25},{25,1},{2,10},{10... | collective-permute-start | bytes 9224 | tf_op jit(solution)/shard_map/ppermute | solution.py:172
  18.1 0.7 %copy-start = (f32[8,96]{1,0:T(8,128)S(1)}, f32[8,96]{1,0:T(8,128)}, u32[]{:S(2)}) copy-start(f32[8,96]{1,0:T(8,128)} %get-tuple-element.59) | copy-start | bytes 9220
  19.1 8.4 %copy-start.1 = (f32[3]{0:T(128)S(1)}, f32[3]{0:T(128)}, u32[]{:S(2)}) copy-start(f32[3]{0:T(128)} %constant.85) | copy-start | bytes 40

commit v14 on v13

--- a/solution.py
+++ b/solution.py
@@ -38,7 +38,8 @@
     place_blocks = (-2.0 * wake_place).reshape(3, wake_count // wake_width, wake_width).transpose(1, 0, 2)
     table_blocks = tables.reshape(6, wake_count // wake_width, wake_width).transpose(1, 0, 2)
     core_blocks = wake_offset.reshape(wake_count // wake_width, wake_width)
-    point_blocks = points.reshape(3, point_count // point_count, point_count).transpose(1, 0, 2)
+    point_width = point_count // 2 if point_count % 256 == 128 else point_count
+    point_blocks = points.reshape(3, point_count // point_width, point_width).transpose(1, 0, 2)
 
     def one_block(point_group):
         point_sq = (
@@ -64,7 +65,7 @@
 
         total, _ = lax.scan(
             accumulate,
-            jnp.zeros((6, point_count), jnp.float32),
+            jnp.zeros((6, point_width), jnp.float32),
             (place_blocks, table_blocks, core_blocks),
         )
         return total

time: 28.5 us -> 29.9 us (1.049)
  local copies, waits for them, and re-layouts: 0.32 us -> 1.09 us
  matrix products: 8.32 us -> 8.72 us
    dot_general x1 -> x2, matrix products: 8.32 us -> 8.72 us  [accumulate(): lax.dot_general(table_part, kernel, (((1,), (1,)), ((), ())), precision=l...]
where the time goes in v14:
time: 29.9 us; the launch traced here: 29.6 us
  blocking collectives  9.51 us (32%)
  matrix products  8.72 us (29%)
  starting transfers between devices  6.06 us (20%)
  Pallas kernels  1.84 us (6%)
  other arithmetic  1.47 us (5%)
  local copies, waits for them, and re-layouts  1.09 us (4%)
  between operations  0.83 us (3%)
    all_gather x1, blocking collectives, body(): lax.all_gather(wake_table, 'narrow', axis=1, tiled=True)  9.51 us
    dot_general x2, matrix products, accumulate(): lax.dot_general(table_part, kernel, (((1,), (1,)), ((), ())), precision=l...  8.72 us
    ppermute x3, starting transfers between devices, exchange_slots(): by_shift.append(lax.ppermute(by_offset[shift], 'region', pairs))  6.06 us
    pallas_call x1, Pallas kernels, prologue(): pl.pallas_call(prologue_kernel, out_shape=tuple([jax.ShapeDtypeStruct((8,...  1.84 us
    mul x1, other arithmetic, advance(): jnp.concatenate([new_place, new_velocity], axis=0) * live_flag[None, :]  0.61 us
  transfers between devices with their start and end apart: 3, of which 0 were waited for; matrix products, arithmetic and copies ran while one was open for 1% of the time, Pallas kernels for 0%

profile of v14, /device:TPU:0, one launch (start us, length us, event | category | flops | bytes accessed | tf_op | source)
XLA Modules:
  0.0 29.6 jit_solution(9993150786936539644)
XLA Ops:
  0.7 1.8 %shard_map.91 = (f32[8,96]{1,0:T(8,128)}, f32[8,96]{1,0:T(8,128)}, f32[8,96]{1,0:T(8,128)}, f32[8,96]{1,0:T(8,128)}, f32[7,1024]{1,0:T(8,128)}) custom-call(s32[1]{0:T(128)S(6)} %copy.21.count_ref, f32[3,192]{1,0:T(4,128)} %pos_ref.1, f32[3,192]{1,0:T(4,128)} %vel_ref.1, f32[1,192]{1,0:T(1,128)} %bitcast.59, s32[1,192]{1,0:T(1,128)} %bitcast.60, ...), custom_call_target="tpu_custom_call" | custom-call | tf_op jit(solution)/shard_map/pallas_call | solution.py:145
  2.5 5.0 %collective-permute-start = (f32[8,96]{1,0:T(8,128)}, f32[8,96]{1,0:T(8,128)S(1)}, u32[]{:S(2)}, u32[]{:S(2)}) collective-permute-start(f32[8,96]{1,0:T(8,128)} %get-tuple-element.63), channel_id=1, source_target_pairs={{0,24},{8,0},{16,8},{24,16},{1,25},{9,1},{17,9},{25,17},{2,26},{10... | collective-permute-start | bytes 9224 | tf_op jit(solution)/shard_map/ppermute | solution.py:173
  7.5 0.0 collective-permute-start.1
  7.5 1.0 %collective-permute-start.2 = (f32[8,96]{1,0:T(8,128)}, f32[8,96]{1,0:T(8,128)S(1)}, u32[]{:S(2)}, u32[]{:S(2)}) collective-permute-start(f32[8,96]{1,0:T(8,128)} %get-tuple-element.65), channel_id=1, source_target_pairs={{0,8},{8,16},{16,24},{24,0},{1,9},{9,17},{17,25},{25,1},{2,10},{10... | collective-permute-start | bytes 9224 | tf_op jit(solution)/shard_map/ppermute | solution.py:173
  8.6 9.5 %all_gather.3 = f32[7,8192]{1,0:T(8,128)S(1)} all-gather(f32[7,1024]{1,0:T(8,128)} %get-tuple-element.67), channel_id=1, replica_groups=mesh['region'=4,'narrow'=8] {'narrow'}, dimensions={1}, use_global_device_ids=true | all-gather | bytes 258048 | tf_op jit(solution)/shard_map/all_gather | solution.py:196
  18.1 0.2 multiply_subtract_fusion.2
  18.4 0.0 copy-start
  18.4 0.1 fusion.20
  18.6 0.0 collective-permute-done
  18.6 0.0 collective-permute-done.1
  18.6 0.0 collective-permute-done.2
  18.6 0.4 %copy-done = f32[8,96]{1,0:T(8,128)S(1)} copy-done((f32[8,96]{1,0:T(8,128)S(1)}, f32[8,96]{1,0:T(8,128)}, u32[]{:S(2)}) %copy-start) | copy-done | bytes 3096
  19.1 0.1 pad_maximum_fusion.3
  19.1 0.1 reshape.71
  19.2 0.0 copy-start.1
  19.2 9.0 %while.10 = (s32[]{:T(128)}, f32[2,6,192]{2,1,0:T(8,128)S(1)}, f32[2,3,192]{2,1,0:T(4,128)S(1)}, f32[1,8192]{1,0:T(1,128)S(1)}, f32[1,3,8192]{2,1,0:T(4,128)S(1)...) while((s32[]{:T(128)}, f32[2,6,192]{2,1,0:T(8,128)S(1)}, ...), condition=%wide.region_1.2_spmd, body=%wide.region_0.1_spmd.sunk | while | flops 70779840 | bytes 609933 | solution.py:73
  19.3 0.1 fusion.33
  19.3 4.4 %fusion.34 = f32[2,6,192]{2,1,0:T(8,128)S(1)} fusion(f32[2,6,192]{2,1,0:T(8,128)S(1)} %get-tuple-element.172, s32[]{:T(128)} %get-tuple-element.171, f32[8192]{0:T(1024)S(1)} %bitcast.46, f32[192]{0:T(256)S(1)} %bitcast.53, f32[8192]{0:T(1024)S(1)} %bitcast.47, f32[192]{0:T(256)S(1)} %bitcast.51, f32[8192]{0:T(1024)S(1)} %bitcast.45, ...), kind=kOutput, calls=%fused_computation.19.clone.1 | convolution fusion | flops 70778880 | bytes 405508 | tf_op jit(solution)/shard_map/while/body/eval_jaxpr/while/body/eval_jaxpr/dot_general | solution.py:61
  23.8 0.1 fusion.33
  23.8 4.4 %fusion.34 = f32[2,6,192]{2,1,0:T(8,128)S(1)} fusion(f32[2,6,192]{2,1,0:T(8,128)S(1)} %get-tuple-element.172, s32[]{:T(128)} %get-tuple-element.171, f32[8192]{0:T(1024)S(1)} %bitcast.46, f32[192]{0:T(256)S(1)} %bitcast.53, f32[8192]{0:T(1024)S(1)} %bitcast.47, f32[192]{0:T(256)S(1)} %bitcast.51, f32[8192]{0:T(1024)S(1)} %bitcast.45, ...), kind=kOutput, calls=%fused_computation.19.clone.1 | convolution fusion | flops 70778880 | bytes 405508 | tf_op jit(solution)/shard_map/while/body/eval_jaxpr/while/body/eval_jaxpr/dot_general | solution.py:61
  28.2 0.1 slice_reduce_fusion.1
  28.3 0.1 squeeze.24
  28.3 0.1 squeeze.25
  28.4 0.1 squeeze.26
  28.5 0.1 slice.155
  28.6 0.1 multiply_subtract_fusion.5
  28.7 0.1 multiply_subtract_fusion.4
  28.8 0.1 multiply_reduce_fusion
  28.9 0.0 copy-done.1
  28.9 0.1 multiply_add_fusion.1
  29.0 0.6 %maximum_multiply_fusion = f32[6,384]{1,0:T(8,128)} fusion(f32[3,384]{1,0:T(4,128)S(1)} %get-tuple-element.89, f32[3,384]{1,0:T(4,128)S(1)} %get-tuple-element.88, f32[384]{0:T(512)S(1)} %get-tuple-element.105), kind=kLoop, calls=%fused_computation.36 | loop fusion | flops 4608 | bytes 19968 | tf_op jit(solution)/shard_map/mul | solution.py:89
  (11 shorter events, 0.1 us)
Async XLA Ops:
  2.5 16.1 %collective-permute-start = (f32[8,96]{1,0:T(8,128)}, f32[8,96]{1,0:T(8,128)S(1)}, u32[]{:S(2)}, u32[]{:S(2)}) collective-permute-start(f32[8,96]{1,0:T(8,128)} %get-tuple-element.63), channel_id=1, source_target_pairs={{0,24},{8,0},{16,8},{24,16},{1,25},{9,1},{17,9},{25,17},{2,26},{10... | collective-permute-start | bytes 9224 | tf_op jit(solution)/shard_map/ppermute | solution.py:173
  7.5 11.1 %collective-permute-start.1 = (f32[8,96]{1,0:T(8,128)}, f32[8,96]{1,0:T(8,128)S(1)}, u32[]{:S(2)}, u32[]{:S(2)}) collective-permute-start(f32[8,96]{1,0:T(8,128)} %get-tuple-element.64), channel_id=1, source_target_pairs={{0,16},{8,24},{16,0},{24,8},{1,17},{9,25},{17,1},{25,9},{2,18},{10... | collective-permute-start | bytes 9224 | tf_op jit(solution)/shard_map/ppermute | solution.py:173
  7.5 11.1 %collective-permute-start.2 = (f32[8,96]{1,0:T(8,128)}, f32[8,96]{1,0:T(8,128)S(1)}, u32[]{:S(2)}, u32[]{:S(2)}) collective-permute-start(f32[8,96]{1,0:T(8,128)} %get-tuple-element.65), channel_id=1, source_target_pairs={{0,8},{8,16},{16,24},{24,0},{1,9},{9,17},{17,25},{25,1},{2,10},{10... | collective-permute-start | bytes 9224 | tf_op jit(solution)/shard_map/ppermute | solution.py:173
  18.4 0.7 %copy-start = (f32[8,96]{1,0:T(8,128)S(1)}, f32[8,96]{1,0:T(8,128)}, u32[]{:S(2)}) copy-start(f32[8,96]{1,0:T(8,128)} %get-tuple-element.66) | copy-start | bytes 9220
  19.2 9.7 %copy-start.1 = (f32[3]{0:T(128)S(1)}, f32[3]{0:T(128)}, u32[]{:S(2)}) copy-start(f32[3]{0:T(128)} %constant.84) | copy-start | bytes 40

commit v15 on v13

--- a/solution.py
+++ b/solution.py
@@ -50,15 +50,15 @@
         def accumulate(running, parts):
             scaled_place, table_part, offset_part = parts
             distance_sq = (
-                (point_sq[:, None] + offset_part[None, :])
-                + point_group[0][:, None] * scaled_place[0][None, :]
-                + point_group[1][:, None] * scaled_place[1][None, :]
-                + point_group[2][:, None] * scaled_place[2][None, :]
+                (offset_part[:, None] + point_sq[None, :])
+                + scaled_place[0][:, None] * point_group[0][None, :]
+                + scaled_place[1][:, None] * point_group[1][None, :]
+                + scaled_place[2][:, None] * point_group[2][None, :]
             )
             inverse_root = lax.rsqrt(distance_sq)
             kernel = inverse_root * inverse_root * inverse_root
             product = lax.dot_general(
-                table_part, kernel, (((1,), (1,)), ((), ())), precision=lax.Precision.HIGH
+                table_part, kernel, (((1,), (0,)), ((), ())), precision=lax.Precision.HIGH
             )
             return (running + product, None)
 

time: 28.5 us -> 27.4 us (0.961)
  matrix products: 8.32 us -> 7.25 us
    dot_general x1, matrix products: 8.32 us -> 7.25 us  [accumulate(): lax.dot_general(table_part, kernel, (((1,), (0,)), ((), ())), precision=l...]
where the time goes in v15:
time: 27.4 us; the launch traced here: 27.1 us
  blocking collectives  9.51 us (35%)
  matrix products  7.25 us (26%)
  starting transfers between devices  6.06 us (22%)
  Pallas kernels  1.84 us (7%)
  other arithmetic  1.28 us (5%)
  between operations  0.82 us (3%)
  local copies, waits for them, and re-layouts  0.32 us (1%)
    all_gather x1, blocking collectives, body(): lax.all_gather(wake_table, 'narrow', axis=1, tiled=True)  9.51 us
    dot_general x1, matrix products, accumulate(): lax.dot_general(table_part, kernel, (((1,), (0,)), ((), ())), precision=l...  7.25 us
    ppermute x3, starting transfers between devices, exchange_slots(): by_shift.append(lax.ppermute(by_offset[shift], 'region', pairs))  6.06 us
    pallas_call x1, Pallas kernels, prologue(): pl.pallas_call(prologue_kernel, out_shape=tuple([jax.ShapeDtypeStruct((8,...  1.84 us
    mul x1, other arithmetic, advance(): jnp.concatenate([new_place, new_velocity], axis=0) * live_flag[None, :]  0.61 us
  transfers between devices with their start and end apart: 3, of which 0 were waited for; matrix products, arithmetic and copies ran while one was open for 1% of the time, Pallas kernels for 0%

profile of v15, /device:TPU:0, one launch (start us, length us, event | category | flops | bytes accessed | tf_op | source)
XLA Modules:
  0.0 27.1 jit_solution(17026913809660965925)
XLA Ops:
  0.7 1.8 %shard_map.91 = (f32[8,96]{1,0:T(8,128)}, f32[8,96]{1,0:T(8,128)}, f32[8,96]{1,0:T(8,128)}, f32[8,96]{1,0:T(8,128)}, f32[7,1024]{1,0:T(8,128)}) custom-call(s32[1]{0:T(128)S(6)} %copy.10.count_ref, f32[3,192]{1,0:T(4,128)} %pos_ref.1, f32[3,192]{1,0:T(4,128)} %vel_ref.1, f32[1,192]{1,0:T(1,128)} %bitcast.12, s32[1,192]{1,0:T(1,128)} %bitcast.13, ...), custom_call_target="tpu_custom_call" | custom-call | tf_op jit(solution)/shard_map/pallas_call | solution.py:144
  2.5 5.0 %collective-permute-start = (f32[8,96]{1,0:T(8,128)}, f32[8,96]{1,0:T(8,128)S(1)}, u32[]{:S(2)}, u32[]{:S(2)}) collective-permute-start(f32[8,96]{1,0:T(8,128)} %get-tuple-element.56), channel_id=1, source_target_pairs={{0,24},{8,0},{16,8},{24,16},{1,25},{9,1},{17,9},{25,17},{2,26},{10... | collective-permute-start | bytes 9224 | tf_op jit(solution)/shard_map/ppermute | solution.py:172
  7.5 0.0 collective-permute-start.1
  7.5 1.0 %collective-permute-start.2 = (f32[8,96]{1,0:T(8,128)}, f32[8,96]{1,0:T(8,128)S(1)}, u32[]{:S(2)}, u32[]{:S(2)}) collective-permute-start(f32[8,96]{1,0:T(8,128)} %get-tuple-element.58), channel_id=1, source_target_pairs={{0,8},{8,16},{16,24},{24,0},{1,9},{9,17},{17,25},{25,1},{2,10},{10... | collective-permute-start | bytes 9224 | tf_op jit(solution)/shard_map/ppermute | solution.py:172
  8.6 9.5 %all_gather.3 = f32[7,8192]{1,0:T(8,128)S(1)} all-gather(f32[7,1024]{1,0:T(8,128)} %get-tuple-element.60), channel_id=1, replica_groups=mesh['region'=4,'narrow'=8] {'narrow'}, dimensions={1}, use_global_device_ids=true | all-gather | bytes 258048 | tf_op jit(solution)/shard_map/all_gather | solution.py:195
  18.1 0.0 copy-start
  18.1 0.2 multiply_subtract_fusion.2
  18.4 0.1 fusion.26
  18.5 0.0 collective-permute-done
  18.5 0.0 collective-permute-done.1
  18.5 0.0 collective-permute-done.2
  18.5 0.2 copy-done
  18.8 0.1 pad_maximum_fusion.6
  18.9 0.1 add_reduce_fusion.1
  19.0 0.1 multiply_reduce_fusion
  19.1 0.0 copy-start.1
  19.1 7.3 %fusion = f32[6,384]{1,0:T(8,128)S(1)} fusion(f32[384]{0:T(512)S(1)} %get-tuple-element.66, f32[8192]{0:T(1024)S(1)} %bitcast.8, f32[384]{0:T(512)S(1)} %get-tuple-element.65, f32[8192]{0:T(1024)S(1)} %bitcast.9, f32[384]{0:T(512)S(1)} %get-tuple-element.64, f32[8192]{0:T(1024)S(1)} %bitcast.7, f32[384]{0:T(512)S(1)} %get-tuple-element.63, ...), kind=kOutput, calls=%fused_computation.1 | convolution fusion | flops 141705216 | bytes 474112 | tf_op jit(solution)/shard_map/while/body/eval_jaxpr/while/body/eval_jaxpr/dot_general | solution.py:60
  26.4 0.0 copy-done.1
  26.4 0.1 slice_add_fusion.1
  26.5 0.6 %maximum_multiply_fusion = f32[6,384]{1,0:T(8,128)} fusion(f32[3,384]{1,0:T(4,128)S(1)} %get-tuple-element.70, f32[3,384]{1,0:T(4,128)S(1)} %get-tuple-element.69, f32[384]{0:T(512)S(1)} %get-tuple-element.81), kind=kLoop, calls=%fused_computation.28 | loop fusion | flops 4608 | bytes 19968 | tf_op jit(solution)/shard_map/mul | solution.py:88
  (3 shorter events, 0.1 us)
Async XLA Ops:
  2.5 16.0 %collective-permute-start = (f32[8,96]{1,0:T(8,128)}, f32[8,96]{1,0:T(8,128)S(1)}, u32[]{:S(2)}, u32[]{:S(2)}) collective-permute-start(f32[8,96]{1,0:T(8,128)} %get-tuple-element.56), channel_id=1, source_target_pairs={{0,24},{8,0},{16,8},{24,16},{1,25},{9,1},{17,9},{25,17},{2,26},{10... | collective-permute-start | bytes 9224 | tf_op jit(solution)/shard_map/ppermute | solution.py:172
  7.5 11.0 %collective-permute-start.1 = (f32[8,96]{1,0:T(8,128)}, f32[8,96]{1,0:T(8,128)S(1)}, u32[]{:S(2)}, u32[]{:S(2)}) collective-permute-start(f32[8,96]{1,0:T(8,128)} %get-tuple-element.57), channel_id=1, source_target_pairs={{0,16},{8,24},{16,0},{24,8},{1,17},{9,25},{17,1},{25,9},{2,18},{10... | collective-permute-start | bytes 9224 | tf_op jit(solution)/shard_map/ppermute | solution.py:172
  7.5 11.0 %collective-permute-start.2 = (f32[8,96]{1,0:T(8,128)}, f32[8,96]{1,0:T(8,128)S(1)}, u32[]{:S(2)}, u32[]{:S(2)}) collective-permute-start(f32[8,96]{1,0:T(8,128)} %get-tuple-element.58), channel_id=1, source_target_pairs={{0,8},{8,16},{16,24},{24,0},{1,9},{9,17},{17,25},{25,1},{2,10},{10... | collective-permute-start | bytes 9224 | tf_op jit(solution)/shard_map/ppermute | solution.py:172
  18.1 0.7 %copy-start = (f32[8,96]{1,0:T(8,128)S(1)}, f32[8,96]{1,0:T(8,128)}, u32[]{:S(2)}) copy-start(f32[8,96]{1,0:T(8,128)} %get-tuple-element.59) | copy-start | bytes 9220
  19.1 7.3 %copy-start.1 = (f32[3]{0:T(128)S(1)}, f32[3]{0:T(128)}, u32[]{:S(2)}) copy-start(f32[3]{0:T(128)} %constant.85) | copy-start | bytes 40

commit v16 on v15

--- a/solution.py
+++ b/solution.py
@@ -25,7 +25,7 @@
 def raw_terms(points, wake_table):
     point_count = points.shape[1]
     wake_count = wake_table.shape[1]
-    wake_width = math.gcd(wake_count, 8192)
+    wake_width = math.gcd(wake_count, 4096)
     wake_place = wake_table[0:3]
     core_square = wake_table[3]
     tables = wake_table[4:10]

time: 27.4 us -> 28 us (1.022)
  local copies, waits for them, and re-layouts: 0.32 us -> 0.63 us
    add x0 -> x1, other arithmetic: none -> 0.3 us  [raw_terms(): wake_place[0] * wake_place[0] + wake_place[1] * wake_place[1]]
    dot_general x1 -> x2, matrix products: 7.25 us -> 7.28 us  [accumulate(): lax.dot_general(table_part, kernel, (((1,), (0,)), ((), ())), precision=l...]
  transfers between devices with their start and end apart: 3 -> 3, of which waited for: 0 -> 0; matrix products, arithmetic and copies ran while one was open for 1% -> 2% of each run, Pallas kernels for 0% -> 0%
where the time goes in v16:
time: 28 us; the launch traced here: 27.7 us
  blocking collectives  9.51 us (34%)
  matrix products  7.28 us (26%)
  starting transfers between devices  6.06 us (22%)
  Pallas kernels  1.84 us (7%)
  other arithmetic  1.49 us (5%)
  between operations  0.85 us (3%)
  local copies, waits for them, and re-layouts  0.63 us (2%)
    all_gather x1, blocking collectives, body(): lax.all_gather(wake_table, 'narrow', axis=1, tiled=True)  9.51 us
    dot_general x2, matrix products, accumulate(): lax.dot_general(table_part, kernel, (((1,), (0,)), ((), ())), precision=l...  7.28 us
    ppermute x3, starting transfers between devices, exchange_slots(): by_shift.append(lax.ppermute(by_offset[shift], 'region', pairs))  6.06 us
    pallas_call x1, Pallas kernels, prologue(): pl.pallas_call(prologue_kernel, out_shape=tuple([jax.ShapeDtypeStruct((8,...  1.84 us
    mul x1, other arithmetic, advance(): jnp.concatenate([new_place, new_velocity], axis=0) * live_flag[None, :]  0.61 us
  transfers between devices with their start and end apart: 3, of which 0 were waited for; matrix products, arithmetic and copies ran while one was open for 2% of the time, Pallas kernels for 0%

profile of v16, /device:TPU:0, one launch (start us, length us, event | category | flops | bytes accessed | tf_op | source)
XLA Modules:
  0.0 27.7 jit_solution(9077427766658349533)
XLA Ops:
  0.7 1.8 %shard_map.91 = (f32[8,96]{1,0:T(8,128)}, f32[8,96]{1,0:T(8,128)}, f32[8,96]{1,0:T(8,128)}, f32[8,96]{1,0:T(8,128)}, f32[7,1024]{1,0:T(8,128)}) custom-call(s32[1]{0:T(128)S(6)} %copy.18.count_ref, f32[3,192]{1,0:T(4,128)} %pos_ref.1, f32[3,192]{1,0:T(4,128)} %vel_ref.1, f32[1,192]{1,0:T(1,128)} %bitcast.33, s32[1,192]{1,0:T(1,128)} %bitcast.34, ...), custom_call_target="tpu_custom_call" | custom-call | tf_op jit(solution)/shard_map/pallas_call | solution.py:144
  2.5 5.0 %collective-permute-start = (f32[8,96]{1,0:T(8,128)}, f32[8,96]{1,0:T(8,128)S(1)}, u32[]{:S(2)}, u32[]{:S(2)}) collective-permute-start(f32[8,96]{1,0:T(8,128)} %get-tuple-element.65), channel_id=1, source_target_pairs={{0,24},{8,0},{16,8},{24,16},{1,25},{9,1},{17,9},{25,17},{2,26},{10... | collective-permute-start | bytes 9224 | tf_op jit(solution)/shard_map/ppermute | solution.py:172
  7.5 0.0 collective-permute-start.1
  7.5 1.0 %collective-permute-start.2 = (f32[8,96]{1,0:T(8,128)}, f32[8,96]{1,0:T(8,128)S(1)}, u32[]{:S(2)}, u32[]{:S(2)}) collective-permute-start(f32[8,96]{1,0:T(8,128)} %get-tuple-element.67), channel_id=1, source_target_pairs={{0,8},{8,16},{16,24},{24,0},{1,9},{9,17},{17,25},{25,1},{2,10},{10... | collective-permute-start | bytes 9224 | tf_op jit(solution)/shard_map/ppermute | solution.py:172
  8.6 9.5 %all_gather.3 = f32[7,8192]{1,0:T(8,128)S(1)} all-gather(f32[7,1024]{1,0:T(8,128)} %get-tuple-element.69), channel_id=1, replica_groups=mesh['region'=4,'narrow'=8] {'narrow'}, dimensions={1}, use_global_device_ids=true | all-gather | bytes 258048 | tf_op jit(solution)/shard_map/all_gather | solution.py:195
  18.1 0.3 %fusion.21 = (f32[8192]{0:T(1024)S(1)}, f32[1,8192]{1,0:T(1,128)S(1)}, f32[1,8192]{1,0:T(1,128)S(1)}, f32[1,8192]{1,0:T(1,128)S(1)}) fusion(f32[7,8192]{1,0:T(8,128)S(1)} %all_gather.3), kind=kLoop, calls=%fused_computation.34 | loop fusion | flops 122880 | bytes 360448 | tf_op jit(solution)/shard_map/add | solution.py:33
  18.4 0.0 copy-start
  18.4 0.1 pad_maximum_fusion
  18.7 0.0 collective-permute-done
  18.7 0.0 collective-permute-done.1
  18.7 0.0 collective-permute-done.2
  18.7 0.4 %copy-done = f32[8,96]{1,0:T(8,128)S(1)} copy-done((f32[8,96]{1,0:T(8,128)S(1)}, f32[8,96]{1,0:T(8,128)}, u32[]{:S(2)}) %copy-start) | copy-done | bytes 3096
  19.1 0.1 fusion.26
  19.2 0.1 pad_maximum_fusion.3
  19.3 0.1 add_reduce_fusion.1
  19.4 0.0 copy-start.1
  19.4 7.5 %while.18 = (s32[]{:T(128)}, f32[6,384]{1,0:T(8,128)S(1)}, f32[2,6,4096]{2,1,0:T(8,128)S(1)}, f32[2,4096]{1,0:T(2,128)S(1)}, f32[384]{0:T(512)S(1)}, /*index=5*/...) while((s32[]{:T(128)}, f32[6,384]{1,0:T(8,128)S(1)}, ...), condition=%wide.region_1.2_spmd.clone, body=%wide.region_0.1_spmd.clone.sunk | while | flops 70783488 | bytes 366755 | solution.py:65
  19.4 0.1 constant_dynamic-slice_fusion.6
  19.6 3.6 %fusion.31 = f32[6,384]{1,0:T(8,128)S(1)} fusion(f32[384]{0:T(512)S(1)} %get-tuple-element.189, f32[4096]{0:T(1024)S(1)} %bitcast.29, f32[384]{0:T(512)S(1)} %get-tuple-element.191, f32[4096]{0:T(1024)S(1)} %bitcast.28, f32[384]{0:T(512)S(1)} %get-tuple-element.193, f32[4096]{0:T(1024)S(1)} %bitcast.27, f32[384]{0:T(512)S(1)} %get-tuple-element.221, ...), kind=kOutput, calls=%fused_computation.18.clone.1 | convolution fusion | flops 70783488 | bytes 226309 | tf_op jit(solution)/shard_map/while/body/eval_jaxpr/while/body/eval_jaxpr/dot_general | solution.py:60
  23.2 0.1 constant_dynamic-slice_fusion.6
  23.3 3.6 %fusion.31 = f32[6,384]{1,0:T(8,128)S(1)} fusion(f32[384]{0:T(512)S(1)} %get-tuple-element.189, f32[4096]{0:T(1024)S(1)} %bitcast.29, f32[384]{0:T(512)S(1)} %get-tuple-element.191, f32[4096]{0:T(1024)S(1)} %bitcast.28, f32[384]{0:T(512)S(1)} %get-tuple-element.193, f32[4096]{0:T(1024)S(1)} %bitcast.27, f32[384]{0:T(512)S(1)} %get-tuple-element.221, ...), kind=kOutput, calls=%fused_computation.18.clone.1 | convolution fusion | flops 70783488 | bytes 226309 | tf_op jit(solution)/shard_map/while/body/eval_jaxpr/while/body/eval_jaxpr/dot_general | solution.py:60
  27.0 0.0 copy-done.1
  27.0 0.1 multiply_add_fusion
  27.1 0.6 %maximum_multiply_fusion = f32[6,384]{1,0:T(8,128)} fusion(f32[3,384]{1,0:T(4,128)S(1)} %get-tuple-element.117, f32[3,384]{1,0:T(4,128)S(1)} %get-tuple-element.116, f32[384]{0:T(512)S(1)} %get-tuple-element.114), kind=kLoop, calls=%fused_computation.39 | loop fusion | flops 4608 | bytes 19968 | tf_op jit(solution)/shard_map/mul | solution.py:88
  (10 shorter events, 0.2 us)
Async XLA Ops:
  2.5 16.2 %collective-permute-start = (f32[8,96]{1,0:T(8,128)}, f32[8,96]{1,0:T(8,128)S(1)}, u32[]{:S(2)}, u32[]{:S(2)}) collective-permute-start(f32[8,96]{1,0:T(8,128)} %get-tuple-element.65), channel_id=1, source_target_pairs={{0,24},{8,0},{16,8},{24,16},{1,25},{9,1},{17,9},{25,17},{2,26},{10... | collective-permute-start | bytes 9224 | tf_op jit(solution)/shard_map/ppermute | solution.py:172
  7.5 11.2 %collective-permute-start.1 = (f32[8,96]{1,0:T(8,128)}, f32[8,96]{1,0:T(8,128)S(1)}, u32[]{:S(2)}, u32[]{:S(2)}) collective-permute-start(f32[8,96]{1,0:T(8,128)} %get-tuple-element.66), channel_id=1, source_target_pairs={{0,16},{8,24},{16,0},{24,8},{1,17},{9,25},{17,1},{25,9},{2,18},{10... | collective-permute-start | bytes 9224 | tf_op jit(solution)/shard_map/ppermute | solution.py:172
  7.5 11.2 %collective-permute-start.2 = (f32[8,96]{1,0:T(8,128)}, f32[8,96]{1,0:T(8,128)S(1)}, u32[]{:S(2)}, u32[]{:S(2)}) collective-permute-start(f32[8,96]{1,0:T(8,128)} %get-tuple-element.67), channel_id=1, source_target_pairs={{0,8},{8,16},{16,24},{24,0},{1,9},{9,17},{17,25},{25,1},{2,10},{10... | collective-permute-start | bytes 9224 | tf_op jit(solution)/shard_map/ppermute | solution.py:172
  18.4 0.7 %copy-start = (f32[8,96]{1,0:T(8,128)S(1)}, f32[8,96]{1,0:T(8,128)}, u32[]{:S(2)}) copy-start(f32[8,96]{1,0:T(8,128)} %get-tuple-element.68) | copy-start | bytes 9220
  19.4 7.6 %copy-start.1 = (f32[3]{0:T(128)S(1)}, f32[3]{0:T(128)}, u32[]{:S(2)}) copy-start(f32[3]{0:T(128)} %constant.85) | copy-start | bytes 40

commit v17 on v15

--- a/solution.py
+++ b/solution.py
@@ -88,22 +88,11 @@
     return jnp.concatenate([new_place, new_velocity], axis=0) * live_flag[None, :]
 
 
-def exact_place(values, placing):
-    high = values.astype(jnp.bfloat16)
-    rest = values - high.astype(jnp.float32)
-    middle = rest.astype(jnp.bfloat16)
-    low = (rest - middle.astype(jnp.float32)).astype(jnp.bfloat16)
-    contract = (((1,), (1,)), ((), ()))
-    total = lax.dot_general(high, placing, contract, preferred_element_type=jnp.float32)
-    total = total + lax.dot_general(middle, placing, contract, preferred_element_type=jnp.float32)
-    return total + lax.dot_general(low, placing, contract, preferred_element_type=jnp.float32)
-
-
 def prologue_kernel(
     count_ref, pos_ref, vel_ref, tau_ref, dest_ref, wpos_ref, wgam_ref, wcore_ref, *refs
 ):
     out_refs = refs[:-2]
-    table_ref, state_ref = refs[-2:]
+    table_ref, split_ref = refs[-2:]
     regions = len(out_refs)
     capacity = out_refs[0].shape[1]
     per_device = dest_ref.shape[1]
@@ -117,18 +106,25 @@
     slot_rank = jnp.sum(before * onehot, axis=0, keepdims=True).astype(jnp.int32)
     column = target * capacity + slot_rank
     live = lax.broadcasted_iota(jnp.int32, (1, per_device), 1) < count_ref[0]
-    state_ref[0:3, :] = pos_ref[...]
-    state_ref[3:6, :] = vel_ref[...]
-    state_ref[6:7, :] = tau_ref[...]
-    state_ref[7:8, :] = jnp.ones((1, per_device), jnp.float32)
-    state = state_ref[...]
+    state = jnp.concatenate(
+        [pos_ref[...], vel_ref[...], tau_ref[...], jnp.ones((1, per_device), jnp.float32)], axis=0
+    )
+    high = state.astype(jnp.bfloat16).astype(jnp.float32)
+    rest = state - high
+    middle = rest.astype(jnp.bfloat16).astype(jnp.float32)
+    split_ref[0:8, :] = high
+    split_ref[8:16, :] = middle
+    split_ref[16:24, :] = rest - middle
+    split = split_ref[...].astype(jnp.bfloat16)
     region = lax.axis_index("region")
-
     for shift, out_ref in enumerate(out_refs):
         dest_region = (region + shift) % regions
         slot_id = lax.broadcasted_iota(jnp.int32, (capacity, per_device), 0) + dest_region * capacity
         placing = ((column == slot_id) & live).astype(jnp.bfloat16)
-        out_ref[...] = exact_place(state, placing)
+        parts = lax.dot_general(
+            split, placing, (((1,), (1,)), ((), ())), preferred_element_type=jnp.float32
+        )
+        out_ref[...] = (parts[0:8] + parts[8:16]) + parts[16:24]
     core = wcore_ref[...]
     table_ref[0:3, :] = wpos_ref[...]
     table_ref[3:4, :] = core * core
@@ -149,7 +145,7 @@
         ),
         in_specs=[pl.BlockSpec(memory_space=pltpu.SMEM)] + [vmem] * 7,
         out_specs=tuple([vmem] * (regions + 1)),
-        scratch_shapes=[pltpu.VMEM((8, per_device), jnp.float32)],
+        scratch_shapes=[pltpu.VMEM((24, per_device), jnp.float32)],
     )(
         counts, dust_pos, dust_vel, dust_tau.reshape(1, per_device), dest.reshape(1, per_device),
         wake_pos, wake_gamma, wake_core.reshape(1, wake_count),

time: 27.4 us -> 27.3 us (level)
  no operation moved by 1% of the time
where the time goes in v17:
time: 27.3 us; the launch traced here: 27 us
  blocking collectives  9.51 us (35%)
  matrix products  7.25 us (27%)
  starting transfers between devices  6.06 us (22%)
  Pallas kernels  1.77 us (6%)
  other arithmetic  1.28 us (5%)
  between operations  0.82 us (3%)
  local copies, waits for them, and re-layouts  0.32 us (1%)
    all_gather x1, blocking collectives, body(): lax.all_gather(wake_table, 'narrow', axis=1, tiled=True)  9.51 us
    dot_general x1, matrix products, accumulate(): lax.dot_general(table_part, kernel, (((1,), (0,)), ((), ())), precision=l...  7.25 us
    ppermute x3, starting transfers between devices, exchange_slots(): by_shift.append(lax.ppermute(by_offset[shift], 'region', pairs))  6.06 us
    pallas_call x1, Pallas kernels, prologue(): pl.pallas_call(prologue_kernel, out_shape=tuple([jax.ShapeDtypeStruct((8,...  1.77 us
    mul x1, other arithmetic, advance(): jnp.concatenate([new_place, new_velocity], axis=0) * live_flag[None, :]  0.61 us
  transfers between devices with their start and end apart: 3, of which 0 were waited for; matrix products, arithmetic and copies ran while one was open for 1% of the time, Pallas kernels for 0%

profile of v17, /device:TPU:0, one launch (start us, length us, event | category | flops | bytes accessed | tf_op | source)
XLA Modules:
  0.0 27.0 jit_solution(2796394720738716141)
XLA Ops:
  0.7 1.8 %shard_map.91 = (f32[8,96]{1,0:T(8,128)}, f32[8,96]{1,0:T(8,128)}, f32[8,96]{1,0:T(8,128)}, f32[8,96]{1,0:T(8,128)}, f32[7,1024]{1,0:T(8,128)}) custom-call(s32[1]{0:T(128)S(6)} %copy.10.count_ref, f32[3,192]{1,0:T(4,128)} %pos_ref.1, f32[3,192]{1,0:T(4,128)} %vel_ref.1, f32[1,192]{1,0:T(1,128)} %bitcast.12, s32[1,192]{1,0:T(1,128)} %bitcast.13, ...), custom_call_target="tpu_custom_call" | custom-call | tf_op jit(solution)/shard_map/pallas_call | solution.py:140
  2.4 5.0 %collective-permute-start = (f32[8,96]{1,0:T(8,128)}, f32[8,96]{1,0:T(8,128)S(1)}, u32[]{:S(2)}, u32[]{:S(2)}) collective-permute-start(f32[8,96]{1,0:T(8,128)} %get-tuple-element.56), channel_id=1, source_target_pairs={{0,24},{8,0},{16,8},{24,16},{1,25},{9,1},{17,9},{25,17},{2,26},{10... | collective-permute-start | bytes 9224 | tf_op jit(solution)/shard_map/ppermute | solution.py:168
  7.5 0.0 collective-permute-start.1
  7.5 1.0 %collective-permute-start.2 = (f32[8,96]{1,0:T(8,128)}, f32[8,96]{1,0:T(8,128)S(1)}, u32[]{:S(2)}, u32[]{:S(2)}) collective-permute-start(f32[8,96]{1,0:T(8,128)} %get-tuple-element.58), channel_id=1, source_target_pairs={{0,8},{8,16},{16,24},{24,0},{1,9},{9,17},{17,25},{25,1},{2,10},{10... | collective-permute-start | bytes 9224 | tf_op jit(solution)/shard_map/ppermute | solution.py:168
  8.5 9.5 %all_gather.3 = f32[7,8192]{1,0:T(8,128)S(1)} all-gather(f32[7,1024]{1,0:T(8,128)} %get-tuple-element.60), channel_id=1, replica_groups=mesh['region'=4,'narrow'=8] {'narrow'}, dimensions={1}, use_global_device_ids=true | all-gather | bytes 258048 | tf_op jit(solution)/shard_map/all_gather | solution.py:191
  18.0 0.0 copy-start
  18.0 0.2 multiply_subtract_fusion.2
  18.3 0.1 fusion.26
  18.4 0.0 collective-permute-done
  18.5 0.0 collective-permute-done.1
  18.5 0.0 collective-permute-done.2
  18.5 0.2 copy-done
  18.7 0.1 pad_maximum_fusion.6
  18.8 0.1 add_reduce_fusion.1
  18.9 0.1 multiply_reduce_fusion
  19.0 0.0 copy-start.1
  19.0 7.3 %fusion = f32[6,384]{1,0:T(8,128)S(1)} fusion(f32[384]{0:T(512)S(1)} %get-tuple-element.66, f32[8192]{0:T(1024)S(1)} %bitcast.8, f32[384]{0:T(512)S(1)} %get-tuple-element.65, f32[8192]{0:T(1024)S(1)} %bitcast.9, f32[384]{0:T(512)S(1)} %get-tuple-element.64, f32[8192]{0:T(1024)S(1)} %bitcast.7, f32[384]{0:T(512)S(1)} %get-tuple-element.63, ...), kind=kOutput, calls=%fused_computation.1 | convolution fusion | flops 141705216 | bytes 474112 | tf_op jit(solution)/shard_map/while/body/eval_jaxpr/while/body/eval_jaxpr/dot_general | solution.py:60
  26.3 0.0 copy-done.1
  26.3 0.1 slice_add_fusion.1
  26.4 0.6 %maximum_multiply_fusion = f32[6,384]{1,0:T(8,128)} fusion(f32[3,384]{1,0:T(4,128)S(1)} %get-tuple-element.70, f32[3,384]{1,0:T(4,128)S(1)} %get-tuple-element.69, f32[384]{0:T(512)S(1)} %get-tuple-element.81), kind=kLoop, calls=%fused_computation.28 | loop fusion | flops 4608 | bytes 19968 | tf_op jit(solution)/shard_map/mul | solution.py:88
  (3 shorter events, 0.1 us)
Async XLA Ops:
  2.4 16.0 %collective-permute-start = (f32[8,96]{1,0:T(8,128)}, f32[8,96]{1,0:T(8,128)S(1)}, u32[]{:S(2)}, u32[]{:S(2)}) collective-permute-start(f32[8,96]{1,0:T(8,128)} %get-tuple-element.56), channel_id=1, source_target_pairs={{0,24},{8,0},{16,8},{24,16},{1,25},{9,1},{17,9},{25,17},{2,26},{10... | collective-permute-start | bytes 9224 | tf_op jit(solution)/shard_map/ppermute | solution.py:168
  7.5 11.0 %collective-permute-start.1 = (f32[8,96]{1,0:T(8,128)}, f32[8,96]{1,0:T(8,128)S(1)}, u32[]{:S(2)}, u32[]{:S(2)}) collective-permute-start(f32[8,96]{1,0:T(8,128)} %get-tuple-element.57), channel_id=1, source_target_pairs={{0,16},{8,24},{16,0},{24,8},{1,17},{9,25},{17,1},{25,9},{2,18},{10... | collective-permute-start | bytes 9224 | tf_op jit(solution)/shard_map/ppermute | solution.py:168
  7.5 11.0 %collective-permute-start.2 = (f32[8,96]{1,0:T(8,128)}, f32[8,96]{1,0:T(8,128)S(1)}, u32[]{:S(2)}, u32[]{:S(2)}) collective-permute-start(f32[8,96]{1,0:T(8,128)} %get-tuple-element.58), channel_id=1, source_target_pairs={{0,8},{8,16},{16,24},{24,0},{1,9},{9,17},{17,25},{25,1},{2,10},{10... | collective-permute-start | bytes 9224 | tf_op jit(solution)/shard_map/ppermute | solution.py:168
  18.0 0.7 %copy-start = (f32[8,96]{1,0:T(8,128)S(1)}, f32[8,96]{1,0:T(8,128)}, u32[]{:S(2)}) copy-start(f32[8,96]{1,0:T(8,128)} %get-tuple-element.59) | copy-start | bytes 9220
  19.0 7.3 %copy-start.1 = (f32[3]{0:T(128)S(1)}, f32[3]{0:T(128)}, u32[]{:S(2)}) copy-start(f32[3]{0:T(128)} %constant.85) | copy-start | bytes 40

commit v18 on v17

--- a/solution.py
+++ b/solution.py
@@ -26,16 +26,10 @@
     point_count = points.shape[1]
     wake_count = wake_table.shape[1]
     wake_width = math.gcd(wake_count, 8192)
-    wake_place = wake_table[0:3]
-    core_square = wake_table[3]
+    scaled_place = wake_table[0:3]
+    wake_offset = wake_table[3]
     tables = wake_table[4:10]
-    wake_offset = (
-        wake_place[0] * wake_place[0]
-        + wake_place[1] * wake_place[1]
-        + wake_place[2] * wake_place[2]
-        + core_square
-    )
-    place_blocks = (-2.0 * wake_place).reshape(3, wake_count // wake_width, wake_width).transpose(1, 0, 2)
+    place_blocks = scaled_place.reshape(3, wake_count // wake_width, wake_width).transpose(1, 0, 2)
     table_blocks = tables.reshape(6, wake_count // wake_width, wake_width).transpose(1, 0, 2)
     core_blocks = wake_offset.reshape(wake_count // wake_width, wake_width)
     point_blocks = points.reshape(3, point_count // point_count, point_count).transpose(1, 0, 2)
@@ -126,8 +120,11 @@
         )
         out_ref[...] = (parts[0:8] + parts[8:16]) + parts[16:24]
     core = wcore_ref[...]
-    table_ref[0:3, :] = wpos_ref[...]
-    table_ref[3:4, :] = core * core
+    place = wpos_ref[...]
+    table_ref[0:3, :] = -2.0 * place
+    table_ref[3:4, :] = (
+        place[0:1] * place[0:1] + place[1:2] * place[1:2] + place[2:3] * place[2:3] + core * core
+    )
     table_ref[4:7, :] = wgam_ref[...]
 
 
@@ -177,9 +174,9 @@
 
 
 def wake_tables(gathered):
-    place = gathered[0:3]
+    scaled_place = gathered[0:3]
     gamma = gathered[4:7]
-    return jnp.concatenate([gathered, cross_rows(gamma, place)], axis=0)
+    return jnp.concatenate([gathered, -0.5 * cross_rows(gamma, scaled_place)], axis=0)
 
 
 def body(dust_pos, dust_vel, dust_tau, dest, counts, wake_pos, wake_gamma, wake_core):

time: 27.3 us -> 27.4 us (level)
  no operation moved by 1% of the time
where the time goes in v18:
time: 27.4 us; the launch traced here: 27.1 us
  blocking collectives  9.51 us (35%)
  matrix products  7.17 us (26%)
  starting transfers between devices  6.06 us (22%)
  Pallas kernels  1.77 us (6%)
  other arithmetic  1.31 us (5%)
  between operations  0.81 us (3%)
  local copies, waits for them, and re-layouts  0.47 us (2%)
    all_gather x1, blocking collectives, body(): lax.all_gather(wake_table, 'narrow', axis=1, tiled=True)  9.51 us
    dot_general x1, matrix products, accumulate(): lax.dot_general(table_part, kernel, (((1,), (0,)), ((), ())), precision=l...  7.17 us
    ppermute x3, starting transfers between devices, exchange_slots(): by_shift.append(lax.ppermute(by_offset[shift], 'region', pairs))  6.06 us
    pallas_call x1, Pallas kernels, prologue(): pl.pallas_call(prologue_kernel, out_shape=tuple([jax.ShapeDtypeStruct((8,...  1.77 us
    mul x1, other arithmetic, advance(): jnp.concatenate([new_place, new_velocity], axis=0) * live_flag[None, :]  0.61 us
  transfers between devices with their start and end apart: 3, of which 0 were waited for; matrix products, arithmetic and copies ran while one was open for 1% of the time, Pallas kernels for 0%

profile of v18, /device:TPU:0, one launch (start us, length us, event | category | flops | bytes accessed | tf_op | source)
XLA Modules:
  0.0 27.1 jit_solution(12265098085545899263)
XLA Ops:
  0.7 1.8 %shard_map.91 = (f32[8,96]{1,0:T(8,128)}, f32[8,96]{1,0:T(8,128)}, f32[8,96]{1,0:T(8,128)}, f32[8,96]{1,0:T(8,128)}, f32[7,1024]{1,0:T(8,128)}) custom-call(s32[1]{0:T(128)S(6)} %copy.10.count_ref, f32[3,192]{1,0:T(4,128)} %pos_ref.1, f32[3,192]{1,0:T(4,128)} %vel_ref.1, f32[1,192]{1,0:T(1,128)} %bitcast.12, s32[1,192]{1,0:T(1,128)} %bitcast.13, ...), custom_call_target="tpu_custom_call" | custom-call | tf_op jit(solution)/shard_map/pallas_call | solution.py:137
  2.4 5.0 %collective-permute-start = (f32[8,96]{1,0:T(8,128)}, f32[8,96]{1,0:T(8,128)S(1)}, u32[]{:S(2)}, u32[]{:S(2)}) collective-permute-start(f32[8,96]{1,0:T(8,128)} %get-tuple-element.56), channel_id=1, source_target_pairs={{0,24},{8,0},{16,8},{24,16},{1,25},{9,1},{17,9},{25,17},{2,26},{10... | collective-permute-start | bytes 9224 | tf_op jit(solution)/shard_map/ppermute | solution.py:165
  7.5 0.0 collective-permute-start.1
  7.5 1.0 %collective-permute-start.2 = (f32[8,96]{1,0:T(8,128)}, f32[8,96]{1,0:T(8,128)S(1)}, u32[]{:S(2)}, u32[]{:S(2)}) collective-permute-start(f32[8,96]{1,0:T(8,128)} %get-tuple-element.58), channel_id=1, source_target_pairs={{0,8},{8,16},{16,24},{24,0},{1,9},{9,17},{17,25},{25,1},{2,10},{10... | collective-permute-start | bytes 9224 | tf_op jit(solution)/shard_map/ppermute | solution.py:165
  8.5 9.5 %all_gather.3 = f32[7,8192]{1,0:T(8,128)S(1)} all-gather(f32[7,1024]{1,0:T(8,128)} %get-tuple-element.60), channel_id=1, replica_groups=mesh['region'=4,'narrow'=8] {'narrow'}, dimensions={1}, use_global_device_ids=true | all-gather | bytes 258048 | tf_op jit(solution)/shard_map/all_gather | solution.py:188
  18.0 0.2 multiply_subtract_fusion.2
  18.2 0.0 copy-start
  18.2 0.1 maximum_multiply_fusion
  18.4 0.0 collective-permute-done
  18.4 0.0 collective-permute-done.1
  18.4 0.0 collective-permute-done.2
  18.4 0.5 %copy-done = f32[8,96]{1,0:T(8,128)S(1)} copy-done((f32[8,96]{1,0:T(8,128)S(1)}, f32[8,96]{1,0:T(8,128)}, u32[]{:S(2)}) %copy-start) | copy-done | bytes 3096
  18.9 0.1 pad_maximum_fusion.2
  19.0 0.1 add_reduce_fusion.1
  19.1 0.1 multiply_reduce_fusion
  19.2 0.0 copy-start.1
  19.2 7.2 %fusion = f32[6,384]{1,0:T(8,128)S(1)} fusion(f32[384]{0:T(512)S(1)} %get-tuple-element.66, f32[8192]{0:T(1024)S(1)} %bitcast.10, f32[384]{0:T(512)S(1)} %get-tuple-element.65, f32[8192]{0:T(1024)S(1)} %bitcast.9, f32[384]{0:T(512)S(1)} %get-tuple-element.64, f32[8192]{0:T(1024)S(1)} %bitcast.8, f32[384]{0:T(512)S(1)} %get-tuple-element.63, ...), kind=kOutput, calls=%fused_computation.1 | convolution fusion | flops 141606912 | bytes 474112 | tf_op jit(solution)/shard_map/while/body/eval_jaxpr/while/body/eval_jaxpr/dot_general | solution.py:54
  26.4 0.0 copy-done.1
  26.4 0.1 slice_add_fusion
  26.5 0.6 %maximum_multiply_fusion.1 = f32[6,384]{1,0:T(8,128)} fusion(f32[3,384]{1,0:T(4,128)S(1)} %get-tuple-element.70, f32[3,384]{1,0:T(4,128)S(1)} %get-tuple-element.69, f32[384]{0:T(512)S(1)} %get-tuple-element.81), kind=kLoop, calls=%fused_computation.25 | loop fusion | flops 4608 | bytes 19968 | tf_op jit(solution)/shard_map/mul | solution.py:82
  (2 shorter events, 0.0 us)
Async XLA Ops:
  2.4 16.0 %collective-permute-start = (f32[8,96]{1,0:T(8,128)}, f32[8,96]{1,0:T(8,128)S(1)}, u32[]{:S(2)}, u32[]{:S(2)}) collective-permute-start(f32[8,96]{1,0:T(8,128)} %get-tuple-element.56), channel_id=1, source_target_pairs={{0,24},{8,0},{16,8},{24,16},{1,25},{9,1},{17,9},{25,17},{2,26},{10... | collective-permute-start | bytes 9224 | tf_op jit(solution)/shard_map/ppermute | solution.py:165
  7.5 10.9 %collective-permute-start.1 = (f32[8,96]{1,0:T(8,128)}, f32[8,96]{1,0:T(8,128)S(1)}, u32[]{:S(2)}, u32[]{:S(2)}) collective-permute-start(f32[8,96]{1,0:T(8,128)} %get-tuple-element.57), channel_id=1, source_target_pairs={{0,16},{8,24},{16,0},{24,8},{1,17},{9,25},{17,1},{25,9},{2,18},{10... | collective-permute-start | bytes 9224 | tf_op jit(solution)/shard_map/ppermute | solution.py:165
  7.5 10.9 %collective-permute-start.2 = (f32[8,96]{1,0:T(8,128)}, f32[8,96]{1,0:T(8,128)S(1)}, u32[]{:S(2)}, u32[]{:S(2)}) collective-permute-start(f32[8,96]{1,0:T(8,128)} %get-tuple-element.58), channel_id=1, source_target_pairs={{0,8},{8,16},{16,24},{24,0},{1,9},{9,17},{17,25},{25,1},{2,10},{10... | collective-permute-start | bytes 9224 | tf_op jit(solution)/shard_map/ppermute | solution.py:165
  18.2 0.7 %copy-start = (f32[8,96]{1,0:T(8,128)S(1)}, f32[8,96]{1,0:T(8,128)}, u32[]{:S(2)}) copy-start(f32[8,96]{1,0:T(8,128)} %get-tuple-element.59) | copy-start | bytes 9220
  19.2 7.2 %copy-start.1 = (f32[3]{0:T(128)S(1)}, f32[3]{0:T(128)}, u32[]{:S(2)}) copy-start(f32[3]{0:T(128)} %constant.85) | copy-start | bytes 40

commit v19 on v18

--- a/solution.py
+++ b/solution.py
@@ -183,9 +183,10 @@
     *outgoing, wake_table = prologue(
         dust_pos, dust_vel, dust_tau, dest, counts, wake_pos, wake_gamma, wake_core
     )
-    outgoing, wake_table = lax.optimization_barrier((tuple(outgoing), wake_table))
+    gathered = lax.all_gather(wake_table, "narrow", axis=1, tiled=True)
+    outgoing, gathered = lax.optimization_barrier((tuple(outgoing), gathered))
     arrived = exchange_slots(outgoing)
-    region_table = wake_tables(lax.all_gather(wake_table, "narrow", axis=1, tiled=True))
+    region_table = wake_tables(gathered)
     points = arrived[0:3]
     raw_sums = raw_terms(points, region_table)
     return advance(arrived, raw_sums)

time: 27.4 us -> 31 us (1.13)
  waiting for transfers between devices: 0.01 us -> 4.05 us
  blocking collectives: 9.51 us -> 11 us
  starting transfers between devices: 6.06 us -> 4.64 us
  local copies, waits for them, and re-layouts: 0.47 us -> 0.02 us
    ppermute x3, waiting for transfers between devices: 0.01 us -> 4.05 us  [exchange_slots(): by_shift.append(lax.ppermute(by_offset[shift], 'region', pairs))]
    all_gather x1, blocking collectives: 9.51 us -> 11 us  [body(): gathered = lax.all_gather(wake_table, 'narrow', axis=1, tiled=True)]
    ppermute x3, starting transfers between devices: 6.06 us -> 4.64 us  [exchange_slots(): by_shift.append(lax.ppermute(by_offset[shift], 'region', pairs))]
    unnamed x4 -> x10, local copies, waits for them, and re-layouts: 0.47 us -> 0.02 us
  transfers between devices with their start and end apart: 3 -> 3, of which waited for: 0 -> 2; matrix products, arithmetic and copies ran while one was open for 1% -> 1% of each run, Pallas kernels for 0% -> 0%
where the time goes in v19:
time: 31 us; the launch traced here: 30.7 us
  blocking collectives  11 us (35%)
  matrix products  7.17 us (23%)
  starting transfers between devices  4.64 us (15%)
  waiting for transfers between devices  4.05 us (13%)
  Pallas kernels  1.77 us (6%)
  other arithmetic  1.3 us (4%)
  between operations  0.78 us (3%)
    all_gather x1, blocking collectives, body(): gathered = lax.all_gather(wake_table, 'narrow', axis=1, tiled=True)  11 us
    dot_general x1, matrix products, accumulate(): lax.dot_general(table_part, kernel, (((1,), (0,)), ((), ())), precision=l...  7.17 us
    ppermute x3, starting transfers between devices, exchange_slots(): by_shift.append(lax.ppermute(by_offset[shift], 'region', pairs))  4.64 us
    ppermute x3, waiting for transfers between devices, exchange_slots(): by_shift.append(lax.ppermute(by_offset[shift], 'region', pairs))  4.05 us
    pallas_call x1, Pallas kernels, prologue(): pl.pallas_call(prologue_kernel, out_shape=tuple([jax.ShapeDtypeStruct((8,...  1.77 us
  transfers between devices with their start and end apart: 3, of which 2 were waited for; matrix products, arithmetic and copies ran while one was open for 1% of the time, Pallas kernels for 0%

profile of v19, /device:TPU:0, one launch (start us, length us, event | category | flops | bytes accessed | tf_op | source)
XLA Modules:
  0.0 30.7 jit_solution(6550093268403688800)
XLA Ops:
  0.7 1.8 %shard_map.91 = (f32[8,96]{1,0:T(8,128)}, f32[8,96]{1,0:T(8,128)}, f32[8,96]{1,0:T(8,128)}, f32[8,96]{1,0:T(8,128)}, f32[7,1024]{1,0:T(8,128)}) custom-call(s32[1]{0:T(128)S(6)} %copy.10.count_ref, f32[3,192]{1,0:T(4,128)} %pos_ref.1, f32[3,192]{1,0:T(4,128)} %vel_ref.1, f32[1,192]{1,0:T(1,128)} %bitcast.12, s32[1,192]{1,0:T(1,128)} %bitcast.13, ...), custom_call_target="tpu_custom_call" | custom-call | tf_op jit(solution)/shard_map/pallas_call | solution.py:137
  2.4 0.0 copy-start.4
  2.4 0.0 copy-start.3
  2.4 0.0 copy-start.2
  2.4 11.0 %all_gather.3 = f32[7,8192]{1,0:T(8,128)S(1)} all-gather(f32[7,1024]{1,0:T(8,128)} %get-tuple-element.65), channel_id=1, replica_groups=mesh['region'=4,'narrow'=8] {'narrow'}, dimensions={1}, use_global_device_ids=true | all-gather | bytes 258048 | tf_op jit(solution)/shard_map/all_gather | solution.py:186
  13.4 0.0 copy-done.4
  13.4 3.6 %collective-permute-start = (f32[8,96]{1,0:T(8,128)S(1)}, f32[8,96]{1,0:T(8,128)S(1)}, u32[]{:S(2)}, u32[]{:S(2)}) collective-permute-start(f32[8,96]{1,0:T(8,128)S(1)} %copy-done.4), channel_id=1, source_target_pairs={{0,24},{8,0},{16,8},{24,16},{1,25},{9,1},{17,9},{25,17},{2,26},{10... | collective-permute-start | bytes 9224 | tf_op jit(solution)/shard_map/ppermute | solution.py:165
  17.0 0.0 copy-done.3
  17.0 0.0 collective-permute-start.1
  17.0 0.0 copy-done.2
  17.1 1.0 %collective-permute-start.2 = (f32[8,96]{1,0:T(8,128)S(1)}, f32[8,96]{1,0:T(8,128)S(1)}, u32[]{:S(2)}, u32[]{:S(2)}) collective-permute-start(f32[8,96]{1,0:T(8,128)S(1)} %copy-done.2), channel_id=1, source_target_pairs={{0,8},{8,16},{16,24},{24,0},{1,9},{9,17},{17,25},{25,1},{2,10},{10... | collective-permute-start | bytes 9224 | tf_op jit(solution)/shard_map/ppermute | solution.py:165
  18.1 0.2 multiply_subtract_fusion.2
  18.3 0.0 copy-start
  18.3 0.1 maximum_multiply_fusion
  18.5 0.0 collective-permute-done
  18.5 3.1 %collective-permute-done.1 = f32[8,96]{1,0:T(8,128)S(1)} collective-permute-done((f32[8,96]{1,0:T(8,128)S(1)}, f32[8,96]{1,0:T(8,128)S(1)}, u32[]{:S(2)}, u32[]{:S(2)}) %collective-permute-start.1) | collective-permute-done | bytes 3104 | tf_op jit(solution)/shard_map/ppermute | solution.py:165
  21.6 1.0 %collective-permute-done.2 = f32[8,96]{1,0:T(8,128)S(1)} collective-permute-done((f32[8,96]{1,0:T(8,128)S(1)}, f32[8,96]{1,0:T(8,128)S(1)}, u32[]{:S(2)}, u32[]{:S(2)}) %collective-permute-start.2) | collective-permute-done | bytes 3104 | tf_op jit(solution)/shard_map/ppermute | solution.py:165
  22.5 0.0 copy-done
  22.5 0.1 add_reduce_fusion.1
  22.6 0.1 pad_maximum_fusion.2
  22.7 0.0 copy-start.1
  22.7 7.2 %fusion = f32[6,384]{1,0:T(8,128)S(1)} fusion(f32[384]{0:T(512)S(1)} %get-tuple-element.76, f32[8192]{0:T(1024)S(1)} %bitcast.10, f32[384]{0:T(512)S(1)} %get-tuple-element.75, f32[8192]{0:T(1024)S(1)} %bitcast.9, f32[384]{0:T(512)S(1)} %get-tuple-element.74, f32[8192]{0:T(1024)S(1)} %bitcast.8, f32[384]{0:T(512)S(1)} %get-tuple-element.73, ...), kind=kOutput, calls=%fused_computation.1 | convolution fusion | flops 141606912 | bytes 474112 | tf_op jit(solution)/shard_map/while/body/eval_jaxpr/while/body/eval_jaxpr/dot_general | solution.py:54
  29.9 0.1 multiply_reduce_fusion
  30.0 0.0 copy-done.1
  30.0 0.1 slice_add_fusion
  30.1 0.6 %maximum_multiply_fusion.1 = f32[6,384]{1,0:T(8,128)} fusion(f32[3,384]{1,0:T(4,128)S(1)} %get-tuple-element.80, f32[3,384]{1,0:T(4,128)S(1)} %get-tuple-element.79, f32[384]{0:T(512)S(1)} %get-tuple-element.91), kind=kLoop, calls=%fused_computation.25 | loop fusion | flops 4608 | bytes 19968 | tf_op jit(solution)/shard_map/mul | solution.py:82
  (1 shorter events, 0.0 us)
Async XLA Ops:
  2.4 11.0 %copy-start.4 = (f32[8,96]{1,0:T(8,128)S(1)}, f32[8,96]{1,0:T(8,128)}, u32[]{:S(2)}) copy-start(f32[8,96]{1,0:T(8,128)} %get-tuple-element.66) | copy-start | bytes 9220
  2.4 14.6 %copy-start.3 = (f32[8,96]{1,0:T(8,128)S(1)}, f32[8,96]{1,0:T(8,128)}, u32[]{:S(2)}) copy-start(f32[8,96]{1,0:T(8,128)} %get-tuple-element.67) | copy-start | bytes 9220
  2.4 14.6 %copy-start.2 = (f32[8,96]{1,0:T(8,128)S(1)}, f32[8,96]{1,0:T(8,128)}, u32[]{:S(2)}) copy-start(f32[8,96]{1,0:T(8,128)} %get-tuple-element.68) | copy-start | bytes 9220
  13.4 5.1 %collective-permute-start = (f32[8,96]{1,0:T(8,128)S(1)}, f32[8,96]{1,0:T(8,128)S(1)}, u32[]{:S(2)}, u32[]{:S(2)}) collective-permute-start(f32[8,96]{1,0:T(8,128)S(1)} %copy-done.4), channel_id=1, source_target_pairs={{0,24},{8,0},{16,8},{24,16},{1,25},{9,1},{17,9},{25,17},{2,26},{10... | collective-permute-start | bytes 9224 | tf_op jit(solution)/shard_map/ppermute | solution.py:165
  17.0 4.5 %collective-permute-start.1 = (f32[8,96]{1,0:T(8,128)S(1)}, f32[8,96]{1,0:T(8,128)S(1)}, u32[]{:S(2)}, u32[]{:S(2)}) collective-permute-start(f32[8,96]{1,0:T(8,128)S(1)} %copy-done.3), channel_id=1, source_target_pairs={{0,16},{8,24},{16,0},{24,8},{1,17},{9,25},{17,1},{25,9},{2,18},{10... | collective-permute-start | bytes 9224 | tf_op jit(solution)/shard_map/ppermute | solution.py:165
  17.1 5.5 %collective-permute-start.2 = (f32[8,96]{1,0:T(8,128)S(1)}, f32[8,96]{1,0:T(8,128)S(1)}, u32[]{:S(2)}, u32[]{:S(2)}) collective-permute-start(f32[8,96]{1,0:T(8,128)S(1)} %copy-done.2), channel_id=1, source_target_pairs={{0,8},{8,16},{16,24},{24,0},{1,9},{9,17},{17,25},{25,1},{2,10},{10... | collective-permute-start | bytes 9224 | tf_op jit(solution)/shard_map/ppermute | solution.py:165
  18.3 4.3 %copy-start = (f32[8,96]{1,0:T(8,128)S(1)}, f32[8,96]{1,0:T(8,128)}, u32[]{:S(2)}) copy-start(f32[8,96]{1,0:T(8,128)} %get-tuple-element.69) | copy-start | bytes 9220
  22.7 7.3 %copy-start.1 = (f32[3]{0:T(128)S(1)}, f32[3]{0:T(128)}, u32[]{:S(2)}) copy-start(f32[3]{0:T(128)} %constant.85) | copy-start | bytes 40

commit v20 on v18

--- a/solution.py
+++ b/solution.py
@@ -71,13 +71,15 @@
     points = arrived[0:3]
     velocity = arrived[3:6]
     live_flag = arrived[7]
-    wind = (cross_rows(raw_sums[0:3], points) - raw_sums[3:6]) / (4.0 * math.pi)
+    swirl = cross_rows(raw_sums[0:3], points) - raw_sums[3:6]
     safe_tau = jnp.where(live_flag > 0.5, arrived[6], 1.0)
     rate = step_size / safe_tau
+    drive = rate * (1.0 / (4.0 * math.pi))
+    damping = 1.0 / (1.0 + rate)
     upward = jnp.array([0.0, 0.0, 1.0], jnp.float32)[:, None]
-    new_velocity = (velocity + rate[None, :] * wind - step_size * gravity * upward) / (
-        1.0 + rate[None, :]
-    )
+    new_velocity = (velocity + drive[None, :] * swirl - step_size * gravity * upward) * damping[
+        None, :
+    ]
     new_place = points + step_size * new_velocity
     return jnp.concatenate([new_place, new_velocity], axis=0) * live_flag[None, :]
 

time: 27.4 us -> 27.4 us (level)
  no operation moved by 1% of the time
where the time goes in v20:
time: 27.4 us; the launch traced here: 27.1 us
  blocking collectives  9.51 us (35%)
  matrix products  7.17 us (26%)
  starting transfers between devices  6.06 us (22%)
  Pallas kernels  1.77 us (6%)
  other arithmetic  1.32 us (5%)
  between operations  0.81 us (3%)
  local copies, waits for them, and re-layouts  0.47 us (2%)
    all_gather x1, blocking collectives, body(): lax.all_gather(wake_table, 'narrow', axis=1, tiled=True)  9.51 us
    dot_general x1, matrix products, accumulate(): lax.dot_general(table_part, kernel, (((1,), (0,)), ((), ())), precision=l...  7.17 us
    ppermute x3, starting transfers between devices, exchange_slots(): by_shift.append(lax.ppermute(by_offset[shift], 'region', pairs))  6.06 us
    pallas_call x1, Pallas kernels, prologue(): pl.pallas_call(prologue_kernel, out_shape=tuple([jax.ShapeDtypeStruct((8,...  1.77 us
    mul x1, other arithmetic, advance(): jnp.concatenate([new_place, new_velocity], axis=0) * live_flag[None, :]  0.61 us
  transfers between devices with their start and end apart: 3, of which 0 were waited for; matrix products, arithmetic and copies ran while one was open for 1% of the time, Pallas kernels for 0%

profile of v20, /device:TPU:0, one launch (start us, length us, event | category | flops | bytes accessed | tf_op | source)
XLA Modules:
  0.0 27.1 jit_solution(14708379609814731888)
XLA Ops:
  0.7 1.8 %shard_map.91 = (f32[8,96]{1,0:T(8,128)}, f32[8,96]{1,0:T(8,128)}, f32[8,96]{1,0:T(8,128)}, f32[8,96]{1,0:T(8,128)}, f32[7,1024]{1,0:T(8,128)}) custom-call(s32[1]{0:T(128)S(6)} %copy.10.count_ref, f32[3,192]{1,0:T(4,128)} %pos_ref.1, f32[3,192]{1,0:T(4,128)} %vel_ref.1, f32[1,192]{1,0:T(1,128)} %bitcast.12, s32[1,192]{1,0:T(1,128)} %bitcast.13, ...), custom_call_target="tpu_custom_call" | custom-call | tf_op jit(solution)/shard_map/pallas_call | solution.py:139
  2.4 5.0 %collective-permute-start = (f32[8,96]{1,0:T(8,128)}, f32[8,96]{1,0:T(8,128)S(1)}, u32[]{:S(2)}, u32[]{:S(2)}) collective-permute-start(f32[8,96]{1,0:T(8,128)} %get-tuple-element.56), channel_id=1, source_target_pairs={{0,24},{8,0},{16,8},{24,16},{1,25},{9,1},{17,9},{25,17},{2,26},{10... | collective-permute-start | bytes 9224 | tf_op jit(solution)/shard_map/ppermute | solution.py:167
  7.5 0.0 collective-permute-start.1
  7.5 1.0 %collective-permute-start.2 = (f32[8,96]{1,0:T(8,128)}, f32[8,96]{1,0:T(8,128)S(1)}, u32[]{:S(2)}, u32[]{:S(2)}) collective-permute-start(f32[8,96]{1,0:T(8,128)} %get-tuple-element.58), channel_id=1, source_target_pairs={{0,8},{8,16},{16,24},{24,0},{1,9},{9,17},{17,25},{25,1},{2,10},{10... | collective-permute-start | bytes 9224 | tf_op jit(solution)/shard_map/ppermute | solution.py:167
  8.5 9.5 %all_gather.3 = f32[7,8192]{1,0:T(8,128)S(1)} all-gather(f32[7,1024]{1,0:T(8,128)} %get-tuple-element.60), channel_id=1, replica_groups=mesh['region'=4,'narrow'=8] {'narrow'}, dimensions={1}, use_global_device_ids=true | all-gather | bytes 258048 | tf_op jit(solution)/shard_map/all_gather | solution.py:190
  18.0 0.2 multiply_subtract_fusion.2
  18.2 0.0 copy-start
  18.2 0.1 maximum_multiply_fusion
  18.4 0.0 collective-permute-done
  18.4 0.0 collective-permute-done.1
  18.4 0.0 collective-permute-done.2
  18.4 0.5 %copy-done = f32[8,96]{1,0:T(8,128)S(1)} copy-done((f32[8,96]{1,0:T(8,128)S(1)}, f32[8,96]{1,0:T(8,128)}, u32[]{:S(2)}) %copy-start) | copy-done | bytes 3096
  18.9 0.1 fusion.24
  19.0 0.1 pad_maximum_fusion.2
  19.1 0.1 add_reduce_fusion
  19.2 0.0 copy-start.1
  19.2 7.2 %fusion = f32[6,384]{1,0:T(8,128)S(1)} fusion(f32[384]{0:T(512)S(1)} %get-tuple-element.66, f32[8192]{0:T(1024)S(1)} %bitcast.10, f32[384]{0:T(512)S(1)} %get-tuple-element.65, f32[8192]{0:T(1024)S(1)} %bitcast.9, f32[384]{0:T(512)S(1)} %get-tuple-element.64, f32[8192]{0:T(1024)S(1)} %bitcast.8, f32[384]{0:T(512)S(1)} %get-tuple-element.63, ...), kind=kOutput, calls=%fused_computation.1 | convolution fusion | flops 141606912 | bytes 474112 | tf_op jit(solution)/shard_map/while/body/eval_jaxpr/while/body/eval_jaxpr/dot_general | solution.py:54
  26.4 0.0 copy-done.1
  26.4 0.1 slice_add_fusion
  26.5 0.6 %maximum_multiply_fusion.1 = f32[6,384]{1,0:T(8,128)} fusion(f32[3,384]{1,0:T(4,128)S(1)} %get-tuple-element.70, f32[3,384]{1,0:T(4,128)S(1)} %get-tuple-element.69, f32[384]{0:T(512)S(1)} %get-tuple-element.67), kind=kLoop, calls=%fused_computation.25 | loop fusion | flops 4608 | bytes 19968 | tf_op jit(solution)/shard_map/mul | solution.py:84
  (3 shorter events, 0.1 us)
Async XLA Ops:
  2.4 16.0 %collective-permute-start = (f32[8,96]{1,0:T(8,128)}, f32[8,96]{1,0:T(8,128)S(1)}, u32[]{:S(2)}, u32[]{:S(2)}) collective-permute-start(f32[8,96]{1,0:T(8,128)} %get-tuple-element.56), channel_id=1, source_target_pairs={{0,24},{8,0},{16,8},{24,16},{1,25},{9,1},{17,9},{25,17},{2,26},{10... | collective-permute-start | bytes 9224 | tf_op jit(solution)/shard_map/ppermute | solution.py:167
  7.5 10.9 %collective-permute-start.1 = (f32[8,96]{1,0:T(8,128)}, f32[8,96]{1,0:T(8,128)S(1)}, u32[]{:S(2)}, u32[]{:S(2)}) collective-permute-start(f32[8,96]{1,0:T(8,128)} %get-tuple-element.57), channel_id=1, source_target_pairs={{0,16},{8,24},{16,0},{24,8},{1,17},{9,25},{17,1},{25,9},{2,18},{10... | collective-permute-start | bytes 9224 | tf_op jit(solution)/shard_map/ppermute | solution.py:167
  7.5 10.9 %collective-permute-start.2 = (f32[8,96]{1,0:T(8,128)}, f32[8,96]{1,0:T(8,128)S(1)}, u32[]{:S(2)}, u32[]{:S(2)}) collective-permute-start(f32[8,96]{1,0:T(8,128)} %get-tuple-element.58), channel_id=1, source_target_pairs={{0,8},{8,16},{16,24},{24,0},{1,9},{9,17},{17,25},{25,1},{2,10},{10... | collective-permute-start | bytes 9224 | tf_op jit(solution)/shard_map/ppermute | solution.py:167
  18.2 0.7 %copy-start = (f32[8,96]{1,0:T(8,128)S(1)}, f32[8,96]{1,0:T(8,128)}, u32[]{:S(2)}) copy-start(f32[8,96]{1,0:T(8,128)} %get-tuple-element.59) | copy-start | bytes 9220
  19.2 7.2 %copy-start.1 = (f32[3]{0:T(128)S(1)}, f32[3]{0:T(128)}, u32[]{:S(2)}) copy-start(f32[3]{0:T(128)} %constant.84) | copy-start | bytes 40

commit v21 on v20

--- a/solution.py
+++ b/solution.py
@@ -29,6 +29,9 @@
     scaled_place = wake_table[0:3]
     wake_offset = wake_table[3]
     tables = wake_table[4:10]
+    columns = lax.optimization_barrier(jnp.stack([scaled_place[0], scaled_place[1], scaled_place[2], wake_offset], axis=1))
+    scaled_place = columns[:, 0:3].T
+    wake_offset = columns[:, 3]
     place_blocks = scaled_place.reshape(3, wake_count // wake_width, wake_width).transpose(1, 0, 2)
     table_blocks = tables.reshape(6, wake_count // wake_width, wake_width).transpose(1, 0, 2)
     core_blocks = wake_offset.reshape(wake_count // wake_width, wake_width)

time: 27.4 us -> 27.6 us (level)
  transfers between devices with their start and end apart: 3 -> 3, of which waited for: 0 -> 0; matrix products, arithmetic and copies ran while one was open for 1% -> 2% of each run, Pallas kernels for 0% -> 0%
where the time goes in v21:
time: 27.6 us; the launch traced here: 27.3 us
  blocking collectives  9.51 us (34%)
  matrix products  7.17 us (26%)
  starting transfers between devices  6.06 us (22%)
  Pallas kernels  1.77 us (6%)
  other arithmetic  1.45 us (5%)
  between operations  0.85 us (3%)
  local copies, waits for them, and re-layouts  0.45 us (2%)
    all_gather x1, blocking collectives, body(): lax.all_gather(wake_table, 'narrow', axis=1, tiled=True)  9.51 us
    dot_general x1, matrix products, accumulate(): lax.dot_general(table_part, kernel, (((1,), (0,)), ((), ())), precision=l...  7.17 us
    ppermute x3, starting transfers between devices, exchange_slots(): by_shift.append(lax.ppermute(by_offset[shift], 'region', pairs))  6.06 us
    pallas_call x1, Pallas kernels, prologue(): pl.pallas_call(prologue_kernel, out_shape=tuple([jax.ShapeDtypeStruct((8,...  1.77 us
    mul x1, other arithmetic, advance(): jnp.concatenate([new_place, new_velocity], axis=0) * live_flag[None, :]  0.61 us
  transfers between devices with their start and end apart: 3, of which 0 were waited for; matrix products, arithmetic and copies ran while one was open for 2% of the time, Pallas kernels for 0%

profile of v21, /device:TPU:0, one launch (start us, length us, event | category | flops | bytes accessed | tf_op | source)
XLA Modules:
  0.0 27.3 jit_solution(16249677034501089792)
XLA Ops:
  0.7 1.8 %shard_map.91 = (f32[8,96]{1,0:T(8,128)}, f32[8,96]{1,0:T(8,128)}, f32[8,96]{1,0:T(8,128)}, f32[8,96]{1,0:T(8,128)}, f32[7,1024]{1,0:T(8,128)}) custom-call(s32[1]{0:T(128)S(6)} %copy.10.count_ref, f32[3,192]{1,0:T(4,128)} %pos_ref.1, f32[3,192]{1,0:T(4,128)} %vel_ref.1, f32[1,192]{1,0:T(1,128)} %bitcast.22, s32[1,192]{1,0:T(1,128)} %bitcast.23, ...), custom_call_target="tpu_custom_call" | custom-call | tf_op jit(solution)/shard_map/pallas_call | solution.py:142
  2.4 5.0 %collective-permute-start = (f32[8,96]{1,0:T(8,128)}, f32[8,96]{1,0:T(8,128)S(1)}, u32[]{:S(2)}, u32[]{:S(2)}) collective-permute-start(f32[8,96]{1,0:T(8,128)} %get-tuple-element.56), channel_id=1, source_target_pairs={{0,24},{8,0},{16,8},{24,16},{1,25},{9,1},{17,9},{25,17},{2,26},{10... | collective-permute-start | bytes 9224 | tf_op jit(solution)/shard_map/ppermute | solution.py:170
  7.5 0.0 collective-permute-start.1
  7.5 1.0 %collective-permute-start.2 = (f32[8,96]{1,0:T(8,128)}, f32[8,96]{1,0:T(8,128)S(1)}, u32[]{:S(2)}, u32[]{:S(2)}) collective-permute-start(f32[8,96]{1,0:T(8,128)} %get-tuple-element.58), channel_id=1, source_target_pairs={{0,8},{8,16},{16,24},{24,0},{1,9},{9,17},{17,25},{25,1},{2,10},{10... | collective-permute-start | bytes 9224 | tf_op jit(solution)/shard_map/ppermute | solution.py:170
  8.5 9.5 %all_gather.3 = f32[7,8192]{1,0:T(8,128)S(1)} all-gather(f32[7,1024]{1,0:T(8,128)} %get-tuple-element.60), channel_id=1, replica_groups=mesh['region'=4,'narrow'=8] {'narrow'}, dimensions={1}, use_global_device_ids=true | all-gather | bytes 258048 | tf_op jit(solution)/shard_map/all_gather | solution.py:193
  18.0 0.2 multiply_subtract_fusion.2
  18.2 0.1 pad_maximum_fusion.2
  18.3 0.0 copy-start
  18.4 0.1 fusion.26
  18.4 0.1 maximum_multiply_fusion
  18.7 0.0 collective-permute-done
  18.7 0.0 collective-permute-done.1
  18.7 0.0 collective-permute-done.2
  18.7 0.3 %copy-done = f32[8,96]{1,0:T(8,128)S(1)} copy-done((f32[8,96]{1,0:T(8,128)S(1)}, f32[8,96]{1,0:T(8,128)}, u32[]{:S(2)}) %copy-start) | copy-done | bytes 3096
  19.0 0.1 fusion.24
  19.1 0.1 pad_maximum_fusion.3
  19.2 0.1 add_reduce_fusion
  19.4 0.0 copy-start.1
  19.4 7.2 %fusion = f32[6,384]{1,0:T(8,128)S(1)} fusion(f32[384]{0:T(512)S(1)} %get-tuple-element.66, f32[8192]{0:T(1024)S(1)} %bitcast.19, f32[384]{0:T(512)S(1)} %get-tuple-element.65, f32[8192]{0:T(1024)S(1)} %bitcast.20, f32[384]{0:T(512)S(1)} %get-tuple-element.64, f32[8192]{0:T(1024)S(1)} %bitcast.18, f32[384]{0:T(512)S(1)} %get-tuple-element.63, ...), kind=kOutput, calls=%fused_computation.1 | convolution fusion | flops 141606912 | bytes 474112 | tf_op jit(solution)/shard_map/while/body/eval_jaxpr/while/body/eval_jaxpr/dot_general | solution.py:57
  26.6 0.0 copy-done.1
  26.6 0.1 slice_add_fusion
  26.7 0.6 %maximum_multiply_fusion.1 = f32[6,384]{1,0:T(8,128)} fusion(f32[3,384]{1,0:T(4,128)S(1)} %get-tuple-element.70, f32[3,384]{1,0:T(4,128)S(1)} %get-tuple-element.69, f32[384]{0:T(512)S(1)} %get-tuple-element.67), kind=kLoop, calls=%fused_computation.28 | loop fusion | flops 4608 | bytes 19968 | tf_op jit(solution)/shard_map/mul | solution.py:87
  (5 shorter events, 0.1 us)
Async XLA Ops:
  2.4 16.3 %collective-permute-start = (f32[8,96]{1,0:T(8,128)}, f32[8,96]{1,0:T(8,128)S(1)}, u32[]{:S(2)}, u32[]{:S(2)}) collective-permute-start(f32[8,96]{1,0:T(8,128)} %get-tuple-element.56), channel_id=1, source_target_pairs={{0,24},{8,0},{16,8},{24,16},{1,25},{9,1},{17,9},{25,17},{2,26},{10... | collective-permute-start | bytes 9224 | tf_op jit(solution)/shard_map/ppermute | solution.py:170
  7.5 11.2 %collective-permute-start.1 = (f32[8,96]{1,0:T(8,128)}, f32[8,96]{1,0:T(8,128)S(1)}, u32[]{:S(2)}, u32[]{:S(2)}) collective-permute-start(f32[8,96]{1,0:T(8,128)} %get-tuple-element.57), channel_id=1, source_target_pairs={{0,16},{8,24},{16,0},{24,8},{1,17},{9,25},{17,1},{25,9},{2,18},{10... | collective-permute-start | bytes 9224 | tf_op jit(solution)/shard_map/ppermute | solution.py:170
  7.5 11.2 %collective-permute-start.2 = (f32[8,96]{1,0:T(8,128)}, f32[8,96]{1,0:T(8,128)S(1)}, u32[]{:S(2)}, u32[]{:S(2)}) collective-permute-start(f32[8,96]{1,0:T(8,128)} %get-tuple-element.58), channel_id=1, source_target_pairs={{0,8},{8,16},{16,24},{24,0},{1,9},{9,17},{17,25},{25,1},{2,10},{10... | collective-permute-start | bytes 9224 | tf_op jit(solution)/shard_map/ppermute | solution.py:170
  18.3 0.7 %copy-start = (f32[8,96]{1,0:T(8,128)S(1)}, f32[8,96]{1,0:T(8,128)}, u32[]{:S(2)}) copy-start(f32[8,96]{1,0:T(8,128)} %get-tuple-element.59) | copy-start | bytes 9220
  19.4 7.2 %copy-start.1 = (f32[3]{0:T(128)S(1)}, f32[3]{0:T(128)}, u32[]{:S(2)}) copy-start(f32[3]{0:T(128)} %constant.84) | copy-start | bytes 40
